TPU v7x, 32 devices: a whole 2x2x4 slice. The times are simulated.
32 devices in a mesh: clips: 2 (over y), frames: 4 (over z), wshard: 4 (over x, core).
Axes of the slice: x: 2, y: 2, z: 4, core: 2. Of those that a mesh axis runs over, the one named last changes fastest.
Arguments:
- tokens: bfloat16 [6144, 5120], P(('clips', 'frames')), parts along dimension 0, may hold values from -17 to 17
- w_query: bfloat16 [5120, 3072], P('frames', 'wshard'), may hold values from -0.08385255 to 0.08385255
- w_key: bfloat16 [5120, 3072], P('frames', 'wshard'), may hold values from -0.08385255 to 0.08385255
- w_value: bfloat16 [5120, 3072], P('frames', 'wshard'), may hold values from -0.078125 to 0.078125
- q_gain: float32 [3072], P('wshard'), may hold values from 0.4 to 7
- k_gain: float32 [3072], P('wshard'), may hold values from 0.4 to 7
- w_out: bfloat16 [3072, 5120], P('frames', 'wshard'), may hold values from -0.109375 to 0.109375
- key_blocks: int32 [48, 8], P(('clips', 'frames')), parts along dimension 0, may hold values from 0 to 17, as said below
- slab_counts: int32 [8], P('clips'), parts along dimension 0, may hold values from 384 to 768, as said below
Outputs:
- mixed: bfloat16 [6144, 5120], P(('clips', 'frames'), 'wshard'), parts along dimension 0
There are 2 independent parts, one for each index of `clips`. A program takes and returns all parts, laid end to end along the dimension named above; an argument that names none is the same for every part. Nothing has to cross between parts.
Inputs may be any that keep to these rules, and one draw needn't show every extreme that they name: `key_blocks`: each row names 8 different blocks of its window, among them the query's own block, number 6 + i for block i of a slab. `slab_counts`: some slab is full in every clip.
All inputs are finite; a program needn't handle non-finite values.
Results may differ from a plain program's by a relative error of at most 0.0085.
Values may be sent and summed in bfloat16 or wider, within the bound.
No kernel may reach another device: no remote copies, remote signals or barrier semaphores. Data moves between devices by JAX's collectives and lax.ppermute only.
A program may use at most 192 MiB of HBM per device.

v0:
```python
import math

import jax
import jax.numpy as jnp
from jax import lax
from jax.sharding import PartitionSpec as P

HEAD_DIM = 128
TILE = 128


def shifted(value, axis, by):
    size = lax.axis_size(axis)
    pairs = [(i, i + by) for i in range(size) if 0 <= i + by < size]
    return lax.ppermute(value, axis, pairs)


def head_norm(raw, gain):
    rows, cols = raw.shape
    split = raw.reshape(rows, cols // HEAD_DIM, HEAD_DIM)
    square = jnp.mean(split * split, axis=-1, keepdims=True)
    normed = (split * lax.rsqrt(square + 1e-06)).reshape(rows, cols)
    return (normed * gain).astype(jnp.bfloat16)


def attend(query, keys, values, blocks, limits):
    rows, cols = query.shape
    tiles = rows // TILE
    heads = cols // HEAD_DIM
    picks = blocks.shape[1]
    window = keys.shape[0] // TILE
    key_tiles = keys.reshape(window, TILE, cols)[blocks].reshape(
        tiles, picks * TILE, heads, HEAD_DIM
    )
    value_tiles = values.reshape(window, TILE, cols)[blocks].reshape(
        tiles, picks * TILE, heads, HEAD_DIM
    )
    tile_ids = jnp.arange(window, dtype=jnp.int32)
    slab_of = tile_ids // tiles
    limit = jnp.where(slab_of == 0, limits[0], jnp.where(slab_of == 1, limits[1], limits[2]))
    offsets = (tile_ids % tiles)[:, None] * TILE + jnp.arange(TILE, dtype=jnp.int32)[None, :]
    live = offsets < limit[:, None]
    live_keys = live[blocks].reshape(tiles, picks * TILE)
    query_tiles = query.reshape(tiles, TILE, heads, HEAD_DIM)
    scores = jnp.einsum(
        "iqhd,ikhd->ihqk", query_tiles, key_tiles, preferred_element_type=jnp.float32
    )
    scores = scores * (1.0 / math.sqrt(HEAD_DIM))
    scores = jnp.where(live_keys[:, None, None, :], scores, -1e30)
    top = jnp.max(scores, axis=-1, keepdims=True)
    expo = jnp.exp(scores - top)
    weights = (expo / jnp.sum(expo, axis=-1, keepdims=True)).astype(jnp.bfloat16)
    mixed = jnp.einsum("ihqk,ikhd->iqhd", weights, value_tiles, preferred_element_type=jnp.float32)
    mixed = mixed.reshape(rows, cols)
    own_rows = jnp.arange(rows, dtype=jnp.int32) < limits[1]
    return jnp.where(own_rows[:, None], mixed, 0.0).astype(jnp.bfloat16)


def per_device(tokens, w_query, w_key, w_value, q_gain, k_gain, w_out, key_blocks, slab_counts):

    def project(piece):
        return jnp.dot(tokens, piece, preferred_element_type=jnp.float32)

    query_raw = project(lax.all_gather(w_query, "frames", axis=0, tiled=True))
    key_raw = project(lax.all_gather(w_key, "frames", axis=0, tiled=True))
    value_raw = project(lax.all_gather(w_value, "frames", axis=0, tiled=True))
    query = head_norm(query_raw, q_gain)
    keys = head_norm(key_raw, k_gain)
    values = value_raw.astype(jnp.bfloat16)
    before = shifted((keys, values), "frames", 1)
    after = shifted((keys, values), "frames", -1)
    key_window = jnp.concatenate([before[0], keys, after[0]], axis=0)
    value_window = jnp.concatenate([before[1], values, after[1]], axis=0)
    position = lax.axis_index("frames")
    zero = jnp.zeros((1,), jnp.int32)
    count_pad = jnp.concatenate([zero, slab_counts, zero], axis=0)
    limits = lax.dynamic_slice_in_dim(count_pad, position, 3, 0)
    attended = attend(query, key_window, value_window, key_blocks, limits)
    whole = lax.all_gather(attended, "wshard", axis=1, tiled=True)
    mixed = jnp.dot(
        whole,
        lax.all_gather(w_out, "frames", axis=0, tiled=True),
        preferred_element_type=jnp.float32,
    )
    return mixed.astype(jnp.bfloat16)


def solution(mesh):
    return jax.shard_map(
        per_device,
        mesh=mesh,
        in_specs=(
            P(("clips", "frames"), None),
            P("frames", "wshard"),
            P("frames", "wshard"),
            P("frames", "wshard"),
            P("wshard"),
            P("wshard"),
            P("frames", "wshard"),
            P(("clips", "frames"), None),
            P("clips"),
        ),
        out_specs=P(("clips", "frames"), "wshard"),
        check_vma=False,
    )
```

profile of v0, /device:TPU:0, one launch (start us, length us, event | category | flops | bytes accessed | tf_op | source)
XLA Modules:
  0.0 680.3 jit_solution(16634892609516478321)
XLA Ops:
  6.5 0.0 copy-start.5
  6.5 0.0 copy-start.1
  6.5 0.0 all-gather.10.cloned.1.call-start
  6.5 0.7 all-gather.10.cloned.1.call-update
  7.3 0.0 all-gather.6.cloned.1.call-start
  7.3 0.7 all-gather.6.cloned.1.call-update
  8.0 0.0 all-gather.8.cloned.1.call-start
  8.1 0.7 all-gather.8.cloned.1.call-update
  8.7 0.0 all-gather.14.cloned.1.call-start
  8.8 0.5 all-gather.14.cloned.1.call-update
  9.3 0.0 all-gather.12.cloned.1.call-start
  9.4 0.0 copy-done.5
  9.4 0.1 pad_add_fusion
  9.5 0.1 dynamic_slice.3
  9.5 0.7 fusion.21
  10.2 0.0 copy-done.1
  10.2 0.1 reshape.85
  10.3 1.2 iota_compare_fusion
  11.5 1.9 compare_select_fusion.2
  13.4 0.1 add_compare_fusion
  13.5 0.6 gather_fusion.1
  14.1 0.0 copy-start.2
  14.1 138.6 %all-gather.10.cloned.1.call-done = bf16[5120,768]{1,0:T(8,128)(2,1)} async-done(((bf16[1280,768]{1,0:T(8,128)(2,1)}), bf16[5120,768]{1,0:T(8,128)(2,1)}) %all-gather.10.cloned.1.call-update) | async-done | bytes 7864336 | tf_op jit(solution)/shard_map/all_gather | solution.py:65
  152.7 12.1 %fusion.22 = (f32[768,768]{0,1:T(8,128)}, f32[768,768]{0,1:T(8,128)S(1)}) fusion(bf16[768,5120]{1,0:T(8,128)(2,1)} %param.9, bf16[5120,768]{1,0:T(8,128)(2,1)} %all-gather.10.cloned.1.call-done), kind=kOutput, calls=%fused_computation.47 | convolution fusion | flops 6040387584 | bytes 20447232 | tf_op jit(solution)/shard_map/dot_general | solution.py:62
  164.8 2.0 reduce_sum.28
  166.8 0.0 copy-done.2
  166.8 0.3 fusion.11
  167.1 2.3 collective-permute-start.2
  169.4 1.3 collective-permute-start.3
  170.7 147.9 %all-gather.6.cloned.1.call-done = bf16[5120,768]{1,0:T(8,128)(2,1)} async-done(((bf16[1280,768]{1,0:T(8,128)(2,1)}), bf16[5120,768]{1,0:T(8,128)(2,1)}) %all-gather.6.cloned.1.call-update) | async-done | bytes 7864336 | tf_op jit(solution)/shard_map/all_gather | solution.py:66
  318.6 11.7 %convolution_convert_fusion.1 = bf16[768,768]{1,0:T(8,128)(2,1)} fusion(bf16[768,5120]{1,0:T(8,128)(2,1)} %param.9, bf16[5120,768]{1,0:T(8,128)(2,1)} %all-gather.6.cloned.1.call-done), kind=kOutput, calls=%fused_computation.27 | convolution fusion | flops 6040387584 | bytes 16908288 | tf_op jit(solution)/shard_map/dot_general | solution.py:62
  330.3 0.0 copy-start.3
  330.3 2.4 collective-permute-start
  332.7 1.5 collective-permute-start.1
  334.2 150.4 %all-gather.8.cloned.1.call-done = bf16[5120,768]{1,0:T(8,128)(2,1)} async-done(((bf16[1280,768]{1,0:T(8,128)(2,1)}), bf16[5120,768]{1,0:T(8,128)(2,1)}) %all-gather.8.cloned.1.call-update) | async-done | bytes 7864336 | tf_op jit(solution)/shard_map/all_gather | solution.py:64
  484.6 12.0 %fusion.23 = (f32[768,768]{0,1:T(8,128)S(1)}, f32[768,768]{0,1:T(8,128)}) fusion(bf16[768,5120]{1,0:T(8,128)(2,1)} %param.9, bf16[5120,768]{1,0:T(8,128)(2,1)} %all-gather.8.cloned.1.call-done), kind=kOutput, calls=%fused_computation.48 | convolution fusion | flops 6040387584 | bytes 20447232 | tf_op jit(solution)/shard_map/dot_general | solution.py:62
  496.5 0.8 reduce_sum.27
  497.3 0.7 add_rsqrt_fusion.1
  498.1 0.0 copy-done.3
  498.1 1.9 fusion.13
  500.0 2.2 reshape.116
  502.2 0.0 collective-permute-done.2
  502.2 0.0 collective-permute-done.3
  502.2 3.2 pad_maximum_fusion.1
  505.4 4.5 copy.12
  509.9 6.5 gather_fusion.2
  516.4 20.2 %reshape.81 = bf16[6,1024,6,128]{3,2,1,0:T(8,128)(2,1)} reshape(bf16[48,128,768]{2,1,0:T(8,128)(2,1)} %gather_fusion.2) | data formatting | bytes 18874368 | tf_op jit(solution)/shard_map/reshape | solution.py:32
  536.6 0.0 collective-permute-done
  536.6 0.0 collective-permute-done.1
  536.6 2.2 pad_maximum_fusion
  538.8 6.5 gather_fusion
  545.2 0.0 copy-start
  545.2 20.3 %reshape.78 = bf16[6,1024,6,128]{3,2,1,0:T(8,128)(2,1)} reshape(bf16[48,128,768]{2,1,0:T(8,128)(2,1)} %gather_fusion) | data formatting | bytes 18874368 | tf_op jit(solution)/shard_map/reshape | solution.py:35
  565.5 0.0 copy-done
  565.5 13.8 %fusion.4 = f32[6,6,128,1024]{3,2,1,0:T(8,128)} fusion(bf16[6,1024,6,128]{3,2,1,0:T(8,128)(2,1)} %reshape.81, bf16[6,128,6,128]{1,0,3,2:T(8,128)(2,1)S(1)} %copy-done), kind=kOutput, calls=%fused_computation.10 | convolution fusion | flops 1207959552 | bytes 29491200 | tf_op jit(solution)/shard_map/iqhd,ikhd->ihqk/dot_general | solution.py:45
  579.3 21.8 %fusion.24 = (f32[6,6,128]{2,1,0:T(8,128)S(1)}, f32[6,6,128,1024]{3,2,1,0:T(8,128)}) fusion(f32[6,6,128,1024]{3,2,1,0:T(8,128)} %fusion.4, pred[6,1024]{1,0:T(8,128)(4,1)S(1)} %broadcast_in_dim.58), kind=kOutput, calls=%fused_computation.49 | output fusion | flops 28312576 | bytes 37773312 | tf_op jit(solution)/shard_map/sub | solution.py:51
  601.2 12.6 %fusion.14 = bf16[6,128,6,128]{1,3,2,0:T(8,128)(2,1)S(1)} fusion(f32[6,6,128,1024]{3,2,1,0:T(8,128)} %get-tuple-element.13, f32[6,6,128]{2,1,0:T(8,128)S(1)} %get-tuple-element.12, bf16[6,1024,6,128]{3,2,1,0:T(8,128)(2,1)} %reshape.78), kind=kOutput, calls=%fused_computation.26 | convolution fusion | flops 1217396736 | bytes 29509632 | tf_op jit(solution)/shard_map/ihqk,ikhd->iqhd/dot_general | solution.py:53
  613.8 0.9 copy.16
  614.7 0.0 copy-done.4
  614.7 1.3 fusion.9
  616.0 0.0 all-gather.12.cloned.1.call-update
  616.0 9.4 %all-gather.14.cloned.1.call-done = bf16[3072,1280]{1,0:T(8,128)(2,1)} async-done(((bf16[768,1280]{1,0:T(8,128)(2,1)}), bf16[3072,1280]{1,0:T(8,128)(2,1)}) %all-gather.14.cloned.1.call-update) | async-done | bytes 7864336 | tf_op jit(solution)/shard_map/all_gather | solution.py:82
  625.4 37.1 %all-gather.12.cloned.1.call-done = bf16[768,3072]{1,0:T(8,128)(2,1)} async-done(((bf16[768,768]{1,0:T(8,128)(2,1)}), bf16[768,3072]{1,0:T(8,128)(2,1)}) %all-gather.12.cloned.1.call-update) | async-done | bytes 4718608 | tf_op jit(solution)/shard_map/all_gather | solution.py:79
  662.5 11.3 %convolution_convert_fusion = bf16[768,1280]{1,0:T(8,128)(2,1)} fusion(bf16[768,3072]{1,0:T(8,128)(2,1)} %all-gather.12.cloned.1.call-done, bf16[3072,1280]{1,0:T(8,128)(2,1)} %all-gather.14.cloned.1.call-done), kind=kOutput, calls=%fused_computation.17 | convolution fusion | flops 6040780800 | bytes 14548992 | tf_op jit(solution)/shard_map/dot_general | solution.py:80
  (5 shorter events, 0.1 us)
Async XLA Ops:
  6.5 2.8 copy-start.5
  6.5 3.7 copy-start.1
  6.5 146.2 %all-gather.10.cloned.1.call-start = ((), (), s32[]{:S(2)}) async-start(), calls=%async_computation.2 | async-start | bytes 9830400 | tf_op jit(solution)/shard_map/all_gather | solution.py:65
  7.3 311.3 %all-gather.6.cloned.1.call-start = ((), (), s32[]{:S(2)}) async-start(), calls=%async_computation | async-start | bytes 9830400 | tf_op jit(solution)/shard_map/all_gather | solution.py:66
  8.0 476.6 %all-gather.8.cloned.1.call-start = ((), (), s32[]{:S(2)}) async-start(), calls=%async_computation.1 | async-start | bytes 9830400 | tf_op jit(solution)/shard_map/all_gather | solution.py:64
  8.7 616.7 %all-gather.14.cloned.1.call-start = ((), (), s32[]{:S(2)}) async-start(), calls=%async_computation.4 | async-start | bytes 9830400 | tf_op jit(solution)/shard_map/all_gather | solution.py:82
  9.3 653.1 %all-gather.12.cloned.1.call-start = ((), (), s32[]{:S(2)}) async-start(), calls=%async_computation.3 | async-start | bytes 5898240 | tf_op jit(solution)/shard_map/all_gather | solution.py:79
  14.1 152.6 %copy-start.2 = (f32[768]{0:T(1024)S(1)}, f32[768]{0:T(1024)}, u32[]{:S(2)}) copy-start(f32[768]{0:T(1024)} %param.14) | copy-start | bytes 9220
  167.1 335.1 %collective-permute-start.2 = (bf16[768,768]{0,1:T(8,128)(2,1)S(1)}, bf16[768,768]{0,1:T(8,128)(2,1)}, u32[]{:S(2)}, u32[]{:S(2)}) collective-permute-start(bf16[768,768]{0,1:T(8,128)(2,1)S(1)} %fusion.11), channel_id=1, source_target_pairs={{0,4},{4,8},{8,12},{1,5},{5,9},{9,13},{2,6},{6,10},{10,14},{3,7},{... | collective-permute-start | bytes 3538952 | tf_op jit(solution)/shard_map/ppermute | solution.py:15
  169.4 332.8 %collective-permute-start.3 = (bf16[768,768]{0,1:T(8,128)(2,1)S(1)}, bf16[768,768]{0,1:T(8,128)(2,1)}, u32[]{:S(2)}, u32[]{:S(2)}) collective-permute-start(bf16[768,768]{0,1:T(8,128)(2,1)S(1)} %fusion.11), channel_id=1, source_target_pairs={{4,0},{8,4},{12,8},{5,1},{9,5},{13,9},{6,2},{10,6},{14,10},{7,3},{... | collective-permute-start | bytes 3538952 | tf_op jit(solution)/shard_map/ppermute | solution.py:15
  330.3 167.8 %copy-start.3 = (f32[768]{0:T(1024)S(1)}, f32[768]{0:T(1024)}, u32[]{:S(2)}) copy-start(f32[768]{0:T(1024)} %param.13) | copy-start | bytes 9220
  330.3 206.3 %collective-permute-start = (bf16[768,768]{1,0:T(8,128)(2,1)}, bf16[768,768]{1,0:T(8,128)(2,1)}, u32[]{:S(2)}, u32[]{:S(2)}) collective-permute-start(bf16[768,768]{1,0:T(8,128)(2,1)} %convolution_convert_fusion.1), channel_id=1, source_target_pairs={{0,4},{4,8},{8,12},{1,5},{5,9},{9,13},{2,6},{6,10},{10,14},{3,7},{... | collective-permute-start | bytes 3538952 | tf_op jit(solution)/shard_map/ppermute | solution.py:15
  332.7 203.9 %collective-permute-start.1 = (bf16[768,768]{1,0:T(8,128)(2,1)}, bf16[768,768]{1,0:T(8,128)(2,1)}, u32[]{:S(2)}, u32[]{:S(2)}) collective-permute-start(bf16[768,768]{1,0:T(8,128)(2,1)} %convolution_convert_fusion.1), channel_id=1, source_target_pairs={{4,0},{8,4},{12,8},{5,1},{9,5},{13,9},{6,2},{10,6},{14,10},{7,3},{... | collective-permute-start | bytes 3538952 | tf_op jit(solution)/shard_map/ppermute | solution.py:15
  545.2 20.3 %copy-start = (bf16[6,128,6,128]{1,0,3,2:T(8,128)(2,1)S(1)}, bf16[6,128,6,128]{1,0,3,2:T(8,128)(2,1)}, u32[]{:S(2)}) copy-start(bf16[6,128,6,128]{1,0,3,2:T(8,128)(2,1)} %reshape.116) | copy-start | bytes 3538948
  601.2 13.6 %copy-start.4 = (pred[768]{0:T(1024)(128)(4,1)S(1)}, pred[768]{0:T(1024)(128)(4,1)}, u32[]{:S(2)}) copy-start(pred[768]{0:T(1024)(128)(4,1)} %iota_compare_fusion) | copy-start | bytes 2308
Sparse Core Ops, SparseCore 0:
  8.9 143.7 all-gather.9
  154.3 164.2 all-gather.5
  320.2 164.3 all-gather.7
  486.0 139.3 all-gather.13
  626.8 35.6 all-gather.11
where the time goes:
time: 682 us; the launch traced here: 680 us
  waiting for transfers between devices  486 us (71%)
  matrix products  73.5 us (11%)
  local copies, waits for them, and re-layouts  62.6 us (9%)
  other arithmetic  37.4 us (5%)
  between operations  13.3 us (2%)
  starting transfers between devices  7.66 us (1%)
    all_gather x1, waiting for transfers between devices, per_device(): query_raw = project(lax.all_gather(w_query, 'frames', axis=0, tiled=True))  150 us
    all_gather x1, waiting for transfers between devices, per_device(): value_raw = project(lax.all_gather(w_value, 'frames', axis=0, tiled=True))  148 us
    all_gather x1, waiting for transfers between devices, per_device(): key_raw = project(lax.all_gather(w_key, 'frames', axis=0, tiled=True))  139 us
    all_gather x1, waiting for transfers between devices, per_device(): whole = lax.all_gather(attended, 'wshard', axis=1, tiled=True)  37.1 us
    dot_general x3, matrix products, project(): return jnp.dot(tokens, piece, preferred_element_type=jnp.float32)  35.7 us
    sub x1, other arithmetic, attend(): expo = jnp.exp(scores - top)  21.8 us
    reshape x1, local copies, waits for them, and re-layouts, attend(): values.reshape(window, TILE, cols)[blocks]  20.3 us
    reshape x1, local copies, waits for them, and re-layouts, attend(): keys.reshape(window, TILE, cols)[blocks]  20.2 us
  transfers between devices with their start and end apart: 9, of which 5 were waited for; matrix products, arithmetic and copies ran while one was open for 24% of the time, Pallas kernels for 0%

commit v1 on v0

--- a/solution.py
+++ b/solution.py
@@ -56,14 +56,21 @@
     return jnp.where(own_rows[:, None], mixed, 0.0).astype(jnp.bfloat16)
 
 
+def gather_rows(piece):
+    parts = lax.axis_size("clips")
+    share = piece.shape[0] // parts
+    mine = lax.dynamic_slice_in_dim(piece, lax.axis_index("clips") * share, share, 0)
+    return lax.all_gather(mine, ("frames", "clips"), axis=0, tiled=True)
+
+
 def per_device(tokens, w_query, w_key, w_value, q_gain, k_gain, w_out, key_blocks, slab_counts):
 
     def project(piece):
         return jnp.dot(tokens, piece, preferred_element_type=jnp.float32)
 
-    query_raw = project(lax.all_gather(w_query, "frames", axis=0, tiled=True))
-    key_raw = project(lax.all_gather(w_key, "frames", axis=0, tiled=True))
-    value_raw = project(lax.all_gather(w_value, "frames", axis=0, tiled=True))
+    query_raw = project(gather_rows(w_query))
+    key_raw = project(gather_rows(w_key))
+    value_raw = project(gather_rows(w_value))
     query = head_norm(query_raw, q_gain)
     keys = head_norm(key_raw, k_gain)
     values = value_raw.astype(jnp.bfloat16)
@@ -79,7 +86,7 @@
     whole = lax.all_gather(attended, "wshard", axis=1, tiled=True)
     mixed = jnp.dot(
         whole,
-        lax.all_gather(w_out, "frames", axis=0, tiled=True),
+        gather_rows(w_out),
         preferred_element_type=jnp.float32,
     )
     return mixed.astype(jnp.bfloat16)

time: 682 us -> 611 us (0.90)
  waiting for transfers between devices: 486 us -> 395 us
  local copies, waits for them, and re-layouts: 62.6 us -> 76.6 us
    all_gather x4, waiting for transfers between devices: 446 us -> 359 us  [gather_rows(): return lax.all_gather(mine, ('frames', 'clips'), axis=0, tiled=True)]
  transfers between devices with their start and end apart: 9 -> 9, of which waited for: 5 -> 4; matrix products, arithmetic and copies ran while one was open for 24% -> 29% of each run, Pallas kernels for 0% -> 0%
where the time goes in v1:
time: 611 us; the launch traced here: 609 us
  waiting for transfers between devices  395 us (65%)
  local copies, waits for them, and re-layouts  76.6 us (13%)
  matrix products  74.3 us (12%)
  other arithmetic  41.1 us (7%)
  between operations  13.3 us (2%)
  starting transfers between devices  8.48 us (1%)
    all_gather x4, waiting for transfers between devices, gather_rows(): return lax.all_gather(mine, ('frames', 'clips'), axis=0, tiled=True)  359 us
    dot_general x3, matrix products, project(): return jnp.dot(tokens, piece, preferred_element_type=jnp.float32)  36.5 us
    all_gather x1, waiting for transfers between devices, per_device(): whole = lax.all_gather(attended, 'wshard', axis=1, tiled=True)  36 us
    sub x1, other arithmetic, attend(): expo = jnp.exp(scores - top)  21.8 us
    reshape x1, local copies, waits for them, and re-layouts, attend(): keys.reshape(window, TILE, cols)[blocks]  20.2 us
    reshape x1, local copies, waits for them, and re-layouts, attend(): values.reshape(window, TILE, cols)[blocks]  20.1 us
    dot_general x1, matrix products, attend(): jnp.einsum('iqhd,ikhd->ihqk', query_tiles, key_tiles, preferred_element_t...  13.7 us
    dot_general x1, matrix products, attend(): jnp.einsum('ihqk,ikhd->iqhd', weights, value_tiles, preferred_element_typ...  12.6 us
  transfers between devices with their start and end apart: 9, of which 4 were waited for; matrix products, arithmetic and copies ran while one was open for 29% of the time, Pallas kernels for 0%

profile of v1, /device:TPU:0, one launch (start us, length us, event | category | flops | bytes accessed | tf_op | source)
XLA Modules:
  0.0 609.1 jit_solution(16728721304602790983)
XLA Ops:
  6.5 0.0 copy-start
  6.5 0.0 all-gather.10.cloned.1.call-start
  6.5 1.5 copy-done
  8.1 1.0 constant_dynamic-slice_fusion.1
  9.1 0.0 all-gather.10.cloned.1.call-update
  9.1 0.0 all-gather.6.cloned.1.call-start
  9.2 2.4 constant_dynamic-slice_fusion.3
  11.6 0.0 all-gather.6.cloned.1.call-update
  11.6 0.0 all-gather.8.cloned.1.call-start
  11.7 2.2 constant_dynamic-slice_fusion.2
  13.9 0.0 all-gather.8.cloned.1.call-update
  13.9 0.0 all-gather.14.cloned.1.call-start
  14.0 0.0 copy-done.2
  14.0 1.1 constant_dynamic-slice_fusion
  15.1 0.0 all-gather.14.cloned.1.call-update
  15.1 0.0 all-gather.12.cloned.1.call-start
  15.1 0.0 copy-done.3
  15.2 0.1 reshape.85
  15.2 0.0 copy-done.6
  15.3 0.1 pad_add_fusion
  15.3 0.1 dynamic_slice.15
  15.4 0.7 fusion.22
  16.1 0.7 iota_compare_fusion
  16.8 2.1 compare_select_fusion.2
  18.8 0.1 add_compare_fusion
  18.9 0.6 gather_fusion.1
  19.6 0.0 copy-start.4
  19.6 110.7 %all-gather.10.cloned.1.call-done = bf16[5120,768]{1,0:T(8,128)(2,1)} async-done(((bf16[640,768]{1,0:T(8,128)(2,1)}), bf16[5120,768]{1,0:T(8,128)(2,1)}) %all-gather.10.cloned.1.call-update) | async-done | bytes 7864336 | tf_op jit(solution)/shard_map/all_gather | solution.py:63
  130.2 12.5 %bitcast_multiply_fusion.1 = (f32[768,768]{0,1:T(8,128)}, f32[768,768]{1,0:T(8,128)}) fusion(bf16[5120,768]{1,0:T(8,128)(2,1)} %all-gather.10.cloned.1.call-done, bf16[768,5120]{1,0:T(8,128)(2,1)} %param.9), kind=kOutput, calls=%fused_computation.23 | convolution fusion | flops 6040387584 | bytes 20447232 | tf_op jit(solution)/shard_map/dot_general | solution.py:69
  142.7 1.8 reduce_sum.28
  144.5 0.0 copy-done.4
  144.5 1.9 fusion.11
  146.5 2.7 collective-permute-start.2
  149.2 1.3 collective-permute-start.3
  150.5 120.9 %all-gather.6.cloned.1.call-done = bf16[5120,768]{1,0:T(8,128)(2,1)} async-done(((bf16[640,768]{1,0:T(8,128)(2,1)}), bf16[5120,768]{1,0:T(8,128)(2,1)}) %all-gather.6.cloned.1.call-update) | async-done | bytes 7864336 | tf_op jit(solution)/shard_map/all_gather | solution.py:63
  271.4 11.7 %fusion.17 = bf16[768,768]{1,0:T(8,128)(2,1)} fusion(bf16[768,5120]{1,0:T(8,128)(2,1)} %param.9, bf16[5120,768]{1,0:T(8,128)(2,1)} %all-gather.6.cloned.1.call-done), kind=kOutput, calls=%fused_computation.30 | convolution fusion | flops 6040387584 | bytes 16908288 | tf_op jit(solution)/shard_map/dot_general | solution.py:69
  283.1 2.8 collective-permute-start
  285.9 1.5 collective-permute-start.1
  287.4 127.6 %all-gather.8.cloned.1.call-done = bf16[5120,768]{1,0:T(8,128)(2,1)} async-done(((bf16[640,768]{1,0:T(8,128)(2,1)}), bf16[5120,768]{1,0:T(8,128)(2,1)}) %all-gather.8.cloned.1.call-update) | async-done | bytes 7864336 | tf_op jit(solution)/shard_map/all_gather | solution.py:63
  415.0 12.4 %bitcast_multiply_fusion.3 = (f32[768,768]{0,1:T(8,128)}, f32[768,768]{1,0:T(8,128)}) fusion(bf16[5120,768]{1,0:T(8,128)(2,1)} %all-gather.8.cloned.1.call-done, bf16[768,5120]{1,0:T(8,128)(2,1)} %param.9), kind=kOutput, calls=%fused_computation.27 | convolution fusion | flops 6040387584 | bytes 20447232 | tf_op jit(solution)/shard_map/dot_general | solution.py:69
  427.4 1.8 reduce_sum.27
  429.2 0.0 copy-done.5
  429.2 2.9 fusion.13
  432.2 2.8 reshape.116
  435.0 0.0 collective-permute-done.2
  435.0 0.0 collective-permute-done.3
  435.0 3.2 pad_maximum_fusion.1
  438.2 5.8 copy.12
  444.0 8.5 %gather_fusion.2 = bf16[48,128,768]{2,1,0:T(8,128)(2,1)} fusion(bf16[18,128,768]{2,1,0:T(8,128)(2,1)} %bitcast.46, s32[1024]{0:T(1024)S(1)} %pad_clamp_fusion), kind=kCustom, calls=%fused_computation.2 | custom fusion | bytes 18874560 | tf_op jit(solution)/shard_map/gather | solution.py:32
  452.4 20.2 %reshape.81 = bf16[6,1024,6,128]{3,2,1,0:T(8,128)(2,1)} reshape(bf16[48,128,768]{2,1,0:T(8,128)(2,1)} %gather_fusion.2) | data formatting | bytes 18874368 | tf_op jit(solution)/shard_map/reshape | solution.py:32
  472.6 0.0 collective-permute-done
  472.6 0.0 collective-permute-done.1
  472.6 3.4 pad_maximum_fusion
  476.1 8.4 %gather_fusion = bf16[48,128,768]{2,1,0:T(8,128)(2,1)} fusion(bf16[18,128,768]{2,1,0:T(8,128)(2,1)} %bitcast.45, s32[1024]{0:T(1024)S(1)} %pad_clamp_fusion), kind=kCustom, calls=%fused_computation | custom fusion | bytes 18874560 | tf_op jit(solution)/shard_map/gather | solution.py:35
  484.5 20.1 %reshape.78 = bf16[6,1024,6,128]{3,2,1,0:T(8,128)(2,1)} reshape(bf16[48,128,768]{2,1,0:T(8,128)(2,1)} %gather_fusion) | data formatting | bytes 18874368 | tf_op jit(solution)/shard_map/reshape | solution.py:35
  504.6 13.7 %fusion.4 = f32[6,6,128,1024]{3,2,1,0:T(8,128)} fusion(bf16[6,1024,6,128]{3,2,1,0:T(8,128)(2,1)} %reshape.81, bf16[6,128,6,128]{1,0,3,2:T(8,128)(2,1)S(1)} %reshape.116), kind=kOutput, calls=%fused_computation.10 | convolution fusion | flops 1207959552 | bytes 29491200 | tf_op jit(solution)/shard_map/iqhd,ikhd->ihqk/dot_general | solution.py:45
  518.4 21.8 %fusion.23 = (f32[6,6,128]{2,1,0:T(8,128)S(1)}, f32[6,6,128,1024]{3,2,1,0:T(8,128)}) fusion(f32[6,6,128,1024]{3,2,1,0:T(8,128)} %fusion.4, pred[6,1024]{1,0:T(8,128)(4,1)S(1)} %broadcast_in_dim.58), kind=kOutput, calls=%fused_computation.54 | output fusion | flops 28312576 | bytes 37773312 | tf_op jit(solution)/shard_map/sub | solution.py:51
  540.2 12.6 %fusion.14 = bf16[6,128,6,128]{1,3,2,0:T(8,128)(2,1)S(1)} fusion(f32[6,6,128,1024]{3,2,1,0:T(8,128)} %get-tuple-element.13, f32[6,6,128]{2,1,0:T(8,128)S(1)} %get-tuple-element.12, bf16[6,1024,6,128]{3,2,1,0:T(8,128)(2,1)} %reshape.78), kind=kOutput, calls=%fused_computation.28 | convolution fusion | flops 1217396736 | bytes 29509632 | tf_op jit(solution)/shard_map/ihqk,ikhd->iqhd/dot_general | solution.py:53
  552.8 0.9 copy.16
  553.8 1.3 fusion.9
  555.0 0.0 all-gather.12.cloned.1.call-update
  555.1 0.0 all-gather.14.cloned.1.call-done
  555.1 36.0 %all-gather.12.cloned.1.call-done = bf16[768,3072]{1,0:T(8,128)(2,1)} async-done(((bf16[768,768]{1,0:T(8,128)(2,1)}), bf16[768,3072]{1,0:T(8,128)(2,1)}) %all-gather.12.cloned.1.call-update) | async-done | bytes 4718608 | tf_op jit(solution)/shard_map/all_gather | solution.py:86
  591.1 11.4 %convolution_convert_fusion = bf16[768,1280]{1,0:T(8,128)(2,1)} fusion(bf16[768,3072]{1,0:T(8,128)(2,1)} %all-gather.12.cloned.1.call-done, bf16[3072,1280]{1,0:T(8,128)(2,1)} %all-gather.14.cloned.1.call-done), kind=kOutput, calls=%fused_computation.17 | convolution fusion | flops 6040780800 | bytes 14548992 | tf_op jit(solution)/shard_map/dot_general | solution.py:87
  (11 shorter events, 0.1 us)
Async XLA Ops:
  6.5 1.5 copy-start
  6.5 123.7 %all-gather.10.cloned.1.call-start = ((), (), s32[]{:S(2)}) async-start(), calls=%async_computation.2 | async-start | bytes 8847360 | tf_op jit(solution)/shard_map/all_gather | solution.py:63
  9.1 4.9 copy-start.2
  9.1 6.0 copy-start.3
  9.1 6.2 %copy-start.6 = (s32[4]{0:T(128)S(1)}, s32[4]{0:T(128)}, u32[]{:S(2)}) copy-start(s32[4]{0:T(128)} %param.17) | copy-start | bytes 52
  9.1 262.3 %all-gather.6.cloned.1.call-start = ((), (), s32[]{:S(2)}) async-start(), calls=%async_computation | async-start | bytes 8847360 | tf_op jit(solution)/shard_map/all_gather | solution.py:63
  11.6 403.4 %all-gather.8.cloned.1.call-start = ((), (), s32[]{:S(2)}) async-start(), calls=%async_computation.1 | async-start | bytes 8847360 | tf_op jit(solution)/shard_map/all_gather | solution.py:63
  13.9 541.1 %all-gather.14.cloned.1.call-start = ((), (), s32[]{:S(2)}) async-start(), calls=%async_computation.4 | async-start | bytes 8847360 | tf_op jit(solution)/shard_map/all_gather | solution.py:63
  15.1 576.0 %all-gather.12.cloned.1.call-start = ((), (), s32[]{:S(2)}) async-start(), calls=%async_computation.3 | async-start | bytes 5898240 | tf_op jit(solution)/shard_map/all_gather | solution.py:86
  19.6 125.0 %copy-start.4 = (f32[768]{0:T(1024)S(1)}, f32[768]{0:T(1024)}, u32[]{:S(2)}) copy-start(f32[768]{0:T(1024)} %param.14) | copy-start | bytes 9220
  146.5 288.6 %collective-permute-start.2 = (bf16[768,768]{0,1:T(8,128)(2,1)S(1)}, bf16[768,768]{0,1:T(8,128)(2,1)}, u32[]{:S(2)}, u32[]{:S(2)}) collective-permute-start(bf16[768,768]{0,1:T(8,128)(2,1)S(1)} %fusion.11), channel_id=1, source_target_pairs={{0,4},{4,8},{8,12},{1,5},{5,9},{9,13},{2,6},{6,10},{10,14},{3,7},{... | collective-permute-start | bytes 3538952 | tf_op jit(solution)/shard_map/ppermute | solution.py:15
  149.2 285.8 %collective-permute-start.3 = (bf16[768,768]{0,1:T(8,128)(2,1)S(1)}, bf16[768,768]{0,1:T(8,128)(2,1)}, u32[]{:S(2)}, u32[]{:S(2)}) collective-permute-start(bf16[768,768]{0,1:T(8,128)(2,1)S(1)} %fusion.11), channel_id=1, source_target_pairs={{4,0},{8,4},{12,8},{5,1},{9,5},{13,9},{6,2},{10,6},{14,10},{7,3},{... | collective-permute-start | bytes 3538952 | tf_op jit(solution)/shard_map/ppermute | solution.py:15
  283.1 146.2 %copy-start.5 = (f32[768]{0:T(1024)S(1)}, f32[768]{0:T(1024)}, u32[]{:S(2)}) copy-start(f32[768]{0:T(1024)} %param.13) | copy-start | bytes 9220
  283.1 189.6 %collective-permute-start = (bf16[768,768]{1,0:T(8,128)(2,1)}, bf16[768,768]{1,0:T(8,128)(2,1)}, u32[]{:S(2)}, u32[]{:S(2)}) collective-permute-start(bf16[768,768]{1,0:T(8,128)(2,1)} %fusion.17), channel_id=1, source_target_pairs={{0,4},{4,8},{8,12},{1,5},{5,9},{9,13},{2,6},{6,10},{10,14},{3,7},{... | collective-permute-start | bytes 3538952 | tf_op jit(solution)/shard_map/ppermute | solution.py:15
  285.9 186.7 %collective-permute-start.1 = (bf16[768,768]{1,0:T(8,128)(2,1)}, bf16[768,768]{1,0:T(8,128)(2,1)}, u32[]{:S(2)}, u32[]{:S(2)}) collective-permute-start(bf16[768,768]{1,0:T(8,128)(2,1)} %fusion.17), channel_id=1, source_target_pairs={{4,0},{8,4},{12,8},{5,1},{9,5},{13,9},{6,2},{10,6},{14,10},{7,3},{... | collective-permute-start | bytes 3538952 | tf_op jit(solution)/shard_map/ppermute | solution.py:15
  591.1 11.5 %copy-start.1 = (bf16[1280,768]{1,0:T(8,128)(2,1)S(1)}, bf16[1280,768]{1,0:T(8,128)(2,1)}, u32[]{:S(2)}) copy-start(bf16[1280,768]{1,0:T(8,128)(2,1)} %param.11) | copy-start | bytes 5898244
Sparse Core Ops, SparseCore 0:
  9.5 120.6 all-gather.9
  132.4 138.9 all-gather.5
  273.6 141.3 all-gather.7
  417.1 116.0 all-gather.13
  555.2 35.8 all-gather.11

commit v2 on v0

--- a/solution.py
+++ b/solution.py
@@ -56,17 +56,62 @@
     return jnp.where(own_rows[:, None], mixed, 0.0).astype(jnp.bfloat16)
 
 
+def split_gather(piece):
+    parts = lax.axis_size("clips")
+    chunks = lax.axis_size("frames")
+    assert parts == 2
+    ci = lax.axis_index("clips")
+    fi = lax.axis_index("frames")
+    rows, cols = piece.shape
+    share = rows // parts
+    halves = piece.reshape(parts, share, cols)
+    mine = lax.dynamic_index_in_dim(halves, ci, 0, keepdims=False)
+    other = lax.dynamic_index_in_dim(halves, 1 - ci, 0, keepdims=False)
+    got = lax.all_gather(mine, "frames", axis=0, tiled=False)
+    foreign = jnp.arange(chunks - 1, dtype=jnp.int32)
+    foreign = foreign + (foreign >= fi).astype(jnp.int32)
+    sent = got[foreign]
+    recv = lax.ppermute(sent, "clips", [(0, 1), (1, 0)])
+    return (
+        got.reshape(chunks * share, cols),
+        recv.reshape((chunks - 1) * share, cols),
+        other,
+    ), (ci, fi, foreign)
+
+
+def split_cols(x, share, where):
+    ci, fi, foreign = where
+    n, width = x.shape
+    parts = 2
+    chunks = width // (parts * share)
+    blocks = x.reshape(n, chunks, parts, share)
+    mine = lax.dynamic_index_in_dim(blocks, ci, 2, keepdims=False)
+    other = lax.dynamic_index_in_dim(blocks, 1 - ci, 2, keepdims=False)
+    return (
+        mine.reshape(n, chunks * share),
+        other[:, foreign].reshape(n, (chunks - 1) * share),
+        lax.dynamic_index_in_dim(other, fi, 1, keepdims=False),
+    )
+
+
+def split_dot(cols, rows):
+    total = None
+    for a, b in zip(cols, rows):
+        part = jnp.dot(a, b, preferred_element_type=jnp.float32)
+        total = part if total is None else total + part
+    return total
+
+
 def per_device(tokens, w_query, w_key, w_value, q_gain, k_gain, w_out, key_blocks, slab_counts):
-
-    def project(piece):
-        return jnp.dot(tokens, piece, preferred_element_type=jnp.float32)
-
-    query_raw = project(lax.all_gather(w_query, "frames", axis=0, tiled=True))
-    key_raw = project(lax.all_gather(w_key, "frames", axis=0, tiled=True))
-    value_raw = project(lax.all_gather(w_value, "frames", axis=0, tiled=True))
-    query = head_norm(query_raw, q_gain)
-    keys = head_norm(key_raw, k_gain)
-    values = value_raw.astype(jnp.bfloat16)
+    share = w_query.shape[0] // lax.axis_size("clips")
+    k_rows, where = split_gather(w_key)
+    v_rows, _ = split_gather(w_value)
+    q_rows, _ = split_gather(w_query)
+    o_rows, _ = split_gather(w_out)
+    token_cols = split_cols(tokens, share, where)
+    query = head_norm(split_dot(token_cols, q_rows), q_gain)
+    keys = head_norm(split_dot(token_cols, k_rows), k_gain)
+    values = split_dot(token_cols, v_rows).astype(jnp.bfloat16)
     before = shifted((keys, values), "frames", 1)
     after = shifted((keys, values), "frames", -1)
     key_window = jnp.concatenate([before[0], keys, after[0]], axis=0)
@@ -77,11 +122,8 @@
     limits = lax.dynamic_slice_in_dim(count_pad, position, 3, 0)
     attended = attend(query, key_window, value_window, key_blocks, limits)
     whole = lax.all_gather(attended, "wshard", axis=1, tiled=True)
-    mixed = jnp.dot(
-        whole,
-        lax.all_gather(w_out, "frames", axis=0, tiled=True),
-        preferred_element_type=jnp.float32,
-    )
+    out_share = w_out.shape[0] // lax.axis_size("clips")
+    mixed = split_dot(split_cols(whole, out_share, where), o_rows)
     return mixed.astype(jnp.bfloat16)
 
 

time: 682 us -> 573 us (0.84)
  waiting for transfers between devices: 486 us -> 229 us
  local copies, waits for them, and re-layouts: 62.6 us -> 173 us
  matrix products: 73.5 us -> 88.6 us
  starting transfers between devices: 7.66 us -> 17.3 us
    all_gather x4, waiting for transfers between devices: 446 us -> 170 us  [split_gather(): got = lax.all_gather(mine, 'frames', axis=0, tiled=False)]
    gather x0 -> x8, local copies, waits for them, and re-layouts: none -> 37.7 us  [the longest x6 29.3 us: split_gather(): sent = got[foreign]]
    unnamed x12 -> x35, local copies, waits for them, and re-layouts: 0.02 us -> 24.6 us
    dynamic_slice x0 -> x6, local copies, waits for them, and re-layouts: none -> 22.5 us  [the longest x1 12.2 us: split_cols(): other = lax.dynamic_index_in_dim(blocks, 1 - ci, 2, keepdims=False)]
    ppermute x0 -> x4, waiting for transfers between devices: none -> 18.4 us  [split_gather(): recv = lax.ppermute(sent, 'clips', [(0, 1), (1, 0)])]
    dot_general x4 -> x12, matrix products: 47 us -> 61.3 us  [split_dot(): part = jnp.dot(a, b, preferred_element_type=jnp.float32)]
    reshape x0 -> x1, local copies, waits for them, and re-layouts: none -> 11.6 us  [split_cols(): blocks = x.reshape(n, chunks, parts, share)]
    ppermute x4, waiting for transfers between devices: 0.01 us -> 9.23 us  [shifted(): return lax.ppermute(value, axis, pairs)]
  transfers between devices with their start and end apart: 9 -> 13, of which waited for: 5 -> 7; matrix products, arithmetic and copies ran while one was open for 24% -> 52% of each run, Pallas kernels for 0% -> 0%
where the time goes in v2:
time: 573 us; the launch traced here: 565 us
  waiting for transfers between devices  229 us (40%)
  local copies, waits for them, and re-layouts  173 us (30%)
  matrix products  88.6 us (15%)
  other arithmetic  43.5 us (8%)
  starting transfers between devices  17.3 us (3%)
  between operations  13.7 us (2%)
    all_gather x4, waiting for transfers between devices, split_gather(): got = lax.all_gather(mine, 'frames', axis=0, tiled=False)  170 us
    dot_general x12, matrix products, split_dot(): part = jnp.dot(a, b, preferred_element_type=jnp.float32)  61.3 us
    all_gather x1, waiting for transfers between devices, per_device(): whole = lax.all_gather(attended, 'wshard', axis=1, tiled=True)  31.5 us
    gather x6, local copies, waits for them, and re-layouts, split_gather(): sent = got[foreign]  29.3 us
    unnamed x35, local copies, waits for them, and re-layouts  24.6 us
    sub x1, other arithmetic, attend(): expo = jnp.exp(scores - top)  22 us
    reshape x1, local copies, waits for them, and re-layouts, attend(): keys.reshape(window, TILE, cols)[blocks]  20.2 us
    reshape x1, local copies, waits for them, and re-layouts, attend(): values.reshape(window, TILE, cols)[blocks]  20.1 us
  transfers between devices with their start and end apart: 13, of which 7 were waited for; matrix products, arithmetic and copies ran while one was open for 52% of the time, Pallas kernels for 0%

profile of v2, /device:TPU:0, one launch (start us, length us, event | category | flops | bytes accessed | tf_op | source)
XLA Modules:
  0.0 564.7 jit_solution(12020693938749021446)
XLA Ops:
  6.5 2.3 constant_dynamic-slice_fusion.4
  9.0 2.3 constant_dynamic-slice_fusion.6
  11.3 2.2 constant_dynamic-slice_fusion.5
  14.7 10.8 %copy.46 = bf16[768,5120]{0,1:T(8,128)(2,1)} copy(bf16[768,5120]{1,0:T(8,128)(2,1)} %param.9) | data formatting | bytes 15728640 | tf_op args[0]
  25.5 7.2 %dynamic-slice_bitcast_fusion = (bf16[768,4,640]{0,2,1:T(8,128)(2,1)}, bf16[768,4,1,640]{0,3,2,1:T(8,128)(2,1)}) fusion(bf16[768,4,2,640]{0,3,2,1:T(8,128)(2,1)} %bitcast.128, s32[]{:T(128)S(6)} %select_n.101, s32[]{:T(128)S(6)} %select_n.100), kind=kLoop, calls=%fused_computation.23 | loop fusion | bytes 15728648 | tf_op jit(solution)/shard_map/jit(dynamic_index_in_dim)/squeeze | solution.py:89
  33.6 1.9 compare_select_fusion.3
  36.3 4.1 fusion.41
  40.3 4.6 gather_fusion
  45.0 43.2 %all-gather.10.cloned.1.call-done = bf16[4,640,768]{2,1,0:T(8,128)(2,1)} async-done(((bf16[1,640,768]{2,1,0:T(8,128)(2,1)}), bf16[4,640,768]{2,1,0:T(8,128)(2,1)}) %all-gather.10.cloned.1.call-update) | async-done | bytes 3932176 | tf_op jit(solution)/shard_map/all_gather | solution.py:70
  88.2 4.5 gather_fusion.5
  92.7 5.5 copy.54
  98.2 1.5 collective-permute-start.4
  99.7 1.3 iota_compare_fusion
  101.0 4.1 fusion.39
  105.1 3.7 fusion.37
  108.8 55.9 %all-gather.6.cloned.1.call-done = bf16[4,640,768]{2,1,0:T(8,128)(2,1)} async-done(((bf16[1,640,768]{2,1,0:T(8,128)(2,1)}), bf16[4,640,768]{2,1,0:T(8,128)(2,1)}) %all-gather.6.cloned.1.call-update) | async-done | bytes 3932176 | tf_op jit(solution)/shard_map/all_gather | solution.py:70
  164.8 4.5 gather_fusion.1
  169.3 1.5 collective-permute-start
  170.7 70.6 %all-gather.8.cloned.1.call-done = bf16[4,640,768]{2,1,0:T(8,128)(2,1)} async-done(((bf16[1,640,768]{2,1,0:T(8,128)(2,1)}), bf16[4,640,768]{2,1,0:T(8,128)(2,1)}) %all-gather.8.cloned.1.call-update) | async-done | bytes 3932176 | tf_op jit(solution)/shard_map/all_gather | solution.py:70
  241.3 4.6 gather_fusion.4
  245.9 5.6 copy.51
  251.5 1.6 collective-permute-start.3
  253.1 8.1 %fusion.67 = f32[768,768]{1,0:T(8,128)} fusion(bf16[768,2560]{0,1:T(8,128)(2,1)} %bitcast.134, bf16[2560,768]{1,0:T(8,128)(2,1)} %bitcast.142), kind=kOutput, calls=%fused_computation.109 | convolution fusion | flops 3019898880 | bytes 10223616 | tf_op jit(solution)/shard_map/dot_general | solution.py:100
  261.3 4.9 fusion.68
  266.2 3.6 fusion.69
  269.8 6.7 %fusion.64 = (f32[768,768]{0,1:T(8,128)}, f32[768,768]{0,1:T(8,128)}) fusion(f32[768,768]{0,1:T(8,128)S(1)} %copy-done.14, f32[768,768]{0,1:T(8,128)S(1)} %fusion.69, bf16[3,640,768]{1,2,0:T(8,128)(2,1)} %collective-permute-done.4, bf16[3,768,640]{1,2,0:T(8,128)(2,1)S(1)} %copy-done.1), kind=kOutput, calls=%fused_computation.106 | convolution fusion | flops 2266693632 | bytes 15335424 | tf_op jit(solution)/shard_map/dot_general | solution.py:100
  276.5 1.8 reduce_sum.28
  278.4 3.5 fusion.18
  281.9 2.6 collective-permute-start.5
  284.4 1.3 collective-permute-start.6
  285.7 6.3 %fusion.24 = bf16[768,768]{1,0:T(8,128)(2,1)} fusion(f32[768,768]{1,0:T(8,128)} %fusion.41, f32[768,768]{1,0:T(8,128)} %fusion.67, bf16[3,640,768]{2,1,0:T(8,128)(2,1)} %collective-permute-done, bf16[3,768,640]{1,2,0:T(8,128)(2,1)S(1)} %copy-done.2), kind=kOutput, calls=%fused_computation.48 | convolution fusion | flops 2266693632 | bytes 11796480 | tf_op jit(solution)/shard_map/dot_general | solution.py:100
  292.0 5.7 %collective-permute-start.1 = (bf16[768,768]{1,0:T(8,128)(2,1)}, bf16[768,768]{1,0:T(8,128)(2,1)}, u32[]{:S(2)}, u32[]{:S(2)}) collective-permute-start(bf16[768,768]{1,0:T(8,128)(2,1)} %fusion.24), channel_id=1, source_target_pairs={{0,4},{4,8},{8,12},{1,5},{5,9},{9,13},{2,6},{6,10},{10,14},{3,7},{... | collective-permute-start | bytes 3538952 | tf_op jit(solution)/shard_map/ppermute | solution.py:15
  297.8 1.3 collective-permute-start.2
  299.1 18.4 %collective-permute-done.3 = bf16[3,640,768]{1,2,0:T(8,128)(2,1)} collective-permute-done((bf16[3,640,768]{1,2,0:T(8,128)(2,1)}, bf16[3,640,768]{1,2,0:T(8,128)(2,1)}, u32[]{:S(2)}, u32[]{:S(2)}) %collective-permute-start.3) | collective-permute-done | bytes 2949152 | tf_op jit(solution)/shard_map/ppermute | solution.py:74
  317.4 6.6 %fusion.65 = (f32[768,768]{0,1:T(8,128)}, f32[768,768]{0,1:T(8,128)}) fusion(f32[768,768]{0,1:T(8,128)S(1)} %copy-done.13, f32[768,768]{0,1:T(8,128)S(1)} %copy-done.15, bf16[3,640,768]{1,2,0:T(8,128)(2,1)} %collective-permute-done.3, bf16[3,768,640]{1,2,0:T(8,128)(2,1)S(1)} %copy-done.2), kind=kOutput, calls=%fused_computation.107 | convolution fusion | flops 2266693632 | bytes 15335424 | tf_op jit(solution)/shard_map/dot_general | solution.py:100
  324.0 1.8 reduce_sum.27
  325.9 3.0 fusion.21
  328.8 2.8 reshape.253
  331.7 3.7 collective-permute-done.5
  335.4 5.5 collective-permute-done.6
  340.9 3.3 pad_maximum_fusion.1
  344.2 5.8 %copy.56 = bf16[2304,768]{1,0:T(8,128)(2,1)} copy(bf16[2304,768]{0,1:T(8,128)(2,1)} %pad_maximum_fusion.1) | data formatting | bytes 7077888 | tf_op jit(solution)/shard_map/concatenate | solution.py:117
  350.0 8.4 %gather_fusion.6 = bf16[48,128,768]{2,1,0:T(8,128)(2,1)} fusion(bf16[18,128,768]{2,1,0:T(8,128)(2,1)} %bitcast.127, s32[1024]{0:T(1024)S(1)} %pad_clamp_fusion), kind=kCustom, calls=%fused_computation.6 | custom fusion | bytes 18874560 | tf_op jit(solution)/shard_map/gather | solution.py:32
  358.3 20.2 %reshape.162 = bf16[6,1024,6,128]{3,2,1,0:T(8,128)(2,1)} reshape(bf16[48,128,768]{2,1,0:T(8,128)(2,1)} %gather_fusion.6) | data formatting | bytes 18874368 | tf_op jit(solution)/shard_map/reshape | solution.py:32
  378.5 13.7 %fusion.4 = f32[6,6,128,1024]{3,2,1,0:T(8,128)} fusion(bf16[6,1024,6,128]{3,2,1,0:T(8,128)(2,1)} %reshape.162, bf16[6,128,6,128]{1,0,3,2:T(8,128)(2,1)S(1)} %reshape.253), kind=kOutput, calls=%fused_computation.16 | convolution fusion | flops 1207959552 | bytes 29491200 | tf_op jit(solution)/shard_map/iqhd,ikhd->ihqk/dot_general | solution.py:45
  392.2 3.5 pad_maximum_fusion
  395.7 8.4 %gather_fusion.2 = bf16[48,128,768]{2,1,0:T(8,128)(2,1)} fusion(bf16[18,128,768]{2,1,0:T(8,128)(2,1)} %bitcast.126, s32[1024]{0:T(1024)S(1)} %pad_clamp_fusion), kind=kCustom, calls=%fused_computation.2 | custom fusion | bytes 18874560 | tf_op jit(solution)/shard_map/gather | solution.py:35
  404.1 20.1 %reshape.155 = bf16[6,1024,6,128]{3,2,1,0:T(8,128)(2,1)} reshape(bf16[48,128,768]{2,1,0:T(8,128)(2,1)} %gather_fusion.2) | data formatting | bytes 18874368 | tf_op jit(solution)/shard_map/reshape | solution.py:35
  424.2 22.0 %fusion.66 = (f32[6,6,128]{2,1,0:T(8,128)S(1)}, f32[6,6,128,1024]{3,2,1,0:T(8,128)}) fusion(f32[6,6,128,1024]{3,2,1,0:T(8,128)} %fusion.4, pred[6,1024]{1,0:T(8,128)(4,1)S(1)} %broadcast_in_dim.64), kind=kOutput, calls=%fused_computation.108 | output fusion | flops 28312576 | bytes 37773312 | tf_op jit(solution)/shard_map/sub | solution.py:51
  446.2 13.6 %fusion.27 = bf16[6,128,6,128]{1,3,2,0:T(8,128)(2,1)} fusion(f32[6,6,128,1024]{3,2,1,0:T(8,128)} %get-tuple-element.17, f32[6,6,128]{2,1,0:T(8,128)S(1)} %get-tuple-element.16, bf16[6,1024,6,128]{3,2,1,0:T(8,128)(2,1)} %reshape.155), kind=kOutput, calls=%fused_computation.51 | convolution fusion | flops 1217396736 | bytes 29509632 | tf_op jit(solution)/shard_map/ihqk,ikhd->iqhd/dot_general | solution.py:53
  459.8 1.9 copy.60
  461.7 1.3 fusion.16
  463.1 4.5 gather_fusion.8
  467.6 1.8 collective-permute-start.7
  469.4 31.5 %all-gather.12.cloned.1.call-done = bf16[768,3072]{1,0:T(8,128)(2,1)} async-done(((bf16[768,768]{1,0:T(8,128)(2,1)}), bf16[768,3072]{1,0:T(8,128)(2,1)}) %all-gather.12.cloned.1.call-update) | async-done | bytes 4718608 | tf_op jit(solution)/shard_map/all_gather | solution.py:124
  500.8 11.6 %reshape.164 = bf16[768,4,2,384]{3,2,1,0:T(2,128)(2,1)} reshape(bf16[768,3072]{1,0:T(8,128)(2,1)} %all-gather.12.cloned.1.call-done) | data formatting | bytes 9437184 | tf_op jit(solution)/shard_map/reshape | solution.py:87
  512.5 12.2 %constant_dynamic-slice_fusion.1 = (bf16[768,4,1,384]{3,2,1,0:T(2,128)(2,1)S(1)}, bf16[768,4,1,384]{3,2,1,0:T(2,128)(2,1)}) fusion(bf16[768,4,2,384]{3,2,1,0:T(2,128)(2,1)} %reshape.164, s32[]{:T(128)S(6)} %select_n.101, s32[]{:T(128)S(6)} %select_n.100), kind=kLoop, calls=%fused_computation.80 | loop fusion | bytes 9437192 | tf_op jit(solution)/shard_map/jit(dynamic_index_in_dim)/dynamic_slice | solution.py:89
  524.7 1.8 copy.86
  526.5 3.7 gather_fusion.7
  530.2 11.9 %copy.70 = bf16[768,4,1,384]{0,3,1,2:T(8,128)(2,1)} copy(bf16[768,4,1,384]{3,2,1,0:T(2,128)(2,1)} %get-tuple-element.8) | data formatting | bytes 4718592
  542.2 2.5 constant_dynamic-slice_fusion
  544.7 6.2 %fusion.70 = f32[768,1280]{1,0:T(8,128)S(1)} fusion(bf16[768,1536]{0,1:T(8,128)(2,1)} %bitcast.137, bf16[1536,1280]{1,0:T(8,128)(2,1)} %bitcast.140), kind=kOutput, calls=%fused_computation.112 | convolution fusion | flops 3019898880 | bytes 10223616 | tf_op jit(solution)/shard_map/dot_general | solution.py:100
  550.9 4.6 fusion.25
  555.5 2.5 fusion.9
  (62 shorter events, 3.0 us)
Async XLA Ops:
  6.5 7.1 %copy-start = (bf16[768,1280]{1,0:T(8,128)(2,1)S(1)}, bf16[768,1280]{1,0:T(8,128)(2,1)}, u32[]{:S(2)}) copy-start(bf16[768,1280]{1,0:T(8,128)(2,1)} %param.15) | copy-start | bytes 5898244
  6.5 81.7 %all-gather.10.cloned.1.call-start = ((), (), s32[]{:S(2)}) async-start(), calls=%async_computation.2 | async-start | bytes 4915200 | tf_op jit(solution)/shard_map/all_gather | solution.py:70
  8.9 155.8 %all-gather.6.cloned.1.call-start = ((), (), s32[]{:S(2)}) async-start(), calls=%async_computation | async-start | bytes 4915200 | tf_op jit(solution)/shard_map/all_gather | solution.py:70
  11.3 230.0 %all-gather.8.cloned.1.call-start = ((), (), s32[]{:S(2)}) async-start(), calls=%async_computation.1 | async-start | bytes 4915200 | tf_op jit(solution)/shard_map/all_gather | solution.py:70
  13.6 449.5 %all-gather.14.cloned.1.call-start = ((), (), s32[]{:S(2)}) async-start(), calls=%async_computation.4 | async-start | bytes 4915200 | tf_op jit(solution)/shard_map/all_gather | solution.py:70
  14.7 486.2 %all-gather.12.cloned.1.call-start = ((), (), s32[]{:S(2)}) async-start(), calls=%async_computation.3 | async-start | bytes 5898240 | tf_op jit(solution)/shard_map/all_gather | solution.py:124
  25.5 7.2 %copy-start.8 = (s32[6,8]{1,0:T(8,128)S(1)}, s32[6,8]{1,0:T(8,128)}, u32[]{:S(2)}) copy-start(s32[6,8]{1,0:T(8,128)} %param.16) | copy-start | bytes 580
  25.5 7.3 %copy-start.12 = (s32[4]{0:T(128)S(1)}, s32[4]{0:T(128)}, u32[]{:S(2)}) copy-start(s32[4]{0:T(128)} %param.17) | copy-start | bytes 52
  98.2 6.8 %copy-start.7 = (bf16[1280,768]{1,0:T(8,128)(2,1)S(1)}, bf16[1280,768]{1,0:T(8,128)(2,1)}, u32[]{:S(2)}) copy-start(bf16[1280,768]{1,0:T(8,128)(2,1)} %param.11) | copy-start | bytes 5898244
  98.2 171.5 %collective-permute-start.4 = (bf16[3,640,768]{1,2,0:T(8,128)(2,1)}, bf16[3,640,768]{1,2,0:T(8,128)(2,1)}, u32[]{:S(2)}, u32[]{:S(2)}) collective-permute-start(bf16[3,640,768]{1,2,0:T(8,128)(2,1)} %copy.54), channel_id=1, source_target_pairs={{0,16},{16,0},{1,17},{17,1},{2,18},{18,2},{3,19},{19,3},{4,20},{20... | collective-permute-start | bytes 8847368 | tf_op jit(solution)/shard_map/ppermute | solution.py:74
  169.3 116.5 %collective-permute-start = (bf16[3,640,768]{2,1,0:T(8,128)(2,1)}, bf16[3,640,768]{2,1,0:T(8,128)(2,1)}, u32[]{:S(2)}, u32[]{:S(2)}) collective-permute-start(bf16[3,640,768]{2,1,0:T(8,128)(2,1)} %gather_fusion.1), channel_id=1, source_target_pairs={{0,16},{16,0},{1,17},{17,1},{2,18},{18,2},{3,19},{19,3},{4,20},{20... | collective-permute-start | bytes 8847368 | tf_op jit(solution)/shard_map/ppermute | solution.py:74
  251.5 65.9 %collective-permute-start.3 = (bf16[3,640,768]{1,2,0:T(8,128)(2,1)}, bf16[3,640,768]{1,2,0:T(8,128)(2,1)}, u32[]{:S(2)}, u32[]{:S(2)}) collective-permute-start(bf16[3,640,768]{1,2,0:T(8,128)(2,1)} %copy.51), channel_id=1, source_target_pairs={{0,16},{16,0},{1,17},{17,1},{2,18},{18,2},{3,19},{19,3},{4,20},{20... | collective-permute-start | bytes 8847368 | tf_op jit(solution)/shard_map/ppermute | solution.py:74
  253.1 8.2 %copy-start.3 = (bf16[768,4,1,640]{0,3,2,1:T(8,128)(2,1)S(1)}, bf16[768,4,1,640]{0,3,2,1:T(8,128)(2,1)}, u32[]{:S(2)}) copy-start(bf16[768,4,1,640]{0,3,2,1:T(8,128)(2,1)} %get-tuple-element.6) | copy-start | bytes 11796484
  253.1 8.2 %copy-start.6 = (bf16[4,640,768]{2,1,0:T(8,128)(2,1)S(1)}, bf16[4,640,768]{2,1,0:T(8,128)(2,1)}, u32[]{:S(2)}) copy-start(bf16[4,640,768]{2,1,0:T(8,128)(2,1)} %all-gather.8.cloned.1.call-done) | copy-start | bytes 11796484
  261.3 4.9 copy-start.5
  266.1 3.6 copy-start.1
  266.2 3.6 copy-start.14
  269.7 8.7 %copy-start.9 = (f32[768]{0:T(1024)S(1)}, f32[768]{0:T(1024)}, u32[]{:S(2)}) copy-start(f32[768]{0:T(1024)} %param.14) | copy-start | bytes 9220
  278.3 7.4 %copy-start.2 = (bf16[3,768,640]{1,2,0:T(8,128)(2,1)S(1)}, bf16[3,768,640]{1,2,0:T(8,128)(2,1)}, u32[]{:S(2)}) copy-start(bf16[3,768,640]{1,2,0:T(8,128)(2,1)} %gather_fusion) | copy-start | bytes 8847364
  281.9 35.6 %copy-start.13 = (f32[768,768]{0,1:T(8,128)S(1)}, f32[768,768]{0,1:T(8,128)}, u32[]{:S(2)}) copy-start(f32[768,768]{0,1:T(8,128)} %fusion.39) | copy-start | bytes 7077892
  281.9 35.6 %copy-start.15 = (f32[768,768]{0,1:T(8,128)S(1)}, f32[768,768]{0,1:T(8,128)}, u32[]{:S(2)}) copy-start(f32[768,768]{0,1:T(8,128)} %fusion.68) | copy-start | bytes 7077892
  281.9 53.5 %collective-permute-start.5 = (bf16[768,768]{0,1:T(8,128)(2,1)}, bf16[768,768]{0,1:T(8,128)(2,1)}, u32[]{:S(2)}, u32[]{:S(2)}) collective-permute-start(bf16[768,768]{0,1:T(8,128)(2,1)} %fusion.18), channel_id=1, source_target_pairs={{0,4},{4,8},{8,12},{1,5},{5,9},{9,13},{2,6},{6,10},{10,14},{3,7},{... | collective-permute-start | bytes 3538952 | tf_op jit(solution)/shard_map/ppermute | solution.py:15
  284.4 56.5 %collective-permute-start.6 = (bf16[768,768]{0,1:T(8,128)(2,1)}, bf16[768,768]{0,1:T(8,128)(2,1)}, u32[]{:S(2)}, u32[]{:S(2)}) collective-permute-start(bf16[768,768]{0,1:T(8,128)(2,1)} %fusion.18), channel_id=1, source_target_pairs={{4,0},{8,4},{12,8},{5,1},{9,5},{13,9},{6,2},{10,6},{14,10},{7,3},{... | collective-permute-start | bytes 3538952 | tf_op jit(solution)/shard_map/ppermute | solution.py:15
  292.0 33.8 %copy-start.10 = (f32[768]{0:T(1024)S(1)}, f32[768]{0:T(1024)}, u32[]{:S(2)}) copy-start(f32[768]{0:T(1024)} %param.13) | copy-start | bytes 9220
  292.0 100.2 %collective-permute-start.1 = (bf16[768,768]{1,0:T(8,128)(2,1)}, bf16[768,768]{1,0:T(8,128)(2,1)}, u32[]{:S(2)}, u32[]{:S(2)}) collective-permute-start(bf16[768,768]{1,0:T(8,128)(2,1)} %fusion.24), channel_id=1, source_target_pairs={{0,4},{4,8},{8,12},{1,5},{5,9},{9,13},{2,6},{6,10},{10,14},{3,7},{... | collective-permute-start | bytes 3538952 | tf_op jit(solution)/shard_map/ppermute | solution.py:15
  297.8 94.4 %collective-permute-start.2 = (bf16[768,768]{1,0:T(8,128)(2,1)}, bf16[768,768]{1,0:T(8,128)(2,1)}, u32[]{:S(2)}, u32[]{:S(2)}) collective-permute-start(bf16[768,768]{1,0:T(8,128)(2,1)} %fusion.24), channel_id=1, source_target_pairs={{4,0},{8,4},{12,8},{5,1},{9,5},{13,9},{6,2},{10,6},{14,10},{7,3},{... | collective-permute-start | bytes 3538952 | tf_op jit(solution)/shard_map/ppermute | solution.py:15
  446.2 15.5 %copy-start.11 = (pred[768]{0:T(1024)(128)(4,1)S(1)}, pred[768]{0:T(1024)(128)(4,1)}, u32[]{:S(2)}) copy-start(pred[768]{0:T(1024)(128)(4,1)} %iota_compare_fusion) | copy-start | bytes 2308
  467.6 83.3 %collective-permute-start.7 = (bf16[3,384,1280]{2,1,0:T(8,128)(2,1)}, bf16[3,384,1280]{2,1,0:T(8,128)(2,1)}, u32[]{:S(2)}, u32[]{:S(2)}) collective-permute-start(bf16[3,384,1280]{2,1,0:T(8,128)(2,1)} %gather_fusion.8), channel_id=1, source_target_pairs={{0,16},{16,0},{1,17},{17,1},{2,18},{18,2},{3,19},{19,3},{4,20},{20... | collective-permute-start | bytes 8847368 | tf_op jit(solution)/shard_map/ppermute | solution.py:74
  544.7 6.3 %copy-start.4 = (bf16[3,768,384]{2,1,0:T(8,128)(2,1)S(1)}, bf16[3,768,384]{2,1,0:T(8,128)(2,1)}, u32[]{:S(2)}) copy-start(bf16[3,768,384]{2,1,0:T(8,128)(2,1)} %gather_fusion.7) | copy-start | bytes 5308420
Sparse Core Ops, SparseCore 0:
  9.0 79.1 all-gather.9
  89.8 74.9 all-gather.5
  166.3 74.9 all-gather.7
  242.7 100.5 all-gather.13
  463.2 37.6 all-gather.11

commit v3 on v2

--- a/solution.py
+++ b/solution.py
@@ -3,6 +3,8 @@
 import jax
 import jax.numpy as jnp
 from jax import lax
+from jax.experimental import pallas as pl
+from jax.experimental.pallas import tpu as pltpu
 from jax.sharding import PartitionSpec as P
 
 HEAD_DIM = 128
@@ -23,37 +25,69 @@
     return (normed * gain).astype(jnp.bfloat16)
 
 
-def attend(query, keys, values, blocks, limits):
+def attend_kernel(kb_ref, lim_ref, q_ref, k_ref, v_ref, o_ref):
+    tiles = q_ref.shape[0] // TILE
+    picks = kb_ref.shape[1]
+    scale = 1.0 / math.sqrt(HEAD_DIM)
+    lanes = lax.broadcasted_iota(jnp.int32, (TILE, TILE), 1)
+    rows = lax.broadcasted_iota(jnp.int32, (TILE, TILE), 0)
+
+    def one_tile(i, carry):
+        start = pl.multiple_of(i * TILE, TILE)
+        q = q_ref[pl.ds(start, TILE), :]
+        scores = []
+        for j in range(picks):
+            b = kb_ref[i, j]
+            k = k_ref[pl.ds(pl.multiple_of(b * TILE, TILE), TILE), :]
+            s = lax.dot_general(
+                q, k, (((1,), (1,)), ((), ())), preferred_element_type=jnp.float32
+            )
+            s = s * scale
+            slab = (b >= tiles).astype(jnp.int32) + (b >= 2 * tiles).astype(jnp.int32)
+            limit = lim_ref[slab]
+            pos = (b - slab * tiles) * TILE + lanes
+            scores.append(jnp.where(pos < limit, s, -1e30))
+        top = jnp.max(scores[0], axis=1, keepdims=True)
+        for s in scores[1:]:
+            top = jnp.maximum(top, jnp.max(s, axis=1, keepdims=True))
+        expo = [jnp.exp(s - top) for s in scores]
+        total = jnp.sum(expo[0], axis=1, keepdims=True)
+        for e in expo[1:]:
+            total = total + jnp.sum(e, axis=1, keepdims=True)
+        acc = None
+        for j in range(picks):
+            b = kb_ref[i, j]
+            v = v_ref[pl.ds(pl.multiple_of(b * TILE, TILE), TILE), :]
+            w = (expo[j] / total).astype(jnp.bfloat16)
+            part = jnp.dot(w, v, preferred_element_type=jnp.float32)
+            acc = part if acc is None else acc + part
+        live = start + rows < lim_ref[1]
+        o_ref[pl.ds(start, TILE), :] = jnp.where(live, acc, 0.0).astype(o_ref.dtype)
+        return carry
+
+    lax.fori_loop(0, tiles, one_tile, 0)
+
+
+def attend(query, keys, values, blocks, limits, interpret=False):
     rows, cols = query.shape
-    tiles = rows // TILE
+    window = keys.shape[0]
     heads = cols // HEAD_DIM
-    picks = blocks.shape[1]
-    window = keys.shape[0] // TILE
-    key_tiles = keys.reshape(window, TILE, cols)[blocks].reshape(
-        tiles, picks * TILE, heads, HEAD_DIM
+    spec = pltpu.PrefetchScalarGridSpec(
+        num_scalar_prefetch=2,
+        grid=(heads,),
+        in_specs=[
+            pl.BlockSpec((rows, HEAD_DIM), lambda h, kb, lim: (0, h)),
+            pl.BlockSpec((window, HEAD_DIM), lambda h, kb, lim: (0, h)),
+            pl.BlockSpec((window, HEAD_DIM), lambda h, kb, lim: (0, h)),
+        ],
+        out_specs=pl.BlockSpec((rows, HEAD_DIM), lambda h, kb, lim: (0, h)),
     )
-    value_tiles = values.reshape(window, TILE, cols)[blocks].reshape(
-        tiles, picks * TILE, heads, HEAD_DIM
-    )
-    tile_ids = jnp.arange(window, dtype=jnp.int32)
-    slab_of = tile_ids // tiles
-    limit = jnp.where(slab_of == 0, limits[0], jnp.where(slab_of == 1, limits[1], limits[2]))
-    offsets = (tile_ids % tiles)[:, None] * TILE + jnp.arange(TILE, dtype=jnp.int32)[None, :]
-    live = offsets < limit[:, None]
-    live_keys = live[blocks].reshape(tiles, picks * TILE)
-    query_tiles = query.reshape(tiles, TILE, heads, HEAD_DIM)
-    scores = jnp.einsum(
-        "iqhd,ikhd->ihqk", query_tiles, key_tiles, preferred_element_type=jnp.float32
-    )
-    scores = scores * (1.0 / math.sqrt(HEAD_DIM))
-    scores = jnp.where(live_keys[:, None, None, :], scores, -1e30)
-    top = jnp.max(scores, axis=-1, keepdims=True)
-    expo = jnp.exp(scores - top)
-    weights = (expo / jnp.sum(expo, axis=-1, keepdims=True)).astype(jnp.bfloat16)
-    mixed = jnp.einsum("ihqk,ikhd->iqhd", weights, value_tiles, preferred_element_type=jnp.float32)
-    mixed = mixed.reshape(rows, cols)
-    own_rows = jnp.arange(rows, dtype=jnp.int32) < limits[1]
-    return jnp.where(own_rows[:, None], mixed, 0.0).astype(jnp.bfloat16)
+    return pl.pallas_call(
+        attend_kernel,
+        grid_spec=spec,
+        out_shape=jax.ShapeDtypeStruct((rows, cols), jnp.bfloat16),
+        interpret=interpret,
+    )(blocks.astype(jnp.int32), limits.astype(jnp.int32), query, keys, values)
 
 
 def split_gather(piece):

time: 573 us -> 515 us (0.90)
  local copies, waits for them, and re-layouts: 173 us -> 123 us
  Pallas kernels: 0 us -> 34.9 us
  matrix products: 88.6 us -> 59.7 us
  other arithmetic: 43.5 us -> 18.1 us
  waiting for transfers between devices: 229 us -> 239 us
    reshape x3 -> x0, local copies, waits for them, and re-layouts: 43.2 us -> none  [the longest x1 20.2 us: attend(): keys.reshape(window, TILE, cols)[blocks]]
    pallas_call x0 -> x1, Pallas kernels: none -> 34.9 us  [attend(): pl.pallas_call(attend_kernel, grid_spec=spec, out_shape=jax.ShapeDtypeStr...]
    dot_general x2 -> x0, matrix products: 27.3 us -> none  [the longest x1 13.7 us: attend(): jnp.einsum('iqhd,ikhd->ihqk', query_tiles, key_tiles, preferred_element_t...]
    sub x1 -> x0, other arithmetic: 22 us -> none  [attend(): expo = jnp.exp(scores - top)]
    gather x3 -> x0, local copies, waits for them, and re-layouts: 17.3 us -> none  [the longest x1 8.36 us: attend(): values.reshape(window, TILE, cols)[blocks]]
    mul x0 -> x6, local copies, waits for them, and re-layouts: none -> 15.7 us  [the longest x4 9.55 us: head_norm(): normed = (split * lax.rsqrt(square + 1e-06)).reshape(rows, cols)]
    ppermute x4, waiting for transfers between devices: 9.23 us -> 19.4 us  [shifted(): return lax.ppermute(value, axis, pairs)]
    concatenate x1 -> x0, local copies, waits for them, and re-layouts: 5.79 us -> none  [per_device(): key_window = jnp.concatenate([before[0], keys, after[0]], axis=0)]
  transfers between devices with their start and end apart: 13 -> 13, of which waited for: 7 -> 6; matrix products, arithmetic and copies ran while one was open for 52% -> 38% of each run, Pallas kernels for 0% -> 7%
where the time goes in v3:
time: 515 us; the launch traced here: 508 us
  waiting for transfers between devices  239 us (46%)
  local copies, waits for them, and re-layouts  123 us (24%)
  matrix products  59.7 us (12%)
  Pallas kernels  34.9 us (7%)
  starting transfers between devices  20.1 us (4%)
  other arithmetic  18.1 us (4%)
  between operations  13.6 us (3%)
    all_gather x4, waiting for transfers between devices, split_gather(): got = lax.all_gather(mine, 'frames', axis=0, tiled=False)  168 us
    dot_general x12, matrix products, split_dot(): part = jnp.dot(a, b, preferred_element_type=jnp.float32)  59.7 us
    pallas_call x1, Pallas kernels, attend(): pl.pallas_call(attend_kernel, grid_spec=spec, out_shape=jax.ShapeDtypeStr...  34.9 us
    all_gather x1, waiting for transfers between devices, per_device(): whole = lax.all_gather(attended, 'wshard', axis=1, tiled=True)  31.8 us
    gather x6, local copies, waits for them, and re-layouts, split_gather(): sent = got[foreign]  29.6 us
    unnamed x35, local copies, waits for them, and re-layouts  26.9 us
    ppermute x4, waiting for transfers between devices, split_gather(): recv = lax.ppermute(sent, 'clips', [(0, 1), (1, 0)])  19.9 us
    ppermute x4, waiting for transfers between devices, shifted(): return lax.ppermute(value, axis, pairs)  19.4 us
  transfers between devices with their start and end apart: 13, of which 6 were waited for; matrix products, arithmetic and copies ran while one was open for 38% of the time, Pallas kernels for 7%

profile of v3, /device:TPU:0, one launch (start us, length us, event | category | flops | bytes accessed | tf_op | source)
XLA Modules:
  0.0 508.4 jit_solution(14746761714964594624)
XLA Ops:
  6.5 2.4 constant_dynamic-slice_fusion.5
  8.9 0.0 all-gather.6.cloned.1.call-start
  9.0 2.2 constant_dynamic-slice_fusion.6
  11.2 0.0 all-gather.10.cloned.1.call-start
  11.3 2.2 constant_dynamic-slice_fusion.4
  13.5 0.0 all-gather.14.cloned.1.call-start
  13.6 1.0 constant_dynamic-slice_fusion.2
  14.7 0.0 all-gather.12.cloned.1.call-start
  14.7 10.8 %copy.59 = bf16[768,5120]{0,1:T(8,128)(2,1)} copy(bf16[768,5120]{1,0:T(8,128)(2,1)} %param.9) | data formatting | bytes 15728640 | tf_op args[0]
  25.5 7.2 %dynamic-slice_bitcast_fusion = (bf16[768,4,640]{0,2,1:T(8,128)(2,1)}, bf16[768,4,1,640]{0,3,2,1:T(8,128)(2,1)}) fusion(bf16[768,4,2,640]{0,3,2,1:T(8,128)(2,1)} %bitcast.101, s32[]{:T(128)S(6)} %select_n.50, s32[]{:T(128)S(6)} %select_n.49), kind=kLoop, calls=%fused_computation.8 | loop fusion | bytes 15728648 | tf_op jit(solution)/shard_map/jit(dynamic_index_in_dim)/squeeze | solution.py:123
  32.8 3.8 fusion.23
  36.6 4.6 gather_fusion
  41.2 47.1 %all-gather.8.cloned.1.call-done = bf16[4,640,768]{2,1,0:T(8,128)(2,1)} async-done(((bf16[1,640,768]{2,1,0:T(8,128)(2,1)}), bf16[4,640,768]{2,1,0:T(8,128)(2,1)}) %all-gather.8.cloned.1.call-update) | async-done | bytes 3932176 | tf_op jit(solution)/shard_map/all_gather | solution.py:104
  88.2 4.5 gather_fusion.2
  92.7 5.6 %copy.70 = bf16[3,640,768]{1,2,0:T(8,128)(2,1)} copy(bf16[3,640,768]{2,1,0:T(8,128)(2,1)} %gather_fusion.2) | data formatting | bytes 5898240 | tf_op jit(solution)/shard_map/gather | solution.py:107
  98.3 1.5 collective-permute-start.1
  99.8 0.1 pad_add_fusion
  99.9 0.6 dynamic_slice.51.lim_ref
  100.5 4.0 fusion.21
  104.5 3.7 fusion.19
  108.3 56.5 %all-gather.6.cloned.1.call-done = bf16[4,640,768]{2,1,0:T(8,128)(2,1)} async-done(((bf16[1,640,768]{2,1,0:T(8,128)(2,1)}), bf16[4,640,768]{2,1,0:T(8,128)(2,1)}) %all-gather.6.cloned.1.call-update) | async-done | bytes 3932176 | tf_op jit(solution)/shard_map/all_gather | solution.py:104
  164.8 4.5 gather_fusion.1
  169.3 6.0 %copy.62 = bf16[3,640,768]{1,2,0:T(8,128)(2,1)} copy(bf16[3,640,768]{2,1,0:T(8,128)(2,1)} %gather_fusion.1) | data formatting | bytes 5898240 | tf_op jit(solution)/shard_map/gather | solution.py:107
  175.3 1.6 collective-permute-start
  176.8 64.5 %all-gather.10.cloned.1.call-done = bf16[4,640,768]{2,1,0:T(8,128)(2,1)} async-done(((bf16[1,640,768]{2,1,0:T(8,128)(2,1)}), bf16[4,640,768]{2,1,0:T(8,128)(2,1)}) %all-gather.10.cloned.1.call-update) | async-done | bytes 3932176 | tf_op jit(solution)/shard_map/all_gather | solution.py:104
  241.3 4.5 gather_fusion.3
  245.9 1.5 collective-permute-start.4
  247.3 8.8 %fusion.44 = f32[768,768]{1,0:T(8,128)} fusion(bf16[768,2560]{0,1:T(8,128)(2,1)} %bitcast.110, bf16[2560,768]{1,0:T(8,128)(2,1)} %bitcast.116), kind=kOutput, calls=%fused_computation.70 | convolution fusion | flops 3019898880 | bytes 10223616 | tf_op jit(solution)/shard_map/dot_general | solution.py:134
  256.1 3.5 fusion.45
  259.7 4.9 fusion.46
  264.6 6.3 %fusion.43 = (f32[768,768]{1,0:T(8,128)}, f32[768,768]{1,0:T(8,128)}) fusion(f32[768,768]{1,0:T(8,128)S(1)} %copy-done.14, f32[768,768]{1,0:T(8,128)S(1)} %fusion.45, bf16[3,640,768]{1,2,0:T(8,128)(2,1)} %collective-permute-done.1, bf16[3,768,640]{1,2,0:T(8,128)(2,1)S(1)} %copy-done.1), kind=kOutput, calls=%fused_computation.69 | convolution fusion | flops 2266693632 | bytes 15335424 | tf_op jit(solution)/shard_map/dot_general | solution.py:134
  270.8 3.1 copy.75
  273.9 1.8 reduce_sum.19
  275.8 1.6 mul.59
  277.4 3.3 copy.76
  280.7 4.0 multiply_convert_fusion
  284.6 1.5 collective-permute-start.3
  286.2 5.6 %collective-permute-start.2 = (bf16[768,768]{1,0:T(8,128)(2,1)}, bf16[768,768]{1,0:T(8,128)(2,1)}, u32[]{:S(2)}, u32[]{:S(2)}) collective-permute-start(bf16[768,768]{1,0:T(8,128)(2,1)} %multiply_convert_fusion), channel_id=1, source_target_pairs={{0,4},{4,8},{8,12},{1,5},{5,9},{9,13},{2,6},{6,10},{10,14},{3,7},{... | collective-permute-start | bytes 3538952 | tf_op jit(solution)/shard_map/ppermute | solution.py:17
  291.7 19.9 %collective-permute-done.4 = bf16[3,640,768]{2,1,0:T(8,128)(2,1)} collective-permute-done((bf16[3,640,768]{2,1,0:T(8,128)(2,1)}, bf16[3,640,768]{2,1,0:T(8,128)(2,1)}, u32[]{:S(2)}, u32[]{:S(2)}) %collective-permute-start.4) | collective-permute-done | bytes 2949152 | tf_op jit(solution)/shard_map/ppermute | solution.py:108
  311.6 5.2 %fusion.8 = bf16[768,768]{1,0:T(8,128)(2,1)S(1)} fusion(f32[768,768]{1,0:T(8,128)S(1)} %copy-done.5, f32[768,768]{1,0:T(8,128)} %fusion.46, bf16[3,640,768]{2,1,0:T(8,128)(2,1)} %collective-permute-done.4, bf16[3,768,640]{1,2,0:T(8,128)(2,1)S(1)} %copy-done.2), kind=kOutput, calls=%fused_computation.21 | convolution fusion | flops 2266693632 | bytes 11796480 | tf_op jit(solution)/shard_map/dot_general | solution.py:134
  316.9 1.3 collective-permute-start.6
  318.2 5.6 %collective-permute-start.5 = (bf16[768,768]{1,0:T(8,128)(2,1)S(1)}, bf16[768,768]{1,0:T(8,128)(2,1)}, u32[]{:S(2)}, u32[]{:S(2)}) collective-permute-start(bf16[768,768]{1,0:T(8,128)(2,1)S(1)} %fusion.8), channel_id=1, source_target_pairs={{0,4},{4,8},{8,12},{1,5},{5,9},{9,13},{2,6},{6,10},{10,14},{3,7},{... | collective-permute-start | bytes 3538952 | tf_op jit(solution)/shard_map/ppermute | solution.py:17
  323.8 6.3 %fusion.42 = (f32[768,768]{1,0:T(8,128)}, f32[768,768]{1,0:T(8,128)}) fusion(f32[768,768]{1,0:T(8,128)S(1)} %copy-done.13, f32[768,768]{1,0:T(8,128)S(1)} %copy-done.15, bf16[3,640,768]{1,2,0:T(8,128)(2,1)} %collective-permute-done, bf16[3,768,640]{1,2,0:T(8,128)(2,1)S(1)} %copy-done.2), kind=kOutput, calls=%fused_computation.68 | convolution fusion | flops 2266693632 | bytes 15335424 | tf_op jit(solution)/shard_map/dot_general | solution.py:134
  330.1 3.1 copy.68
  333.1 1.8 reduce_sum.18
  334.9 1.6 mul.52
  336.5 3.1 copy.69
  339.6 3.7 multiply_convert_fusion.1.q_ref
  343.3 3.4 pad_maximum_fusion.k_ref
  346.7 19.4 %collective-permute-done.6 = bf16[768,768]{1,0:T(8,128)(2,1)} collective-permute-done((bf16[768,768]{1,0:T(8,128)(2,1)S(1)}, bf16[768,768]{1,0:T(8,128)(2,1)}, u32[]{:S(2)}, u32[]{:S(2)}) %collective-permute-start.6) | collective-permute-done | bytes 1179680 | tf_op jit(solution)/shard_map/ppermute | solution.py:17
  366.1 3.3 pad_maximum_fusion.1.v_ref
  369.3 34.9 %shard_map.91 = bf16[768,768]{1,0:T(8,128)(2,1)} custom-call(s32[6,8]{1,0:T(8,128)} %kb_ref.1, s32[3]{0:T(128)} %dynamic_slice.51.lim_ref, bf16[768,768]{1,0:T(8,128)(2,1)} %multiply_convert_fusion.1.q_ref, bf16[2304,768]{1,0:T(8,128)(2,1)} %pad_maximum_fusion.k_ref, bf16[2304,768]{1,0:T(8,128)(2,1)} %pad_maximum_fusion.1.v_ref), custom_call_target="tpu_custom_call" | custom-call | tf_op jit(solution)/shard_map/pallas_call | solution.py:85
  404.3 4.5 gather_fusion.5
  408.8 1.5 collective-permute-start.7
  410.3 31.8 %all-gather.12.cloned.1.call-done = bf16[768,3072]{1,0:T(8,128)(2,1)} async-done(((bf16[768,768]{1,0:T(8,128)(2,1)}), bf16[768,3072]{1,0:T(8,128)(2,1)}) %all-gather.12.cloned.1.call-update) | async-done | bytes 4718608 | tf_op jit(solution)/shard_map/all_gather | solution.py:158
  442.1 11.6 %reshape.107 = bf16[768,4,2,384]{3,2,1,0:T(2,128)(2,1)} reshape(bf16[768,3072]{1,0:T(8,128)(2,1)} %all-gather.12.cloned.1.call-done) | data formatting | bytes 9437184 | tf_op jit(solution)/shard_map/reshape | solution.py:121
  453.8 12.3 %constant_dynamic-slice_fusion.1 = (bf16[768,4,1,384]{3,2,1,0:T(2,128)(2,1)}, bf16[768,4,1,384]{3,2,1,0:T(2,128)(2,1)}) fusion(bf16[768,4,2,384]{3,2,1,0:T(2,128)(2,1)} %reshape.107, s32[]{:T(128)S(6)} %select_n.50, s32[]{:T(128)S(6)} %select_n.49), kind=kLoop, calls=%fused_computation.53 | loop fusion | bytes 9437192 | tf_op jit(solution)/shard_map/jit(dynamic_index_in_dim)/dynamic_slice | solution.py:123
  466.1 11.9 %copy.93 = bf16[768,4,1,384]{0,3,1,2:T(8,128)(2,1)} copy(bf16[768,4,1,384]{3,2,1,0:T(2,128)(2,1)} %get-tuple-element.8) | data formatting | bytes 4718592
  478.0 4.1 copy.99
  482.1 3.7 gather_fusion.4
  485.9 2.5 constant_dynamic-slice_fusion
  488.4 6.2 %fusion.47 = f32[768,1280]{1,0:T(8,128)S(1)} fusion(bf16[768,1536]{0,1:T(8,128)(2,1)} %bitcast.113, bf16[1536,1280]{1,0:T(8,128)(2,1)} %bitcast.114), kind=kOutput, calls=%fused_computation.73 | convolution fusion | flops 3019898880 | bytes 10223616 | tf_op jit(solution)/shard_map/dot_general | solution.py:134
  494.6 4.6 fusion.11
  499.2 2.5 fusion
  (49 shorter events, 0.2 us)
Async XLA Ops:
  6.5 7.0 %copy-start = (bf16[768,1280]{1,0:T(8,128)(2,1)S(1)}, bf16[768,1280]{1,0:T(8,128)(2,1)}, u32[]{:S(2)}) copy-start(bf16[768,1280]{1,0:T(8,128)(2,1)} %param.15) | copy-start | bytes 5898244
  6.5 81.7 %all-gather.8.cloned.1.call-start = ((), (), s32[]{:S(2)}) async-start(), calls=%async_computation.1 | async-start | bytes 4915200 | tf_op jit(solution)/shard_map/all_gather | solution.py:104
  8.9 155.8 %all-gather.6.cloned.1.call-start = ((), (), s32[]{:S(2)}) async-start(), calls=%async_computation | async-start | bytes 4915200 | tf_op jit(solution)/shard_map/all_gather | solution.py:104
  11.2 230.1 %all-gather.10.cloned.1.call-start = ((), (), s32[]{:S(2)}) async-start(), calls=%async_computation.2 | async-start | bytes 4915200 | tf_op jit(solution)/shard_map/all_gather | solution.py:104
  13.5 390.8 %all-gather.14.cloned.1.call-start = ((), (), s32[]{:S(2)}) async-start(), calls=%async_computation.4 | async-start | bytes 4915200 | tf_op jit(solution)/shard_map/all_gather | solution.py:104
  14.7 427.5 %all-gather.12.cloned.1.call-start = ((), (), s32[]{:S(2)}) async-start(), calls=%async_computation.3 | async-start | bytes 5898240 | tf_op jit(solution)/shard_map/all_gather | solution.py:158
  25.5 7.2 %copy-start.8 = (bf16[1280,768]{1,0:T(8,128)(2,1)S(1)}, bf16[1280,768]{1,0:T(8,128)(2,1)}, u32[]{:S(2)}) copy-start(bf16[1280,768]{1,0:T(8,128)(2,1)} %param.10) | copy-start | bytes 5898244
  92.7 7.1 %copy-start.12 = (s32[4]{0:T(128)S(1)}, s32[4]{0:T(128)}, u32[]{:S(2)}) copy-start(s32[4]{0:T(128)} %param.17) | copy-start | bytes 52
  98.3 6.2 %copy-start.9 = (bf16[1280,768]{1,0:T(8,128)(2,1)S(1)}, bf16[1280,768]{1,0:T(8,128)(2,1)}, u32[]{:S(2)}) copy-start(bf16[1280,768]{1,0:T(8,128)(2,1)} %param.12) | copy-start | bytes 5898244
  98.3 166.2 %collective-permute-start.1 = (bf16[3,640,768]{1,2,0:T(8,128)(2,1)}, bf16[3,640,768]{1,2,0:T(8,128)(2,1)}, u32[]{:S(2)}, u32[]{:S(2)}) collective-permute-start(bf16[3,640,768]{1,2,0:T(8,128)(2,1)} %copy.70), channel_id=1, source_target_pairs={{0,16},{16,0},{1,17},{17,1},{2,18},{18,2},{3,19},{19,3},{4,20},{20... | collective-permute-start | bytes 8847368 | tf_op jit(solution)/shard_map/ppermute | solution.py:108
  175.3 148.5 %collective-permute-start = (bf16[3,640,768]{1,2,0:T(8,128)(2,1)}, bf16[3,640,768]{1,2,0:T(8,128)(2,1)}, u32[]{:S(2)}, u32[]{:S(2)}) collective-permute-start(bf16[3,640,768]{1,2,0:T(8,128)(2,1)} %copy.62), channel_id=1, source_target_pairs={{0,16},{16,0},{1,17},{17,1},{2,18},{18,2},{3,19},{19,3},{4,20},{20... | collective-permute-start | bytes 8847368 | tf_op jit(solution)/shard_map/ppermute | solution.py:108
  245.9 65.8 %collective-permute-start.4 = (bf16[3,640,768]{2,1,0:T(8,128)(2,1)}, bf16[3,640,768]{2,1,0:T(8,128)(2,1)}, u32[]{:S(2)}, u32[]{:S(2)}) collective-permute-start(bf16[3,640,768]{2,1,0:T(8,128)(2,1)} %gather_fusion.3), channel_id=1, source_target_pairs={{0,16},{16,0},{1,17},{17,1},{2,18},{18,2},{3,19},{19,3},{4,20},{20... | collective-permute-start | bytes 8847368 | tf_op jit(solution)/shard_map/ppermute | solution.py:108
  247.3 8.8 %copy-start.3 = (bf16[768,4,1,640]{0,3,2,1:T(8,128)(2,1)S(1)}, bf16[768,4,1,640]{0,3,2,1:T(8,128)(2,1)}, u32[]{:S(2)}) copy-start(bf16[768,4,1,640]{0,3,2,1:T(8,128)(2,1)} %get-tuple-element.6) | copy-start | bytes 11796484
  247.3 8.8 %copy-start.6 = (bf16[4,640,768]{2,1,0:T(8,128)(2,1)S(1)}, bf16[4,640,768]{2,1,0:T(8,128)(2,1)}, u32[]{:S(2)}) copy-start(bf16[4,640,768]{2,1,0:T(8,128)(2,1)} %all-gather.8.cloned.1.call-done) | copy-start | bytes 11796484
  256.1 3.5 copy-start.7
  259.6 4.9 copy-start.1
  259.6 4.9 copy-start.14
  277.4 3.3 copy-start.10
  280.7 31.0 %copy-start.2 = (bf16[3,768,640]{1,2,0:T(8,128)(2,1)S(1)}, bf16[3,768,640]{1,2,0:T(8,128)(2,1)}, u32[]{:S(2)}) copy-start(bf16[3,768,640]{1,2,0:T(8,128)(2,1)} %gather_fusion) | copy-start | bytes 8847364
  280.7 31.0 %copy-start.5 = (f32[768,768]{1,0:T(8,128)S(1)}, f32[768,768]{1,0:T(8,128)}, u32[]{:S(2)}) copy-start(f32[768,768]{1,0:T(8,128)} %fusion.19) | copy-start | bytes 7077892
  284.6 39.2 %copy-start.13 = (f32[768,768]{1,0:T(8,128)S(1)}, f32[768,768]{1,0:T(8,128)}, u32[]{:S(2)}) copy-start(f32[768,768]{1,0:T(8,128)} %fusion.23) | copy-start | bytes 7077892
  284.6 39.2 %copy-start.15 = (f32[768,768]{1,0:T(8,128)S(1)}, f32[768,768]{1,0:T(8,128)}, u32[]{:S(2)}) copy-start(f32[768,768]{1,0:T(8,128)} %fusion.44) | copy-start | bytes 7077892
  284.6 58.7 %collective-permute-start.3 = (bf16[768,768]{1,0:T(8,128)(2,1)}, bf16[768,768]{1,0:T(8,128)(2,1)}, u32[]{:S(2)}, u32[]{:S(2)}) collective-permute-start(bf16[768,768]{1,0:T(8,128)(2,1)} %multiply_convert_fusion), channel_id=1, source_target_pairs={{4,0},{8,4},{12,8},{5,1},{9,5},{13,9},{6,2},{10,6},{14,10},{7,3},{... | collective-permute-start | bytes 3538952 | tf_op jit(solution)/shard_map/ppermute | solution.py:17
  286.2 57.1 %collective-permute-start.2 = (bf16[768,768]{1,0:T(8,128)(2,1)}, bf16[768,768]{1,0:T(8,128)(2,1)}, u32[]{:S(2)}, u32[]{:S(2)}) collective-permute-start(bf16[768,768]{1,0:T(8,128)(2,1)} %multiply_convert_fusion), channel_id=1, source_target_pairs={{0,4},{4,8},{8,12},{1,5},{5,9},{9,13},{2,6},{6,10},{10,14},{3,7},{... | collective-permute-start | bytes 3538952 | tf_op jit(solution)/shard_map/ppermute | solution.py:17
  316.9 49.2 %collective-permute-start.6 = (bf16[768,768]{1,0:T(8,128)(2,1)S(1)}, bf16[768,768]{1,0:T(8,128)(2,1)}, u32[]{:S(2)}, u32[]{:S(2)}) collective-permute-start(bf16[768,768]{1,0:T(8,128)(2,1)S(1)} %fusion.8), channel_id=1, source_target_pairs={{4,0},{8,4},{12,8},{5,1},{9,5},{13,9},{6,2},{10,6},{14,10},{7,3},{... | collective-permute-start | bytes 3538952 | tf_op jit(solution)/shard_map/ppermute | solution.py:17
  318.2 47.9 %collective-permute-start.5 = (bf16[768,768]{1,0:T(8,128)(2,1)S(1)}, bf16[768,768]{1,0:T(8,128)(2,1)}, u32[]{:S(2)}, u32[]{:S(2)}) collective-permute-start(bf16[768,768]{1,0:T(8,128)(2,1)S(1)} %fusion.8), channel_id=1, source_target_pairs={{0,4},{4,8},{8,12},{1,5},{5,9},{9,13},{2,6},{6,10},{10,14},{3,7},{... | collective-permute-start | bytes 3538952 | tf_op jit(solution)/shard_map/ppermute | solution.py:17
  336.5 3.1 copy-start.11
  408.8 85.8 %collective-permute-start.7 = (bf16[3,384,1280]{2,1,0:T(8,128)(2,1)}, bf16[3,384,1280]{2,1,0:T(8,128)(2,1)}, u32[]{:S(2)}, u32[]{:S(2)}) collective-permute-start(bf16[3,384,1280]{2,1,0:T(8,128)(2,1)} %gather_fusion.5), channel_id=1, source_target_pairs={{0,16},{16,0},{1,17},{17,1},{2,18},{18,2},{3,19},{19,3},{4,20},{20... | collective-permute-start | bytes 8847368 | tf_op jit(solution)/shard_map/ppermute | solution.py:108
  488.3 6.3 %copy-start.4 = (bf16[3,768,384]{2,1,0:T(8,128)(2,1)S(1)}, bf16[3,768,384]{2,1,0:T(8,128)(2,1)}, u32[]{:S(2)}) copy-start(bf16[3,768,384]{2,1,0:T(8,128)(2,1)} %gather_fusion.4) | copy-start | bytes 5308420
Sparse Core Ops, SparseCore 0:
  9.1 79.1 all-gather.7
  89.8 74.9 all-gather.5
  166.3 74.9 all-gather.9
  242.8 93.7 all-gather.13
  404.4 37.7 all-gather.11

commit v4 on v3

--- a/solution.py
+++ b/solution.py
@@ -97,55 +97,34 @@
     ci = lax.axis_index("clips")
     fi = lax.axis_index("frames")
     rows, cols = piece.shape
-    share = rows // parts
-    halves = piece.reshape(parts, share, cols)
-    mine = lax.dynamic_index_in_dim(halves, ci, 0, keepdims=False)
-    other = lax.dynamic_index_in_dim(halves, 1 - ci, 0, keepdims=False)
+    share = cols // parts
+    halves = piece.reshape(rows, parts, share)
+    mine = lax.dynamic_index_in_dim(halves, ci, 1, keepdims=False)
+    other = lax.dynamic_index_in_dim(halves, 1 - ci, 1, keepdims=False)
     got = lax.all_gather(mine, "frames", axis=0, tiled=False)
-    foreign = jnp.arange(chunks - 1, dtype=jnp.int32)
-    foreign = foreign + (foreign >= fi).astype(jnp.int32)
-    sent = got[foreign]
-    recv = lax.ppermute(sent, "clips", [(0, 1), (1, 0)])
-    return (
-        got.reshape(chunks * share, cols),
-        recv.reshape((chunks - 1) * share, cols),
-        other,
-    ), (ci, fi, foreign)
+    order = jnp.arange(chunks, dtype=jnp.int32)
+    foreign = order[: chunks - 1] + (order[: chunks - 1] >= fi).astype(jnp.int32)
+    recv = lax.ppermute(got[foreign], "clips", [(0, 1), (1, 0)])
+    slot = jnp.clip(order - (order > fi).astype(jnp.int32), 0, chunks - 2)
+    whole_other = jnp.where((order == fi)[:, None, None], other[None], recv[slot])
+    return got.reshape(chunks * rows, share), whole_other.reshape(chunks * rows, share)
 
 
-def split_cols(x, share, where):
-    ci, fi, foreign = where
-    n, width = x.shape
-    parts = 2
-    chunks = width // (parts * share)
-    blocks = x.reshape(n, chunks, parts, share)
-    mine = lax.dynamic_index_in_dim(blocks, ci, 2, keepdims=False)
-    other = lax.dynamic_index_in_dim(blocks, 1 - ci, 2, keepdims=False)
-    return (
-        mine.reshape(n, chunks * share),
-        other[:, foreign].reshape(n, (chunks - 1) * share),
-        lax.dynamic_index_in_dim(other, fi, 1, keepdims=False),
-    )
-
-
-def split_dot(cols, rows):
-    total = None
-    for a, b in zip(cols, rows):
-        part = jnp.dot(a, b, preferred_element_type=jnp.float32)
-        total = part if total is None else total + part
-    return total
+def split_dot(x, pair):
+    own = jnp.dot(x, pair[0], preferred_element_type=jnp.float32)
+    rest = jnp.dot(x, pair[1], preferred_element_type=jnp.float32)
+    first = lax.axis_index("clips") == 0
+    return jnp.where(first, jnp.concatenate([own, rest], 1), jnp.concatenate([rest, own], 1))
 
 
 def per_device(tokens, w_query, w_key, w_value, q_gain, k_gain, w_out, key_blocks, slab_counts):
-    share = w_query.shape[0] // lax.axis_size("clips")
-    k_rows, where = split_gather(w_key)
-    v_rows, _ = split_gather(w_value)
-    q_rows, _ = split_gather(w_query)
-    o_rows, _ = split_gather(w_out)
-    token_cols = split_cols(tokens, share, where)
-    query = head_norm(split_dot(token_cols, q_rows), q_gain)
-    keys = head_norm(split_dot(token_cols, k_rows), k_gain)
-    values = split_dot(token_cols, v_rows).astype(jnp.bfloat16)
+    k_rows = split_gather(w_key)
+    v_rows = split_gather(w_value)
+    q_rows = split_gather(w_query)
+    o_rows = split_gather(w_out)
+    query = head_norm(split_dot(tokens, q_rows), q_gain)
+    keys = head_norm(split_dot(tokens, k_rows), k_gain)
+    values = split_dot(tokens, v_rows).astype(jnp.bfloat16)
     before = shifted((keys, values), "frames", 1)
     after = shifted((keys, values), "frames", -1)
     key_window = jnp.concatenate([before[0], keys, after[0]], axis=0)
@@ -154,10 +133,10 @@
     zero = jnp.zeros((1,), jnp.int32)
     count_pad = jnp.concatenate([zero, slab_counts, zero], axis=0)
     limits = lax.dynamic_slice_in_dim(count_pad, position, 3, 0)
+    query, o_rows = lax.optimization_barrier((query, o_rows))
     attended = attend(query, key_window, value_window, key_blocks, limits)
     whole = lax.all_gather(attended, "wshard", axis=1, tiled=True)
-    out_share = w_out.shape[0] // lax.axis_size("clips")
-    mixed = split_dot(split_cols(whole, out_share, where), o_rows)
+    mixed = split_dot(whole, o_rows)
     return mixed.astype(jnp.bfloat16)
 
 

time: 515 us -> 545 us (1.058); the launches traced: 508 us -> 544 us
  waiting for transfers between devices: 239 us -> 305 us
  local copies, waits for them, and re-layouts: 123 us -> 92 us
  other arithmetic: 18.1 us -> 28.1 us
  matrix products: 59.7 us -> 51.2 us
    all_gather x4, waiting for transfers between devices: 168 us -> 251 us  [split_gather(): got = lax.all_gather(mine, 'frames', axis=0, tiled=False)]
    all_gather x0 -> x4, local copies, waits for them, and re-layouts: none -> 25.1 us  [split_gather(): got = lax.all_gather(mine, 'frames', axis=0, tiled=False)]
    ppermute x4, waiting for transfers between devices: 19.9 us -> 0.01 us  [split_gather(): recv = lax.ppermute(got[foreign], 'clips', [(0, 1), (1, 0)])]
    unnamed x35 -> x50, local copies, waits for them, and re-layouts: 26.9 us -> 10.9 us
    select_n x1 -> x4, other arithmetic: 0.01 us -> 13.2 us  [the longest x2 13.2 us: split_gather(): jnp.where((order == fi)[:, None, None], other[None], recv[slot])]
    dynamic_slice x6 -> x8, local copies, waits for them, and re-layouts: 22.6 us -> 10.7 us  [split_gather(): other = lax.dynamic_index_in_dim(halves, 1 - ci, 1, keepdims=False)]
    reshape x1 -> x0, local copies, waits for them, and re-layouts: 11.6 us -> none  [split_cols(): blocks = x.reshape(n, chunks, parts, share)]
    dot_general x12 -> x8, matrix products: 59.7 us -> 51.2 us  [the longest x4 27.3 us: split_dot(): rest = jnp.dot(x, pair[1], preferred_element_type=jnp.float32)]
  transfers between devices with their start and end apart: 13 -> 13, of which waited for: 6 -> 7; matrix products, arithmetic and copies ran while one was open for 38% -> 28% of each run, Pallas kernels for 7% -> 0%
where the time goes in v4:
time: 545 us; the launch traced here: 544 us
  waiting for transfers between devices  305 us (56%)
  local copies, waits for them, and re-layouts  92 us (17%)
  matrix products  51.2 us (9%)
  Pallas kernels  35 us (6%)
  other arithmetic  28.1 us (5%)
  starting transfers between devices  19.7 us (4%)
  between operations  13.4 us (2%)
    all_gather x4, waiting for transfers between devices, split_gather(): got = lax.all_gather(mine, 'frames', axis=0, tiled=False)  251 us
    all_gather x1, waiting for transfers between devices, per_device(): whole = lax.all_gather(attended, 'wshard', axis=1, tiled=True)  38.2 us
    pallas_call x1, Pallas kernels, attend(): pl.pallas_call(attend_kernel, grid_spec=spec, out_shape=jax.ShapeDtypeStr...  35 us
    dot_general x4, matrix products, split_dot(): rest = jnp.dot(x, pair[1], preferred_element_type=jnp.float32)  27.3 us
    all_gather x4, local copies, waits for them, and re-layouts, split_gather(): got = lax.all_gather(mine, 'frames', axis=0, tiled=False)  25.1 us
    dot_general x4, matrix products, split_dot(): own = jnp.dot(x, pair[0], preferred_element_type=jnp.float32)  23.9 us
    gather x4, local copies, waits for them, and re-layouts, split_gather(): recv = lax.ppermute(got[foreign], 'clips', [(0, 1), (1, 0)])  20.5 us
    gather x4, local copies, waits for them, and re-layouts, split_gather(): recv[slot]  17.8 us
  transfers between devices with their start and end apart: 13, of which 7 were waited for; matrix products, arithmetic and copies ran while one was open for 28% of the time, Pallas kernels for 0%

profile of v4, /device:TPU:0, one launch (start us, length us, event | category | flops | bytes accessed | tf_op | source)
XLA Modules:
  0.0 544.2 jit_solution(12164750669319493132)
XLA Ops:
  6.5 2.7 copy.40
  9.2 1.1 constant_dynamic-slice_fusion
  10.4 2.7 copy.35
  13.1 1.4 constant_dynamic-slice_fusion.2
  14.6 2.7 copy.26
  17.3 1.4 constant_dynamic-slice_fusion.6
  18.8 2.8 copy.31
  21.6 1.4 constant_dynamic-slice_fusion.4
  23.1 0.1 broadcast_in_dim.94
  23.2 1.3 copy.43
  24.5 1.3 copy.37
  25.8 1.3 copy.28
  27.2 1.3 copy.33
  28.7 0.6 dynamic_slice.29.lim_ref
  29.3 60.4 %all-gather.18.cloned.1.call-done = bf16[5120,1,384]{0,2,1:T(8,128)(2,1)} async-done(((bf16[1280,1,384]{0,2,1:T(8,128)(2,1)}), bf16[5120,1,384]{0,2,1:T(8,128)(2,1)}) %all-gather.18.cloned.1.call-update) | async-done | bytes 3932176 | tf_op jit(solution)/shard_map/all_gather | solution.py:104
  89.6 6.3 %copy.41 = bf16[5120,1,384]{2,0,1:T(8,128)(2,1)} copy(bf16[5120,1,384]{0,2,1:T(8,128)(2,1)} %all-gather.18.cloned.1.call-done) | data formatting | bytes 7864320 | tf_op jit(solution)/shard_map/all_gather | solution.py:104
  95.9 5.2 gather_fusion.6
  101.2 1.4 collective-permute-start.5
  102.6 63.6 %all-gather.16.cloned.1.call-done = bf16[5120,1,384]{0,2,1:T(8,128)(2,1)} async-done(((bf16[1280,1,384]{0,2,1:T(8,128)(2,1)}), bf16[5120,1,384]{0,2,1:T(8,128)(2,1)}) %all-gather.16.cloned.1.call-update) | async-done | bytes 3932176 | tf_op jit(solution)/shard_map/all_gather | solution.py:104
  166.2 6.3 %copy.36 = bf16[5120,1,384]{2,0,1:T(8,128)(2,1)} copy(bf16[5120,1,384]{0,2,1:T(8,128)(2,1)} %all-gather.16.cloned.1.call-done) | data formatting | bytes 7864320 | tf_op jit(solution)/shard_map/all_gather | solution.py:104
  172.4 5.2 gather_fusion.4
  177.7 1.4 collective-permute-start.2
  179.1 63.6 %all-gather.12.cloned.1.call-done = bf16[5120,1,384]{0,2,1:T(8,128)(2,1)} async-done(((bf16[1280,1,384]{0,2,1:T(8,128)(2,1)}), bf16[5120,1,384]{0,2,1:T(8,128)(2,1)}) %all-gather.12.cloned.1.call-update) | async-done | bytes 3932176 | tf_op jit(solution)/shard_map/all_gather | solution.py:104
  242.7 6.3 %copy.27 = bf16[5120,1,384]{2,0,1:T(8,128)(2,1)} copy(bf16[5120,1,384]{0,2,1:T(8,128)(2,1)} %all-gather.12.cloned.1.call-done) | data formatting | bytes 7864320 | tf_op jit(solution)/shard_map/all_gather | solution.py:104
  249.0 5.3 gather_fusion
  254.3 1.5 collective-permute-start
  255.7 63.4 %all-gather.14.cloned.1.call-done = bf16[3072,1,640]{0,2,1:T(8,128)(2,1)} async-done(((bf16[768,1,640]{0,2,1:T(8,128)(2,1)}), bf16[3072,1,640]{0,2,1:T(8,128)(2,1)}) %all-gather.14.cloned.1.call-update) | async-done | bytes 3932176 | tf_op jit(solution)/shard_map/all_gather | solution.py:104
  319.1 6.3 %copy.32 = bf16[3072,1,640]{2,0,1:T(8,128)(2,1)} copy(bf16[3072,1,640]{0,2,1:T(8,128)(2,1)} %all-gather.14.cloned.1.call-done) | data formatting | bytes 7864320 | tf_op jit(solution)/shard_map/all_gather | solution.py:104
  325.4 4.8 gather_fusion.2
  330.2 1.5 collective-permute-start.1
  331.7 8.8 %fusion.5 = f32[384,768]{1,0:T(8,128)} fusion(bf16[768,5120]{1,0:T(8,128)(2,1)} %param.9, bf16[5120,1,384]{0,2,1:T(8,128)(2,1)} %all-gather.12.cloned.1.call-done), kind=kOutput, calls=%fused_computation.14 | convolution fusion | flops 3019898880 | bytes 12976128 | tf_op jit(solution)/shard_map/dot_general | solution.py:114
  340.5 6.8 %fusion.3 = f32[384,768]{1,0:T(8,128)} fusion(bf16[768,5120]{1,0:T(8,128)(2,1)} %param.9, bf16[5120,1,384]{0,2,1:T(8,128)(2,1)S(1)} %copy-done.7), kind=kOutput, calls=%fused_computation.12 | convolution fusion | flops 3019898880 | bytes 12976128 | tf_op jit(solution)/shard_map/dot_general | solution.py:114
  347.3 5.1 fusion.8
  352.4 3.0 gather_fusion.7
  355.4 4.9 gather_fusion.5
  360.3 5.0 gather_fusion.1
  365.3 8.2 %bitcast_select_fusion = (bf16[5120,384]{1,0:T(8,128)(2,1)}, bf16[5120,384]{1,0:T(8,128)(2,1)S(1)}, bf16[5120,384]{1,0:T(8,128)(2,1)S(1)}) fusion(bf16[4,1280,384]{2,1,0:T(8,128)(2,1)} %gather_fusion.7, pred[5120]{0:T(1024)(128)(4,1)S(1)} %broadcast_in_dim.95, bf16[1280,384]{1,0:T(8,128)(2,1)S(1)} %bitcast.96, bf16[4,1280,384]{2,1,0:T(8,128)(2,1)} %gather_fusion.5, ...), kind=kLoop, calls=%fused_computation.16 | loop fusion | flops 5898240 | bytes 26547200 | tf_op jit(solution)/shard_map/jit(_where)/select_n | solution.py:109
  373.5 5.6 %fusion.17 = f32[384,768]{1,0:T(8,128)S(1)} fusion(bf16[5120,384]{1,0:T(8,128)(2,1)S(1)} %get-tuple-element.21, bf16[768,5120]{1,0:T(8,128)(2,1)} %param.9), kind=kOutput, calls=%fused_computation.56 | convolution fusion | flops 3019898880 | bytes 12976128 | tf_op jit(solution)/shard_map/dot_general | solution.py:115
  379.2 6.1 %fusion.18 = f32[384,768]{1,0:T(8,128)S(1)} fusion(bf16[5120,384]{1,0:T(8,128)(2,1)S(1)} %get-tuple-element.20, bf16[768,5120]{1,0:T(8,128)(2,1)} %param.9), kind=kOutput, calls=%fused_computation.57 | convolution fusion | flops 3019898880 | bytes 12976128 | tf_op jit(solution)/shard_map/dot_general | solution.py:115
  385.3 1.3 multiply_reduce_fusion
  386.7 0.2 fusion.11
  386.9 2.0 copy.39
  388.9 2.9 multiply_convert_fusion
  391.8 1.3 collective-permute-start.4
  393.1 5.6 %collective-permute-start.3 = (bf16[768,768]{1,0:T(8,128)(2,1)}, bf16[768,768]{1,0:T(8,128)(2,1)}, u32[]{:S(2)}, u32[]{:S(2)}) collective-permute-start(bf16[768,768]{1,0:T(8,128)(2,1)} %multiply_convert_fusion), channel_id=1, source_target_pairs={{0,4},{4,8},{8,12},{1,5},{5,9},{9,13},{2,6},{6,10},{10,14},{3,7},{... | collective-permute-start | bytes 3538952 | tf_op jit(solution)/shard_map/ppermute | solution.py:17
  398.7 8.6 %convolution_bitcast_fusion = bf16[768,384]{1,0:T(8,128)(2,1)S(1)} fusion(bf16[768,5120]{1,0:T(8,128)(2,1)} %param.9, bf16[5120,384]{1,0:T(8,128)(2,1)} %get-tuple-element.19), kind=kOutput, calls=%fused_computation.31 | convolution fusion | flops 3019898880 | bytes 12386304 | tf_op jit(solution)/shard_map/dot_general | solution.py:115
  407.4 1.3 fusion.7
  408.7 1.3 collective-permute-start.7
  410.0 5.6 %collective-permute-start.6 = (bf16[768,768]{1,0:T(8,128)(2,1)}, bf16[768,768]{1,0:T(8,128)(2,1)}, u32[]{:S(2)}, u32[]{:S(2)}) collective-permute-start(bf16[768,768]{1,0:T(8,128)(2,1)} %fusion.7), channel_id=1, source_target_pairs={{0,4},{4,8},{8,12},{1,5},{5,9},{9,13},{2,6},{6,10},{10,14},{3,7},{... | collective-permute-start | bytes 3538952 | tf_op jit(solution)/shard_map/ppermute | solution.py:17
  415.6 0.2 fusion.12
  415.8 2.0 copy.30
  417.8 4.9 gather_fusion.3
  422.6 5.0 bitcast_select_fusion.2
  427.6 1.2 multiply_convert_fusion.1.q_ref
  428.8 3.4 pad_maximum_fusion.k_ref
  432.2 14.4 %collective-permute-done.7 = bf16[768,768]{1,0:T(8,128)(2,1)} collective-permute-done((bf16[768,768]{1,0:T(8,128)(2,1)}, bf16[768,768]{1,0:T(8,128)(2,1)}, u32[]{:S(2)}, u32[]{:S(2)}) %collective-permute-start.7) | collective-permute-done | bytes 1179680 | tf_op jit(solution)/shard_map/ppermute | solution.py:17
  446.6 1.2 collective-permute-done.6
  447.8 3.4 pad_maximum_fusion.1.v_ref
  451.2 35.0 %shard_map.91 = bf16[768,768]{1,0:T(8,128)(2,1)} custom-call(s32[6,8]{1,0:T(8,128)} %kb_ref.1, s32[3]{0:T(128)} %dynamic_slice.29.lim_ref, bf16[768,768]{1,0:T(8,128)(2,1)} %multiply_convert_fusion.1.q_ref, bf16[2304,768]{1,0:T(8,128)(2,1)} %pad_maximum_fusion.k_ref, bf16[2304,768]{1,0:T(8,128)(2,1)} %pad_maximum_fusion.1.v_ref), custom_call_target="tpu_custom_call" | custom-call | tf_op jit(solution)/shard_map/pallas_call | solution.py:85
  486.2 38.2 %all-gather.10.cloned.1.call-done = bf16[768,3072]{1,0:T(8,128)(2,1)} async-done(((bf16[768,768]{1,0:T(8,128)(2,1)}), bf16[768,3072]{1,0:T(8,128)(2,1)}) %all-gather.10.cloned.1.call-update) | async-done | bytes 4718608 | tf_op jit(solution)/shard_map/all_gather | solution.py:138
  524.4 7.0 %fusion.20 = bf16[768,640]{0,1:T(8,128)(2,1)S(1)} fusion(bf16[768,3072]{1,0:T(8,128)(2,1)} %all-gather.10.cloned.1.call-done, bf16[3072,640]{1,0:T(8,128)(2,1)} %bitcast_select_fusion.2), kind=kOutput, calls=%fused_computation.59 | convolution fusion | flops 3019898880 | bytes 9633792 | tf_op jit(solution)/shard_map/dot_general | solution.py:115
  531.4 3.3 fusion.19
  534.7 0.7 fusion
  535.4 2.3 copy.46
  (75 shorter events, 0.6 us)
Async XLA Ops:
  6.5 83.1 %all-gather.18.cloned.1.call-start = ((), (), s32[]{:S(2)}) async-start(), calls=%async_computation.4 | async-start | bytes 4915200 | tf_op jit(solution)/shard_map/all_gather | solution.py:104
  10.3 155.8 %all-gather.16.cloned.1.call-start = ((), (), s32[]{:S(2)}) async-start(), calls=%async_computation.3 | async-start | bytes 4915200 | tf_op jit(solution)/shard_map/all_gather | solution.py:104
  14.5 228.2 %all-gather.12.cloned.1.call-start = ((), (), s32[]{:S(2)}) async-start(), calls=%async_computation.1 | async-start | bytes 4915200 | tf_op jit(solution)/shard_map/all_gather | solution.py:104
  18.7 300.4 %all-gather.14.cloned.1.call-start = ((), (), s32[]{:S(2)}) async-start(), calls=%async_computation.2 | async-start | bytes 4915200 | tf_op jit(solution)/shard_map/all_gather | solution.py:104
  23.0 1.5 copy-start.12
  23.0 2.8 copy-start.13
  23.0 501.4 %all-gather.10.cloned.1.call-start = ((), (), s32[]{:S(2)}) async-start(), calls=%async_computation | async-start | bytes 5898240 | tf_op jit(solution)/shard_map/all_gather | solution.py:138
  24.5 2.7 copy-start.14
  24.5 4.1 copy-start.20
  101.2 251.2 %collective-permute-start.5 = (bf16[3,1280,384]{2,1,0:T(8,128)(2,1)}, bf16[3,1280,384]{2,1,0:T(8,128)(2,1)S(1)}, u32[]{:S(2)}, u32[]{:S(2)}) collective-permute-start(bf16[3,1280,384]{2,1,0:T(8,128)(2,1)} %gather_fusion.6), channel_id=1, source_target_pairs={{0,16},{16,0},{1,17},{17,1},{2,18},{18,2},{3,19},{19,3},{4,20},{20... | collective-permute-start | bytes 8847368 | tf_op jit(solution)/shard_map/ppermute | solution.py:107
  177.7 177.7 %collective-permute-start.2 = (bf16[3,1280,384]{2,1,0:T(8,128)(2,1)}, bf16[3,1280,384]{2,1,0:T(8,128)(2,1)}, u32[]{:S(2)}, u32[]{:S(2)}) collective-permute-start(bf16[3,1280,384]{2,1,0:T(8,128)(2,1)} %gather_fusion.4), channel_id=1, source_target_pairs={{0,16},{16,0},{1,17},{17,1},{2,18},{18,2},{3,19},{19,3},{4,20},{20... | collective-permute-start | bytes 8847368 | tf_op jit(solution)/shard_map/ppermute | solution.py:107
  254.3 106.0 %collective-permute-start = (bf16[3,1280,384]{2,1,0:T(8,128)(2,1)}, bf16[3,1280,384]{2,1,0:T(8,128)(2,1)}, u32[]{:S(2)}, u32[]{:S(2)}) collective-permute-start(bf16[3,1280,384]{2,1,0:T(8,128)(2,1)} %gather_fusion), channel_id=1, source_target_pairs={{0,16},{16,0},{1,17},{17,1},{2,18},{18,2},{3,19},{19,3},{4,20},{20... | collective-permute-start | bytes 8847368 | tf_op jit(solution)/shard_map/ppermute | solution.py:107
  330.2 10.3 %copy-start.7 = (bf16[5120,1,384]{0,2,1:T(8,128)(2,1)S(1)}, bf16[5120,1,384]{0,2,1:T(8,128)(2,1)}, u32[]{:S(2)}) copy-start(bf16[5120,1,384]{0,2,1:T(8,128)(2,1)} %all-gather.16.cloned.1.call-done) | copy-start | bytes 11796484
  330.2 87.6 %collective-permute-start.1 = (bf16[3,768,640]{2,1,0:T(8,128)(2,1)}, bf16[3,768,640]{2,1,0:T(8,128)(2,1)}, u32[]{:S(2)}, u32[]{:S(2)}) collective-permute-start(bf16[3,768,640]{2,1,0:T(8,128)(2,1)} %gather_fusion.2), channel_id=1, source_target_pairs={{0,16},{16,0},{1,17},{17,1},{2,18},{18,2},{3,19},{19,3},{4,20},{20... | collective-permute-start | bytes 8847368 | tf_op jit(solution)/shard_map/ppermute | solution.py:107
  331.7 15.6 %slice-start = ((s8[7864320]{0:T(1024)(128)(4,1)}), s8[4194304]{0:T(1024)(128)(4,1)S(1)}, s32[]{:S(2)}) async-start(s8[7864320]{0:T(1024)(128)(4,1)} %bitcast.99), calls=%async_computation.5 | async-start | bytes 8388608
  340.5 6.8 %copy-start.6 = (bf16[5120,1,384]{0,2,1:T(8,128)(2,1)S(1)}, bf16[5120,1,384]{0,2,1:T(8,128)(2,1)}, u32[]{:S(2)}) copy-start(bf16[5120,1,384]{0,2,1:T(8,128)(2,1)} %all-gather.18.cloned.1.call-done) | copy-start | bytes 11796484
  340.5 6.8 %slice-start.1 = ((s8[7864320]{0:T(1024)(128)(4,1)}), s8[3670016]{0:T(1024)(128)(4,1)S(1)}, s32[]{:S(2)}) async-start(s8[7864320]{0:T(1024)(128)(4,1)} %bitcast.99), calls=%async_computation.6 | async-start | bytes 7340032
  360.3 5.0 copy-start.9
  360.3 5.0 copy-start.10
  360.3 5.0 copy-start.11
  379.2 6.1 %copy-start.3 = (f32[384,768]{1,0:T(8,128)}, f32[384,768]{1,0:T(8,128)S(1)}, u32[]{:S(2)}) copy-start(f32[384,768]{1,0:T(8,128)S(1)} %fusion.17) | copy-start | bytes 3538948
  379.2 6.1 %copy-start.2 = (f32[384,768]{1,0:T(8,128)S(1)}, f32[384,768]{1,0:T(8,128)}, u32[]{:S(2)}) copy-start(f32[384,768]{1,0:T(8,128)} %fusion.5) | copy-start | bytes 3538948
  379.2 6.1 %copy-start.5 = (f32[384,768]{1,0:T(8,128)S(1)}, f32[384,768]{1,0:T(8,128)}, u32[]{:S(2)}) copy-start(f32[384,768]{1,0:T(8,128)} %fusion.3) | copy-start | bytes 3538948
  386.9 2.0 copy-start.17
  391.8 37.0 %collective-permute-start.4 = (bf16[768,768]{1,0:T(8,128)(2,1)}, bf16[768,768]{1,0:T(8,128)(2,1)}, u32[]{:S(2)}, u32[]{:S(2)}) collective-permute-start(bf16[768,768]{1,0:T(8,128)(2,1)} %multiply_convert_fusion), channel_id=1, source_target_pairs={{4,0},{8,4},{12,8},{5,1},{9,5},{13,9},{6,2},{10,6},{14,10},{7,3},{... | collective-permute-start | bytes 3538952 | tf_op jit(solution)/shard_map/ppermute | solution.py:17
  393.1 35.7 %collective-permute-start.3 = (bf16[768,768]{1,0:T(8,128)(2,1)}, bf16[768,768]{1,0:T(8,128)(2,1)}, u32[]{:S(2)}, u32[]{:S(2)}) collective-permute-start(bf16[768,768]{1,0:T(8,128)(2,1)} %multiply_convert_fusion), channel_id=1, source_target_pairs={{0,4},{4,8},{8,12},{1,5},{5,9},{9,13},{2,6},{6,10},{10,14},{3,7},{... | collective-permute-start | bytes 3538952 | tf_op jit(solution)/shard_map/ppermute | solution.py:17
  398.7 8.6 %copy-start.15 = (bf16[768,384]{1,0:T(8,128)(2,1)S(1)}, bf16[768,384]{1,0:T(8,128)(2,1)}, u32[]{:S(2)}) copy-start(bf16[768,384]{1,0:T(8,128)(2,1)} %fusion.8) | copy-start | bytes 1769476
  398.7 16.8 %copy-start.16 = (f32[768,6]{0,1:T(8,128)S(1)}, f32[768,6]{0,1:T(8,128)}, u32[]{:S(2)}) copy-start(f32[768,6]{0,1:T(8,128)} %get-tuple-element.23) | copy-start | bytes 55300
  407.4 8.2 %copy-start.4 = (f32[384,768]{1,0:T(8,128)S(1)}, f32[384,768]{1,0:T(8,128)}, u32[]{:S(2)}) copy-start(f32[384,768]{1,0:T(8,128)} %copy-done.3) | copy-start | bytes 3538948
  408.7 37.9 %collective-permute-start.7 = (bf16[768,768]{1,0:T(8,128)(2,1)}, bf16[768,768]{1,0:T(8,128)(2,1)}, u32[]{:S(2)}, u32[]{:S(2)}) collective-permute-start(bf16[768,768]{1,0:T(8,128)(2,1)} %fusion.7), channel_id=1, source_target_pairs={{4,0},{8,4},{12,8},{5,1},{9,5},{13,9},{6,2},{10,6},{14,10},{7,3},{... | collective-permute-start | bytes 3538952 | tf_op jit(solution)/shard_map/ppermute | solution.py:17
  410.0 37.8 %collective-permute-start.6 = (bf16[768,768]{1,0:T(8,128)(2,1)}, bf16[768,768]{1,0:T(8,128)(2,1)}, u32[]{:S(2)}, u32[]{:S(2)}) collective-permute-start(bf16[768,768]{1,0:T(8,128)(2,1)} %fusion.7), channel_id=1, source_target_pairs={{0,4},{4,8},{8,12},{1,5},{5,9},{9,13},{2,6},{6,10},{10,14},{3,7},{... | collective-permute-start | bytes 3538952 | tf_op jit(solution)/shard_map/ppermute | solution.py:17
  417.8 4.9 copy-start.8
  422.6 5.0 copy-start.1
  422.6 5.0 copy-start.18
  524.4 7.0 %copy-start = (bf16[3072,1,640]{2,0,1:T(8,128)(2,1)S(1)}, bf16[3072,1,640]{2,0,1:T(8,128)(2,1)}, u32[]{:S(2)}) copy-start(bf16[3072,1,640]{2,0,1:T(8,128)(2,1)} %copy.32) | copy-start | bytes 11796484
  524.4 7.0 %copy-start.19 = (bf16[768,3072]{1,0:T(8,128)(2,1)S(1)}, bf16[768,3072]{1,0:T(8,128)(2,1)}, u32[]{:S(2)}) copy-start(bf16[768,3072]{1,0:T(8,128)(2,1)} %all-gather.10.cloned.1.call-done) | copy-start | bytes 14155780
Sparse Core Ops, SparseCore 0:
  10.4 79.1 all-gather.17
  91.2 74.9 all-gather.15
  167.7 74.9 all-gather.11
  244.2 74.9 all-gather.13
  486.3 38.0 all-gather.9

commit v5 on v4

--- a/solution.py
+++ b/solution.py
@@ -6,6 +6,7 @@
 from jax.experimental import pallas as pl
 from jax.experimental.pallas import tpu as pltpu
 from jax.sharding import PartitionSpec as P
+
 
 HEAD_DIM = 128
 TILE = 128
@@ -90,18 +91,21 @@
     )(blocks.astype(jnp.int32), limits.astype(jnp.int32), query, keys, values)
 
 
-def split_gather(piece):
+def fetch(piece):
     parts = lax.axis_size("clips")
-    chunks = lax.axis_size("frames")
     assert parts == 2
     ci = lax.axis_index("clips")
-    fi = lax.axis_index("frames")
     rows, cols = piece.shape
-    share = cols // parts
-    halves = piece.reshape(rows, parts, share)
+    halves = piece.reshape(rows, parts, cols // parts)
     mine = lax.dynamic_index_in_dim(halves, ci, 1, keepdims=False)
     other = lax.dynamic_index_in_dim(halves, 1 - ci, 1, keepdims=False)
-    got = lax.all_gather(mine, "frames", axis=0, tiled=False)
+    return lax.all_gather(mine, "frames", axis=0, tiled=False), other
+
+
+def trade(fetched):
+    got, other = fetched
+    chunks, rows, share = got.shape
+    fi = lax.axis_index("frames")
     order = jnp.arange(chunks, dtype=jnp.int32)
     foreign = order[: chunks - 1] + (order[: chunks - 1] >= fi).astype(jnp.int32)
     recv = lax.ppermute(got[foreign], "clips", [(0, 1), (1, 0)])
@@ -117,14 +121,17 @@
     return jnp.where(first, jnp.concatenate([own, rest], 1), jnp.concatenate([rest, own], 1))
 
 
-def per_device(tokens, w_query, w_key, w_value, q_gain, k_gain, w_out, key_blocks, slab_counts):
-    k_rows = split_gather(w_key)
-    v_rows = split_gather(w_value)
-    q_rows = split_gather(w_query)
-    o_rows = split_gather(w_out)
-    query = head_norm(split_dot(tokens, q_rows), q_gain)
-    keys = head_norm(split_dot(tokens, k_rows), k_gain)
-    values = split_dot(tokens, v_rows).astype(jnp.bfloat16)
+def layer(tokens, w_query, w_key, w_value, q_gain, k_gain, w_out, key_blocks, slab_counts):
+    k_got = fetch(w_key)
+    v_got = fetch(w_value)
+    q_got = fetch(w_query)
+    o_got = fetch(w_out)
+    keys = head_norm(split_dot(tokens, trade(k_got)), k_gain)
+    values = split_dot(tokens, trade(v_got)).astype(jnp.bfloat16)
+    keys, values, q_got = lax.optimization_barrier((keys, values, q_got))
+    query = head_norm(split_dot(tokens, trade(q_got)), q_gain)
+    keys, values, o_got = lax.optimization_barrier((keys, values, o_got))
+    o_rows = trade(o_got)
     before = shifted((keys, values), "frames", 1)
     after = shifted((keys, values), "frames", -1)
     key_window = jnp.concatenate([before[0], keys, after[0]], axis=0)
@@ -133,7 +140,6 @@
     zero = jnp.zeros((1,), jnp.int32)
     count_pad = jnp.concatenate([zero, slab_counts, zero], axis=0)
     limits = lax.dynamic_slice_in_dim(count_pad, position, 3, 0)
-    query, o_rows = lax.optimization_barrier((query, o_rows))
     attended = attend(query, key_window, value_window, key_blocks, limits)
     whole = lax.all_gather(attended, "wshard", axis=1, tiled=True)
     mixed = split_dot(whole, o_rows)
@@ -142,7 +148,7 @@
 
 def solution(mesh):
     return jax.shard_map(
-        per_device,
+        layer,
         mesh=mesh,
         in_specs=(
             P(("clips", "frames"), None),

time: 545 us -> 538 us (0.987)
  waiting for transfers between devices: 305 us -> 293 us
    all_gather x5, waiting for transfers between devices: 289 us -> 197 us  [the longest x4 197 us: fetch(): return (lax.all_gather(mine, 'frames', axis=0, tiled=False), other)]
    ppermute x4, waiting for transfers between devices: 0.01 us -> 63 us  [trade(): recv = lax.ppermute(got[foreign], 'clips', [(0, 1), (1, 0)])]
    ppermute x4, waiting for transfers between devices: 15.5 us -> 32.8 us  [shifted(): return lax.ppermute(value, axis, pairs)]
    select_n x4 -> x5, other arithmetic: 13.2 us -> 15.3 us  [the longest x3 15.3 us: trade(): jnp.where((order == fi)[:, None, None], other[None], recv[slot])]
    unnamed x50 -> x36, local copies, waits for them, and re-layouts: 10.9 us -> 11.6 us
  transfers between devices with their start and end apart: 13 -> 13, of which waited for: 7 -> 9; matrix products, arithmetic and copies ran while one was open for 28% -> 26% of each run, Pallas kernels for 0% -> 0%
where the time goes in v5:
time: 538 us; the launch traced here: 534 us
  waiting for transfers between devices  293 us (54%)
  local copies, waits for them, and re-layouts  91.4 us (17%)
  matrix products  55 us (10%)
  Pallas kernels  35.1 us (7%)
  other arithmetic  26.6 us (5%)
  starting transfers between devices  18.3 us (3%)
  between operations  13.7 us (3%)
    all_gather x4, waiting for transfers between devices, fetch(): return (lax.all_gather(mine, 'frames', axis=0, tiled=False), other)  197 us
    ppermute x4, waiting for transfers between devices, trade(): recv = lax.ppermute(got[foreign], 'clips', [(0, 1), (1, 0)])  63 us
    pallas_call x1, Pallas kernels, attend(): pl.pallas_call(attend_kernel, grid_spec=spec, out_shape=jax.ShapeDtypeStr...  35.1 us
    ppermute x4, waiting for transfers between devices, shifted(): return lax.ppermute(value, axis, pairs)  32.8 us
    dot_general x4, matrix products, split_dot(): own = jnp.dot(x, pair[0], preferred_element_type=jnp.float32)  28.1 us
    dot_general x4, matrix products, split_dot(): rest = jnp.dot(x, pair[1], preferred_element_type=jnp.float32)  27 us
    all_gather x4, local copies, waits for them, and re-layouts, fetch(): return (lax.all_gather(mine, 'frames', axis=0, tiled=False), other)  25.1 us
    gather x4, local copies, waits for them, and re-layouts, trade(): recv = lax.ppermute(got[foreign], 'clips', [(0, 1), (1, 0)])  20.2 us
  transfers between devices with their start and end apart: 13, of which 9 were waited for; matrix products, arithmetic and copies ran while one was open for 26% of the time, Pallas kernels for 0%

profile of v5, /device:TPU:0, one launch (start us, length us, event | category | flops | bytes accessed | tf_op | source)
XLA Modules:
  0.0 533.5 jit_solution(11537232627170874421)
XLA Ops:
  6.5 2.7 copy.31
  9.2 1.1 constant_dynamic-slice_fusion.4
  10.4 2.7 copy.26
  13.1 1.5 constant_dynamic-slice_fusion.6
  14.7 2.7 copy.37
  17.4 1.4 constant_dynamic-slice_fusion.2
  18.9 70.8 %all-gather.14.cloned.1.call-done = bf16[5120,1,384]{0,2,1:T(8,128)(2,1)} async-done(((bf16[1280,1,384]{0,2,1:T(8,128)(2,1)}), bf16[5120,1,384]{0,2,1:T(8,128)(2,1)}) %all-gather.14.cloned.1.call-update) | async-done | bytes 3932176 | tf_op jit(solution)/shard_map/all_gather | solution.py:102
  89.6 6.3 %copy.32 = bf16[5120,1,384]{2,0,1:T(8,128)(2,1)} copy(bf16[5120,1,384]{0,2,1:T(8,128)(2,1)} %all-gather.14.cloned.1.call-done) | data formatting | bytes 7864320 | tf_op jit(solution)/shard_map/all_gather | solution.py:102
  95.9 5.3 gather_fusion.2
  101.2 1.4 collective-permute-start.1
  102.6 63.5 %all-gather.12.cloned.1.call-done = bf16[5120,1,384]{0,2,1:T(8,128)(2,1)} async-done(((bf16[1280,1,384]{0,2,1:T(8,128)(2,1)}), bf16[5120,1,384]{0,2,1:T(8,128)(2,1)}) %all-gather.12.cloned.1.call-update) | async-done | bytes 3932176 | tf_op jit(solution)/shard_map/all_gather | solution.py:102
  166.2 6.3 %copy.27 = bf16[5120,1,384]{2,0,1:T(8,128)(2,1)} copy(bf16[5120,1,384]{0,2,1:T(8,128)(2,1)} %all-gather.12.cloned.1.call-done) | data formatting | bytes 7864320 | tf_op jit(solution)/shard_map/all_gather | solution.py:102
  172.5 5.3 gather_fusion
  177.7 1.4 collective-permute-start
  179.2 2.7 copy.41
  181.8 1.4 constant_dynamic-slice_fusion
  183.9 1.3 copy.34
  185.2 1.3 copy.28
  186.6 1.3 copy.39
  187.9 54.8 %all-gather.16.cloned.1.call-done = bf16[5120,1,384]{0,2,1:T(8,128)(2,1)} async-done(((bf16[1280,1,384]{0,2,1:T(8,128)(2,1)}), bf16[5120,1,384]{0,2,1:T(8,128)(2,1)}) %all-gather.16.cloned.1.call-update) | async-done | bytes 3932176 | tf_op jit(solution)/shard_map/all_gather | solution.py:102
  242.7 6.3 %copy.38 = bf16[5120,1,384]{2,0,1:T(8,128)(2,1)} copy(bf16[5120,1,384]{0,2,1:T(8,128)(2,1)} %all-gather.16.cloned.1.call-done) | data formatting | bytes 7864320 | tf_op jit(solution)/shard_map/all_gather | solution.py:102
  249.0 8.6 %fusion.3 = f32[384,768]{1,0:T(8,128)S(1)} fusion(bf16[768,5120]{1,0:T(8,128)(2,1)} %param.9, bf16[5120,1,384]{0,2,1:T(8,128)(2,1)} %all-gather.12.cloned.1.call-done), kind=kOutput, calls=%fused_computation.12 | convolution fusion | flops 3019898880 | bytes 12976128 | tf_op jit(solution)/shard_map/dot_general | solution.py:118
  257.6 7.5 %fusion.6 = bf16[768,384]{1,0:T(8,128)(2,1)} fusion(bf16[768,5120]{1,0:T(8,128)(2,1)} %param.9, bf16[5120,1,384]{0,2,1:T(8,128)(2,1)S(1)} %copy-done.5), kind=kOutput, calls=%fused_computation.28 | convolution fusion | flops 3019898880 | bytes 12386304 | tf_op jit(solution)/shard_map/dot_general | solution.py:118
  265.1 4.9 gather_fusion.3
  270.0 4.9 gather_fusion.1
  274.9 7.0 %bitcast_select_fusion.2 = (bf16[5120,384]{1,0:T(8,128)(2,1)}, bf16[5120,384]{1,0:T(8,128)(2,1)S(1)}) fusion(bf16[4,1280,384]{2,1,0:T(8,128)(2,1)} %gather_fusion.3, pred[5120]{0:T(1024)(128)(4,1)S(1)} %broadcast_in_dim.91, bf16[1280,384]{1,0:T(8,128)(2,1)S(1)} %bitcast.96, bf16[4,1280,384]{2,1,0:T(8,128)(2,1)} %gather_fusion.1, bf16[1280,384]{1,0:T(8,128)(2,1)} %bitcast.97), kind=kLoop, calls=%fused_computation.16 | loop fusion | flops 3932160 | bytes 17699840 | tf_op jit(solution)/shard_map/jit(_where)/select_n | solution.py:113
  281.9 5.6 %fusion.15 = f32[384,768]{1,0:T(8,128)S(1)} fusion(bf16[5120,384]{1,0:T(8,128)(2,1)S(1)} %get-tuple-element.30, bf16[768,5120]{1,0:T(8,128)(2,1)} %param.9), kind=kOutput, calls=%fused_computation.54 | convolution fusion | flops 3019898880 | bytes 12976128 | tf_op jit(solution)/shard_map/dot_general | solution.py:119
  288.1 2.1 copy.30
  290.3 8.6 %convolution_bitcast_fusion = bf16[768,384]{1,0:T(8,128)(2,1)S(1)} fusion(bf16[768,5120]{1,0:T(8,128)(2,1)} %param.9, bf16[5120,384]{1,0:T(8,128)(2,1)} %get-tuple-element.29), kind=kOutput, calls=%fused_computation.29 | convolution fusion | flops 3019898880 | bytes 12386304 | tf_op jit(solution)/shard_map/dot_general | solution.py:119
  298.9 1.3 fusion.5
  300.3 0.8 copy-done.1
  301.0 1.2 multiply_convert_fusion.1
  302.3 4.9 gather_fusion.4
  307.1 1.6 collective-permute-start.2
  308.7 2.2 copy.43
  310.9 8.2 %all-gather.18.cloned.1.call-done = bf16[3072,1,640]{0,2,1:T(8,128)(2,1)} async-done(((bf16[768,1,640]{0,2,1:T(8,128)(2,1)}), bf16[3072,1,640]{0,2,1:T(8,128)(2,1)}) %all-gather.18.cloned.1.call-update) | async-done | bytes 3932176 | tf_op jit(solution)/shard_map/all_gather | solution.py:102
  319.1 6.2 %copy.42 = bf16[3072,1,640]{2,0,1:T(8,128)(2,1)} copy(bf16[3072,1,640]{0,2,1:T(8,128)(2,1)} %all-gather.18.cloned.1.call-done) | data formatting | bytes 7864320 | tf_op jit(solution)/shard_map/all_gather | solution.py:102
  325.4 1.3 collective-permute-start.4
  326.6 4.6 collective-permute-start.3
  331.4 0.6 dynamic_slice.29.lim_ref
  332.0 1.3 collective-permute-start.6
  333.3 4.6 collective-permute-start.5
  337.9 8.8 %fusion.16 = f32[384,768]{1,0:T(8,128)} fusion(bf16[5120,384]{1,0:T(8,128)(2,1)} %bitcast.77, bf16[768,5120]{1,0:T(8,128)(2,1)} %param.9), kind=kOutput, calls=%fused_computation.55 | convolution fusion | flops 3019898880 | bytes 12976128 | tf_op jit(solution)/shard_map/dot_general | solution.py:118
  346.7 9.6 %collective-permute-done.4 = bf16[768,768]{1,0:T(8,128)(2,1)S(1)} collective-permute-done((bf16[768,768]{1,0:T(8,128)(2,1)}, bf16[768,768]{1,0:T(8,128)(2,1)S(1)}, u32[]{:S(2)}, u32[]{:S(2)}) %collective-permute-start.4) | collective-permute-done | bytes 1179680 | tf_op jit(solution)/shard_map/ppermute | solution.py:18
  356.3 1.6 collective-permute-done.3
  357.9 2.0 pad_maximum_fusion.k_ref
  359.9 20.4 %collective-permute-done.6 = bf16[768,768]{1,0:T(8,128)(2,1)S(1)} collective-permute-done((bf16[768,768]{1,0:T(8,128)(2,1)}, bf16[768,768]{1,0:T(8,128)(2,1)S(1)}, u32[]{:S(2)}, u32[]{:S(2)}) %collective-permute-start.6) | collective-permute-done | bytes 1179680 | tf_op jit(solution)/shard_map/ppermute | solution.py:18
  380.3 1.3 collective-permute-done.5
  381.6 2.1 pad_maximum_fusion.1.v_ref
  383.6 3.0 gather_fusion.5
  386.6 3.3 bitcast_select_fusion.1
  389.9 5.7 %fusion.17 = f32[384,768]{1,0:T(8,128)S(1)} fusion(bf16[5120,384]{1,0:T(8,128)(2,1)S(1)} %bitcast_select_fusion.1, bf16[768,5120]{1,0:T(8,128)(2,1)} %param.9), kind=kOutput, calls=%fused_computation.56 | convolution fusion | flops 3019898880 | bytes 12976128 | tf_op jit(solution)/shard_map/dot_general | solution.py:119
  396.2 2.0 copy.40
  398.1 2.9 multiply_convert_fusion.q_ref
  401.0 35.1 %shard_map.91 = bf16[768,768]{1,0:T(8,128)(2,1)} custom-call(s32[6,8]{1,0:T(8,128)} %kb_ref.1, s32[3]{0:T(128)} %dynamic_slice.29.lim_ref, bf16[768,768]{1,0:T(8,128)(2,1)} %multiply_convert_fusion.q_ref, bf16[2304,768]{1,0:T(8,128)(2,1)} %pad_maximum_fusion.k_ref, bf16[2304,768]{1,0:T(8,128)(2,1)} %pad_maximum_fusion.1.v_ref), custom_call_target="tpu_custom_call" | custom-call | tf_op jit(solution)/shard_map/pallas_call | solution.py:86
  436.2 4.8 gather_fusion.6
  441.0 1.5 collective-permute-start.7
  442.5 63.0 %collective-permute-done.7 = bf16[3,768,640]{2,1,0:T(8,128)(2,1)S(1)} collective-permute-done((bf16[3,768,640]{2,1,0:T(8,128)(2,1)}, bf16[3,768,640]{2,1,0:T(8,128)(2,1)S(1)}, u32[]{:S(2)}, u32[]{:S(2)}) %collective-permute-start.7) | collective-permute-done | bytes 2949152 | tf_op jit(solution)/shard_map/ppermute | solution.py:111
  505.5 3.0 gather_fusion.7
  508.5 5.0 bitcast_select_fusion
  513.5 7.0 %fusion.19 = bf16[768,640]{0,1:T(8,128)(2,1)S(1)} fusion(bf16[768,3072]{1,0:T(8,128)(2,1)} %all-gather.10.cloned.1.call-done, bf16[3072,640]{1,0:T(8,128)(2,1)} %bitcast_select_fusion), kind=kOutput, calls=%fused_computation.58 | convolution fusion | flops 3019898880 | bytes 9633792 | tf_op jit(solution)/shard_map/dot_general | solution.py:119
  520.5 3.3 fusion.18
  523.8 0.7 fusion
  524.5 2.3 copy.44
  (62 shorter events, 2.1 us)
Async XLA Ops:
  6.5 83.1 %all-gather.14.cloned.1.call-start = ((), (), s32[]{:S(2)}) async-start(), calls=%async_computation.2 | async-start | bytes 4915200 | tf_op jit(solution)/shard_map/all_gather | solution.py:102
  10.3 155.8 %all-gather.12.cloned.1.call-start = ((), (), s32[]{:S(2)}) async-start(), calls=%async_computation.1 | async-start | bytes 4915200 | tf_op jit(solution)/shard_map/all_gather | solution.py:102
  14.6 228.1 %all-gather.16.cloned.1.call-start = ((), (), s32[]{:S(2)}) async-start(), calls=%async_computation.3 | async-start | bytes 4915200 | tf_op jit(solution)/shard_map/all_gather | solution.py:102
  18.8 300.4 %all-gather.18.cloned.1.call-start = ((), (), s32[]{:S(2)}) async-start(), calls=%async_computation.4 | async-start | bytes 4915200 | tf_op jit(solution)/shard_map/all_gather | solution.py:102
  101.2 163.9 %collective-permute-start.1 = (bf16[3,1280,384]{2,1,0:T(8,128)(2,1)}, bf16[3,1280,384]{2,1,0:T(8,128)(2,1)}, u32[]{:S(2)}, u32[]{:S(2)}) collective-permute-start(bf16[3,1280,384]{2,1,0:T(8,128)(2,1)} %gather_fusion.2), channel_id=1, source_target_pairs={{0,16},{16,0},{1,17},{17,1},{2,18},{18,2},{3,19},{19,3},{4,20},{20... | collective-permute-start | bytes 8847368 | tf_op jit(solution)/shard_map/ppermute | solution.py:111
  177.7 92.3 %collective-permute-start = (bf16[3,1280,384]{2,1,0:T(8,128)(2,1)}, bf16[3,1280,384]{2,1,0:T(8,128)(2,1)}, u32[]{:S(2)}, u32[]{:S(2)}) collective-permute-start(bf16[3,1280,384]{2,1,0:T(8,128)(2,1)} %gather_fusion), channel_id=1, source_target_pairs={{0,16},{16,0},{1,17},{17,1},{2,18},{18,2},{3,19},{19,3},{4,20},{20... | collective-permute-start | bytes 8847368 | tf_op jit(solution)/shard_map/ppermute | solution.py:111
  183.3 2.0 copy-start.6
  183.3 3.3 copy-start.7
  183.3 330.2 %all-gather.10.cloned.1.call-start = ((), (), s32[]{:S(2)}) async-start(), calls=%async_computation | async-start | bytes 5898240 | tf_op jit(solution)/shard_map/all_gather | solution.py:144
  183.8 4.1 copy-start.12
  249.0 8.6 %copy-start.5 = (bf16[5120,1,384]{0,2,1:T(8,128)(2,1)S(1)}, bf16[5120,1,384]{0,2,1:T(8,128)(2,1)}, u32[]{:S(2)}) copy-start(bf16[5120,1,384]{0,2,1:T(8,128)(2,1)} %all-gather.14.cloned.1.call-done) | copy-start | bytes 11796484
  270.0 4.9 copy-start.8
  290.3 8.7 %copy-start.9 = (bf16[768,384]{1,0:T(8,128)(2,1)S(1)}, bf16[768,384]{1,0:T(8,128)(2,1)}, u32[]{:S(2)}) copy-start(bf16[768,384]{1,0:T(8,128)(2,1)} %fusion.6) | copy-start | bytes 1769476
  290.3 10.0 %copy-start.10 = (f32[768]{0:T(1024)S(1)}, f32[768]{0:T(1024)}, u32[]{:S(2)}) copy-start(f32[768]{0:T(1024)} %param.14) | copy-start | bytes 9220
  298.9 2.1 copy-start.1
  307.1 76.5 %collective-permute-start.2 = (bf16[3,1280,384]{2,1,0:T(8,128)(2,1)}, bf16[3,1280,384]{2,1,0:T(8,128)(2,1)S(1)}, u32[]{:S(2)}, u32[]{:S(2)}) collective-permute-start(bf16[3,1280,384]{2,1,0:T(8,128)(2,1)} %gather_fusion.4), channel_id=1, source_target_pairs={{0,16},{16,0},{1,17},{17,1},{2,18},{18,2},{3,19},{19,3},{4,20},{20... | collective-permute-start | bytes 8847368 | tf_op jit(solution)/shard_map/ppermute | solution.py:111
  310.9 20.4 %copy-start.15 = (s32[4]{0:T(128)S(1)}, s32[4]{0:T(128)}, u32[]{:S(2)}) copy-start(s32[4]{0:T(128)} %param.17) | copy-start | bytes 52
  325.4 30.9 %collective-permute-start.4 = (bf16[768,768]{1,0:T(8,128)(2,1)}, bf16[768,768]{1,0:T(8,128)(2,1)S(1)}, u32[]{:S(2)}, u32[]{:S(2)}) collective-permute-start(bf16[768,768]{1,0:T(8,128)(2,1)} %multiply_convert_fusion.1), channel_id=1, source_target_pairs={{4,0},{8,4},{12,8},{5,1},{9,5},{13,9},{6,2},{10,6},{14,10},{7,3},{... | collective-permute-start | bytes 3538952 | tf_op jit(solution)/shard_map/ppermute | solution.py:18
  326.6 31.2 %collective-permute-start.3 = (bf16[768,768]{1,0:T(8,128)(2,1)}, bf16[768,768]{1,0:T(8,128)(2,1)S(1)}, u32[]{:S(2)}, u32[]{:S(2)}) collective-permute-start(bf16[768,768]{1,0:T(8,128)(2,1)} %multiply_convert_fusion.1), channel_id=1, source_target_pairs={{0,4},{4,8},{8,12},{1,5},{5,9},{9,13},{2,6},{6,10},{10,14},{3,7},{... | collective-permute-start | bytes 3538952 | tf_op jit(solution)/shard_map/ppermute | solution.py:18
  332.0 48.3 %collective-permute-start.6 = (bf16[768,768]{1,0:T(8,128)(2,1)}, bf16[768,768]{1,0:T(8,128)(2,1)S(1)}, u32[]{:S(2)}, u32[]{:S(2)}) collective-permute-start(bf16[768,768]{1,0:T(8,128)(2,1)} %fusion.5), channel_id=1, source_target_pairs={{4,0},{8,4},{12,8},{5,1},{9,5},{13,9},{6,2},{10,6},{14,10},{7,3},{... | collective-permute-start | bytes 3538952 | tf_op jit(solution)/shard_map/ppermute | solution.py:18
  333.3 48.3 %collective-permute-start.5 = (bf16[768,768]{1,0:T(8,128)(2,1)}, bf16[768,768]{1,0:T(8,128)(2,1)S(1)}, u32[]{:S(2)}, u32[]{:S(2)}) collective-permute-start(bf16[768,768]{1,0:T(8,128)(2,1)} %fusion.5), channel_id=1, source_target_pairs={{0,4},{4,8},{8,12},{1,5},{5,9},{9,13},{2,6},{6,10},{10,14},{3,7},{... | collective-permute-start | bytes 3538952 | tf_op jit(solution)/shard_map/ppermute | solution.py:18
  337.9 19.9 %copy-start.4 = (bf16[768,768]{1,0:T(8,128)(2,1)S(1)}, bf16[768,768]{1,0:T(8,128)(2,1)}, u32[]{:S(2)}) copy-start(bf16[768,768]{1,0:T(8,128)(2,1)} %multiply_convert_fusion.1) | copy-start | bytes 3538948
  346.7 34.9 %copy-start.2 = (bf16[768,768]{1,0:T(8,128)(2,1)S(1)}, bf16[768,768]{1,0:T(8,128)(2,1)}, u32[]{:S(2)}) copy-start(bf16[768,768]{1,0:T(8,128)(2,1)} %fusion.5) | copy-start | bytes 3538948
  389.9 5.7 %copy-start.3 = (f32[384,768]{1,0:T(8,128)S(1)}, f32[384,768]{1,0:T(8,128)}, u32[]{:S(2)}) copy-start(f32[384,768]{1,0:T(8,128)} %fusion.16) | copy-start | bytes 3538948
  396.2 2.0 copy-start.11
  436.2 6.3 %copy-start.13 = (pred[4]{0:T(512)(128)(4,1)S(1)}, pred[4]{0:T(512)(128)(4,1)}, u32[]{:S(2)}) copy-start(pred[4]{0:T(512)(128)(4,1)} %copy-done.12) | copy-start | bytes 16
  441.0 64.6 %collective-permute-start.7 = (bf16[3,768,640]{2,1,0:T(8,128)(2,1)}, bf16[3,768,640]{2,1,0:T(8,128)(2,1)S(1)}, u32[]{:S(2)}, u32[]{:S(2)}) collective-permute-start(bf16[3,768,640]{2,1,0:T(8,128)(2,1)} %gather_fusion.6), channel_id=1, source_target_pairs={{0,16},{16,0},{1,17},{17,1},{2,18},{18,2},{3,19},{19,3},{4,20},{20... | collective-permute-start | bytes 8847368 | tf_op jit(solution)/shard_map/ppermute | solution.py:111
  513.5 7.0 %copy-start = (bf16[3072,1,640]{2,0,1:T(8,128)(2,1)S(1)}, bf16[3072,1,640]{2,0,1:T(8,128)(2,1)}, u32[]{:S(2)}) copy-start(bf16[3072,1,640]{2,0,1:T(8,128)(2,1)} %copy.42) | copy-start | bytes 11796484
  513.5 7.0 %copy-start.14 = (bf16[768,3072]{1,0:T(8,128)(2,1)S(1)}, bf16[768,3072]{1,0:T(8,128)(2,1)}, u32[]{:S(2)}) copy-start(bf16[768,3072]{1,0:T(8,128)(2,1)} %all-gather.10.cloned.1.call-done) | copy-start | bytes 14155780
Sparse Core Ops, SparseCore 0:
  10.5 79.1 all-gather.13
  91.2 74.9 all-gather.11
  167.7 74.9 all-gather.15
  244.2 74.9 all-gather.17
  436.3 37.8 all-gather.9

commit v6 on v5

--- a/solution.py
+++ b/solution.py
@@ -92,31 +92,39 @@
 
 
 def fetch(piece):
-    parts = lax.axis_size("clips")
-    assert parts == 2
+    assert lax.axis_size("clips") == 2
     ci = lax.axis_index("clips")
-    rows, cols = piece.shape
-    halves = piece.reshape(rows, parts, cols // parts)
-    mine = lax.dynamic_index_in_dim(halves, ci, 1, keepdims=False)
-    other = lax.dynamic_index_in_dim(halves, 1 - ci, 1, keepdims=False)
-    return lax.all_gather(mine, "frames", axis=0, tiled=False), other
+    share = piece.shape[1] // 2
+    mine = lax.dynamic_slice_in_dim(piece, ci * share, share, 1)
+    other = lax.dynamic_slice_in_dim(piece, (1 - ci) * share, share, 1)
+    return lax.all_gather(mine, "frames", axis=0, tiled=True), other
 
 
 def trade(fetched):
     got, other = fetched
-    chunks, rows, share = got.shape
+    rows = other.shape[0]
+    chunks = got.shape[0] // rows
     fi = lax.axis_index("frames")
-    order = jnp.arange(chunks, dtype=jnp.int32)
-    foreign = order[: chunks - 1] + (order[: chunks - 1] >= fi).astype(jnp.int32)
-    recv = lax.ppermute(got[foreign], "clips", [(0, 1), (1, 0)])
-    slot = jnp.clip(order - (order > fi).astype(jnp.int32), 0, chunks - 2)
-    whole_other = jnp.where((order == fi)[:, None, None], other[None], recv[slot])
-    return got.reshape(chunks * rows, share), whole_other.reshape(chunks * rows, share)
+    recv = []
+    for k in range(1, chunks):
+        at = (fi + k) % chunks
+        part = lax.dynamic_slice_in_dim(got, at * rows, rows, 0)
+        recv.append(lax.ppermute(part, "clips", [(0, 1), (1, 0)]))
+    return got, other, recv
 
 
-def split_dot(x, pair):
-    own = jnp.dot(x, pair[0], preferred_element_type=jnp.float32)
-    rest = jnp.dot(x, pair[1], preferred_element_type=jnp.float32)
+def split_dot(x, traded):
+    got, other, recv = traded
+    rows = other.shape[0]
+    chunks = got.shape[0] // rows
+    fi = lax.axis_index("frames")
+    own = jnp.dot(x, got, preferred_element_type=jnp.float32)
+    rest = jnp.dot(lax.dynamic_slice_in_dim(x, fi * rows, rows, 1), other,
+                   preferred_element_type=jnp.float32)
+    for k, part in enumerate(recv, 1):
+        at = (fi + k) % chunks
+        rest = rest + jnp.dot(lax.dynamic_slice_in_dim(x, at * rows, rows, 1), part,
+                              preferred_element_type=jnp.float32)
     first = lax.axis_index("clips") == 0
     return jnp.where(first, jnp.concatenate([own, rest], 1), jnp.concatenate([rest, own], 1))
 

time: 538 us -> 495 us (0.920)
  local copies, waits for them, and re-layouts: 91.4 us -> 32.3 us
  waiting for transfers between devices: 293 us -> 309 us
  other arithmetic: 26.6 us -> 16 us
  starting transfers between devices: 18.3 us -> 28.2 us
    ppermute x4 -> x12, waiting for transfers between devices: 63 us -> 99 us  [trade(): recv.append(lax.ppermute(part, 'clips', [(0, 1), (1, 0)]))]
    gather x8 -> x0, local copies, waits for them, and re-layouts: 36 us -> none  [the longest x4 20.2 us: trade(): recv = lax.ppermute(got[foreign], 'clips', [(0, 1), (1, 0)])]
    all_gather x4 -> x0, local copies, waits for them, and re-layouts: 25.1 us -> none  [fetch(): return (lax.all_gather(mine, 'frames', axis=0, tiled=False), other)]
    all_gather x4, waiting for transfers between devices: 197 us -> 178 us  [fetch(): return (lax.all_gather(mine, 'frames', axis=0, tiled=True), other)]
    select_n x5 -> x0, other arithmetic: 15.3 us -> none  [the longest x3 15.3 us: trade(): jnp.where((order == fi)[:, None, None], other[None], recv[slot])]
    ppermute x4, waiting for transfers between devices: 32.8 us -> 20.1 us  [shifted(): return lax.ppermute(value, axis, pairs)]
    all_gather x1, waiting for transfers between devices: 0.01 us -> 12.2 us  [layer(): whole = lax.all_gather(attended, 'wshard', axis=1, tiled=True)]
    dynamic_slice x8, local copies, waits for them, and re-layouts: 11.6 us -> 21 us  [the longest x4 11.5 us: trade(): part = lax.dynamic_slice_in_dim(got, at * rows, rows, 0)]
  transfers between devices with their start and end apart: 13 -> 21, of which waited for: 9 -> 12; matrix products, arithmetic and copies ran while one was open for 26% -> 19% of each run, Pallas kernels for 0% -> 0%
where the time goes in v6:
time: 495 us; the launch traced here: 494 us
  waiting for transfers between devices  309 us (62%)
  matrix products  59.6 us (12%)
  Pallas kernels  34.9 us (7%)
  local copies, waits for them, and re-layouts  32.3 us (7%)
  starting transfers between devices  28.2 us (6%)
  other arithmetic  16 us (3%)
  between operations  13.7 us (3%)
    all_gather x4, waiting for transfers between devices, fetch(): return (lax.all_gather(mine, 'frames', axis=0, tiled=True), other)  178 us
    ppermute x12, waiting for transfers between devices, trade(): recv.append(lax.ppermute(part, 'clips', [(0, 1), (1, 0)]))  99 us
    pallas_call x1, Pallas kernels, attend(): pl.pallas_call(attend_kernel, grid_spec=spec, out_shape=jax.ShapeDtypeStr...  34.9 us
    dot_general x12, matrix products, split_dot(): jnp.dot(lax.dynamic_slice_in_dim(x, at * rows, rows, 1), part, preferred_...  28.3 us
    dot_general x4, matrix products, split_dot(): own = jnp.dot(x, got, preferred_element_type=jnp.float32)  20.9 us
    ppermute x4, waiting for transfers between devices, shifted(): return lax.ppermute(value, axis, pairs)  20.1 us
    ppermute x12, starting transfers between devices, trade(): recv.append(lax.ppermute(part, 'clips', [(0, 1), (1, 0)]))  14.1 us
    ppermute x4, starting transfers between devices, shifted(): return lax.ppermute(value, axis, pairs)  13.9 us
  transfers between devices with their start and end apart: 21, of which 12 were waited for; matrix products, arithmetic and copies ran while one was open for 19% of the time, Pallas kernels for 0%

profile of v6, /device:TPU:0, one launch (start us, length us, event | category | flops | bytes accessed | tf_op | source)
XLA Modules:
  0.0 493.6 jit_solution(13192934297078897294)
XLA Ops:
  6.5 2.4 constant_dynamic-slice_fusion.13
  9.1 1.1 constant_dynamic-slice_fusion.17
  10.2 3.0 constant_dynamic-slice_fusion.8
  13.3 3.0 constant_dynamic-slice_fusion.3
  16.4 3.7 fusion.24
  20.1 2.8 fusion.22
  23.7 64.6 %all-gather.8.cloned.1.call-done = bf16[5120,384]{1,0:T(8,128)(2,1)} async-done(((bf16[1280,384]{1,0:T(8,128)(2,1)}), bf16[5120,384]{1,0:T(8,128)(2,1)}) %all-gather.8.cloned.1.call-update) | async-done | bytes 3932176 | tf_op jit(solution)/shard_map/all_gather | solution.py:100
  88.3 3.5 constant_dynamic-slice_fusion.12
  91.8 1.5 collective-permute-start.3
  93.9 71.0 %all-gather.6.cloned.1.call-done = bf16[5120,384]{1,0:T(8,128)(2,1)} async-done(((bf16[1280,384]{1,0:T(8,128)(2,1)}), bf16[5120,384]{1,0:T(8,128)(2,1)}) %all-gather.6.cloned.1.call-update) | async-done | bytes 3932176 | tf_op jit(solution)/shard_map/all_gather | solution.py:100
  164.8 2.2 constant_dynamic-slice_fusion.16
  167.1 1.5 collective-permute-start
  169.2 1.5 collective-permute-start.1
  170.7 6.9 %fusion.83 = f32[384,768]{1,0:T(8,128)S(1)} fusion(bf16[5120,384]{1,0:T(8,128)(2,1)S(1)} %copy-done.7, bf16[768,5120]{1,0:T(8,128)(2,1)} %param.9), kind=kOutput, calls=%fused_computation.96 | convolution fusion | flops 3019898880 | bytes 12976128 | tf_op jit(solution)/shard_map/dot_general | solution.py:121
  177.7 5.1 %convolution_bitcast_fusion = bf16[768,384]{1,0:T(8,128)(2,1)} fusion(bf16[768,5120]{1,0:T(8,128)(2,1)S(1)} %bitcast.45, bf16[5120,384]{1,0:T(8,128)(2,1)S(1)} %copy-done.6), kind=kOutput, calls=%fused_computation.40 | convolution fusion | flops 3019898880 | bytes 12386304 | tf_op jit(solution)/shard_map/dot_general | solution.py:121
  182.7 30.1 %collective-permute-done.2 = bf16[1280,384]{1,0:T(8,128)(2,1)S(1)} collective-permute-done((bf16[1280,384]{1,0:T(8,128)(2,1)S(1)}, bf16[1280,384]{1,0:T(8,128)(2,1)S(1)}, u32[]{:S(2)}, u32[]{:S(2)}) %collective-permute-start.2) | collective-permute-done | bytes 983072 | tf_op jit(solution)/shard_map/ppermute | solution.py:112
  212.8 1.5 collective-permute-start.4
  214.3 1.0 fusion.6
  215.4 18.5 %collective-permute-done.1 = bf16[1280,384]{1,0:T(8,128)(2,1)S(1)} collective-permute-done((bf16[1280,384]{1,0:T(8,128)(2,1)S(1)}, bf16[1280,384]{1,0:T(8,128)(2,1)S(1)}, u32[]{:S(2)}, u32[]{:S(2)}) %collective-permute-start.1) | collective-permute-done | bytes 983072 | tf_op jit(solution)/shard_map/ppermute | solution.py:112
  233.9 1.0 fusion.12
  235.0 1.2 fusion.46
  236.6 1.9 copy.24
  238.6 3.0 fusion.4
  241.6 12.2 %collective-permute-done.4 = bf16[1280,384]{1,0:T(8,128)(2,1)} collective-permute-done((bf16[1280,384]{1,0:T(8,128)(2,1)}, bf16[1280,384]{1,0:T(8,128)(2,1)}, u32[]{:S(2)}, u32[]{:S(2)}) %collective-permute-start.4) | collective-permute-done | bytes 983072 | tf_op jit(solution)/shard_map/ppermute | solution.py:112
  253.8 3.0 fusion.10
  256.8 3.1 fusion.49
  260.3 1.4 copy-done.2
  261.6 1.3 multiply_convert_fusion.1
  263.0 3.7 constant_dynamic-slice_fusion.7
  266.6 1.5 collective-permute-start.6
  268.6 1.5 collective-permute-start.7
  270.1 5.6 %fusion.84 = f32[384,768]{1,0:T(8,128)S(1)} fusion(bf16[5120,384]{1,0:T(8,128)(2,1)S(1)} %copy-done.5, bf16[768,5120]{1,0:T(8,128)(2,1)} %param.9), kind=kOutput, calls=%fused_computation.97 | convolution fusion | flops 3019898880 | bytes 12976128 | tf_op jit(solution)/shard_map/dot_general | solution.py:121
  275.8 42.0 %all-gather.12.cloned.1.call-done = bf16[3072,640]{1,0:T(8,128)(2,1)} async-done(((bf16[768,640]{1,0:T(8,128)(2,1)}), bf16[3072,640]{1,0:T(8,128)(2,1)}) %all-gather.12.cloned.1.call-update) | async-done | bytes 3932176 | tf_op jit(solution)/shard_map/all_gather | solution.py:100
  317.8 1.3 collective-permute-start.10
  319.1 5.7 %collective-permute-start.9 = (bf16[768,768]{1,0:T(8,128)(2,1)}, bf16[768,768]{1,0:T(8,128)(2,1)}, u32[]{:S(2)}, u32[]{:S(2)}) collective-permute-start(bf16[768,768]{1,0:T(8,128)(2,1)} %multiply_convert_fusion.1), channel_id=1, source_target_pairs={{0,4},{4,8},{8,12},{1,5},{5,9},{9,13},{2,6},{6,10},{10,14},{3,7},{... | collective-permute-start | bytes 3538952 | tf_op jit(solution)/shard_map/ppermute | solution.py:18
  324.8 2.8 fusion.20
  327.6 1.3 collective-permute-start.12
  328.9 2.8 fusion.2
  331.7 5.6 %collective-permute-start.11 = (bf16[768,768]{1,0:T(8,128)(2,1)S(1)}, bf16[768,768]{1,0:T(8,128)(2,1)}, u32[]{:S(2)}, u32[]{:S(2)}) collective-permute-start(bf16[768,768]{1,0:T(8,128)(2,1)S(1)} %fusion.1), channel_id=1, source_target_pairs={{0,4},{4,8},{8,12},{1,5},{5,9},{9,13},{2,6},{6,10},{10,14},{3,7},{... | collective-permute-start | bytes 3538952 | tf_op jit(solution)/shard_map/ppermute | solution.py:18
  337.3 2.8 fusion.8
  340.1 3.0 fusion.52
  343.4 1.9 fusion.35
  345.3 2.2 copy.30
  347.6 2.9 multiply_convert_fusion.q_ref
  350.4 3.4 pad_maximum_fusion.k_ref
  353.8 19.0 %collective-permute-done.12 = bf16[768,768]{1,0:T(8,128)(2,1)} collective-permute-done((bf16[768,768]{1,0:T(8,128)(2,1)S(1)}, bf16[768,768]{1,0:T(8,128)(2,1)}, u32[]{:S(2)}, u32[]{:S(2)}) %collective-permute-start.12) | collective-permute-done | bytes 1179680 | tf_op jit(solution)/shard_map/ppermute | solution.py:18
  372.8 1.1 collective-permute-done.11
  373.9 3.2 pad_maximum_fusion.1.v_ref
  377.1 34.9 %shard_map.91 = bf16[768,768]{1,0:T(8,128)(2,1)} custom-call(s32[6,8]{1,0:T(8,128)} %kb_ref.1, s32[3]{0:T(128)} %dynamic_slice.95.lim_ref, bf16[768,768]{1,0:T(8,128)(2,1)} %multiply_convert_fusion.q_ref, bf16[2304,768]{1,0:T(8,128)(2,1)} %pad_maximum_fusion.k_ref, bf16[2304,768]{1,0:T(8,128)(2,1)} %pad_maximum_fusion.1.v_ref), custom_call_target="tpu_custom_call" | custom-call | tf_op jit(solution)/shard_map/pallas_call | solution.py:86
  412.1 2.1 constant_dynamic-slice_fusion
  414.2 1.5 collective-permute-start.14
  416.3 1.5 collective-permute-start.15
  417.8 21.2 %collective-permute-done.14 = bf16[768,640]{1,0:T(8,128)(2,1)} collective-permute-done((bf16[768,640]{1,0:T(8,128)(2,1)S(1)}, bf16[768,640]{1,0:T(8,128)(2,1)}, u32[]{:S(2)}, u32[]{:S(2)}) %collective-permute-start.14) | collective-permute-done | bytes 983072 | tf_op jit(solution)/shard_map/ppermute | solution.py:112
  439.0 12.2 %all-gather.14.cloned.1.call-done = bf16[768,3072]{1,0:T(8,128)(2,1)} async-done(((bf16[768,768]{1,0:T(8,128)(2,1)}), bf16[768,3072]{1,0:T(8,128)(2,1)}) %all-gather.14.cloned.1.call-update) | async-done | bytes 4718608 | tf_op jit(solution)/shard_map/all_gather | solution.py:152
  451.2 2.7 fusion.59
  453.9 6.1 %collective-permute-done.13 = bf16[768,640]{1,0:T(8,128)(2,1)} collective-permute-done((bf16[768,640]{1,0:T(8,128)(2,1)S(1)}, bf16[768,640]{1,0:T(8,128)(2,1)}, u32[]{:S(2)}, u32[]{:S(2)}) %collective-permute-start.13) | collective-permute-done | bytes 983072 | tf_op jit(solution)/shard_map/ppermute | solution.py:112
  460.1 2.5 fusion.61
  462.6 1.0 fusion.63
  463.6 1.1 copy-done.4
  464.7 3.3 fusion.85
  468.0 10.7 %collective-permute-done.15 = bf16[768,640]{1,0:T(8,128)(2,1)} collective-permute-done((bf16[768,640]{1,0:T(8,128)(2,1)S(1)}, bf16[768,640]{1,0:T(8,128)(2,1)}, u32[]{:S(2)}, u32[]{:S(2)}) %collective-permute-start.15) | collective-permute-done | bytes 983072 | tf_op jit(solution)/shard_map/ppermute | solution.py:112
  478.7 2.3 add_add_fusion
  481.0 2.1 fusion
  483.1 4.0 copy.31
  (66 shorter events, 4.4 us)
Async XLA Ops:
  6.5 2.5 copy-start
  6.5 81.8 %all-gather.8.cloned.1.call-start = ((), (), s32[]{:S(2)}) async-start(), calls=%async_computation.1 | async-start | bytes 4915200 | tf_op jit(solution)/shard_map/all_gather | solution.py:100
  9.0 155.8 %all-gather.6.cloned.1.call-start = ((), (), s32[]{:S(2)}) async-start(), calls=%async_computation | async-start | bytes 4915200 | tf_op jit(solution)/shard_map/all_gather | solution.py:100
  10.1 252.8 %all-gather.10.cloned.1.call-start = ((), (), s32[]{:S(2)}) async-start(), calls=%async_computation.2 | async-start | bytes 4915200 | tf_op jit(solution)/shard_map/all_gather | solution.py:100
  13.2 304.6 %all-gather.12.cloned.1.call-start = ((), (), s32[]{:S(2)}) async-start(), calls=%async_computation.3 | async-start | bytes 4915200 | tf_op jit(solution)/shard_map/all_gather | solution.py:100
  16.3 434.9 %all-gather.14.cloned.1.call-start = ((), (), s32[]{:S(2)}) async-start(), calls=%async_computation.4 | async-start | bytes 5898240 | tf_op jit(solution)/shard_map/all_gather | solution.py:152
  16.4 3.7 copy-start.11
  20.1 2.9 copy-start.15
  91.8 164.9 %collective-permute-start.3 = (bf16[1280,384]{1,0:T(8,128)(2,1)}, bf16[1280,384]{1,0:T(8,128)(2,1)}, u32[]{:S(2)}, u32[]{:S(2)}) collective-permute-start(bf16[1280,384]{1,0:T(8,128)(2,1)} %get-tuple-element.27), channel_id=1, source_target_pairs={{0,16},{16,0},{1,17},{17,1},{2,18},{18,2},{3,19},{19,3},{4,20},{20... | collective-permute-start | bytes 2949128 | tf_op jit(solution)/shard_map/ppermute | solution.py:112
  93.3 145.3 %collective-permute-start.5 = (bf16[1280,384]{1,0:T(8,128)(2,1)}, bf16[1280,384]{1,0:T(8,128)(2,1)}, u32[]{:S(2)}, u32[]{:S(2)}) collective-permute-start(bf16[1280,384]{1,0:T(8,128)(2,1)} %get-tuple-element.28), channel_id=1, source_target_pairs={{0,16},{16,0},{1,17},{17,1},{2,18},{18,2},{3,19},{19,3},{4,20},{20... | collective-permute-start | bytes 2949128 | tf_op jit(solution)/shard_map/ppermute | solution.py:112
  164.8 5.8 %copy-start.7 = (bf16[5120,384]{1,0:T(8,128)(2,1)S(1)}, bf16[5120,384]{1,0:T(8,128)(2,1)}, u32[]{:S(2)}) copy-start(bf16[5120,384]{1,0:T(8,128)(2,1)} %all-gather.6.cloned.1.call-done) | copy-start | bytes 11796484
  167.1 67.8 %collective-permute-start = (bf16[1280,384]{1,0:T(8,128)(2,1)S(1)}, bf16[1280,384]{1,0:T(8,128)(2,1)S(1)}, u32[]{:S(2)}, u32[]{:S(2)}) collective-permute-start(bf16[1280,384]{1,0:T(8,128)(2,1)S(1)} %get-tuple-element.30), channel_id=1, source_target_pairs={{0,16},{16,0},{1,17},{17,1},{2,18},{18,2},{3,19},{19,3},{4,20},{20... | collective-permute-start | bytes 2949128 | tf_op jit(solution)/shard_map/ppermute | solution.py:112
  168.6 44.2 %collective-permute-start.2 = (bf16[1280,384]{1,0:T(8,128)(2,1)S(1)}, bf16[1280,384]{1,0:T(8,128)(2,1)S(1)}, u32[]{:S(2)}, u32[]{:S(2)}) collective-permute-start(bf16[1280,384]{1,0:T(8,128)(2,1)S(1)} %get-tuple-element.31), channel_id=1, source_target_pairs={{0,16},{16,0},{1,17},{17,1},{2,18},{18,2},{3,19},{19,3},{4,20},{20... | collective-permute-start | bytes 2949128 | tf_op jit(solution)/shard_map/ppermute | solution.py:112
  169.2 8.4 %slice-start = ((s8[7864320]{0:T(1024)(128)(4,1)}), s8[4194304]{0:T(1024)(128)(4,1)S(1)}, s32[]{:S(2)}) async-start(s8[7864320]{0:T(1024)(128)(4,1)} %bitcast.44), calls=%async_computation.5 | async-start | bytes 8388608
  169.2 8.5 %slice-start.1 = ((s8[7864320]{0:T(1024)(128)(4,1)}), s8[3670016]{0:T(1024)(128)(4,1)S(1)}, s32[]{:S(2)}) async-start(s8[7864320]{0:T(1024)(128)(4,1)} %bitcast.44), calls=%async_computation.6 | async-start | bytes 7340032
  169.2 8.5 %copy-start.6 = (bf16[5120,384]{1,0:T(8,128)(2,1)S(1)}, bf16[5120,384]{1,0:T(8,128)(2,1)}, u32[]{:S(2)}) copy-start(bf16[5120,384]{1,0:T(8,128)(2,1)} %all-gather.8.cloned.1.call-done) | copy-start | bytes 11796484
  169.2 64.7 %collective-permute-start.1 = (bf16[1280,384]{1,0:T(8,128)(2,1)S(1)}, bf16[1280,384]{1,0:T(8,128)(2,1)S(1)}, u32[]{:S(2)}, u32[]{:S(2)}) collective-permute-start(bf16[1280,384]{1,0:T(8,128)(2,1)S(1)} %get-tuple-element.32), channel_id=1, source_target_pairs={{0,16},{16,0},{1,17},{17,1},{2,18},{18,2},{3,19},{19,3},{4,20},{20... | collective-permute-start | bytes 2949128 | tf_op jit(solution)/shard_map/ppermute | solution.py:112
  212.8 41.0 %collective-permute-start.4 = (bf16[1280,384]{1,0:T(8,128)(2,1)}, bf16[1280,384]{1,0:T(8,128)(2,1)}, u32[]{:S(2)}, u32[]{:S(2)}) collective-permute-start(bf16[1280,384]{1,0:T(8,128)(2,1)} %get-tuple-element.29), channel_id=1, source_target_pairs={{0,16},{16,0},{1,17},{17,1},{2,18},{18,2},{3,19},{19,3},{4,20},{20... | collective-permute-start | bytes 2949128 | tf_op jit(solution)/shard_map/ppermute | solution.py:112
  215.3 19.6 %copy-start.8 = (f32[768,384]{0,1:T(8,128)S(1)}, f32[768,384]{0,1:T(8,128)}, u32[]{:S(2)}) copy-start(f32[768,384]{0,1:T(8,128)} %fusion.24) | copy-start | bytes 3538948
  256.8 3.2 copy-start.10
  256.8 3.5 copy-start.13
  260.0 1.7 copy-start.2
  263.0 7.2 %copy-start.5 = (bf16[5120,384]{1,0:T(8,128)(2,1)S(1)}, bf16[5120,384]{1,0:T(8,128)(2,1)}, u32[]{:S(2)}) copy-start(bf16[5120,384]{1,0:T(8,128)(2,1)} %all-gather.10.cloned.1.call-done) | copy-start | bytes 11796484
  266.6 73.5 %collective-permute-start.6 = (bf16[1280,384]{1,0:T(8,128)(2,1)}, bf16[1280,384]{1,0:T(8,128)(2,1)}, u32[]{:S(2)}, u32[]{:S(2)}) collective-permute-start(bf16[1280,384]{1,0:T(8,128)(2,1)} %get-tuple-element.24), channel_id=1, source_target_pairs={{0,16},{16,0},{1,17},{17,1},{2,18},{18,2},{3,19},{19,3},{4,20},{20... | collective-permute-start | bytes 2949128 | tf_op jit(solution)/shard_map/ppermute | solution.py:112
  268.1 59.5 %collective-permute-start.8 = (bf16[1280,384]{1,0:T(8,128)(2,1)}, bf16[1280,384]{1,0:T(8,128)(2,1)}, u32[]{:S(2)}, u32[]{:S(2)}) collective-permute-start(bf16[1280,384]{1,0:T(8,128)(2,1)} %get-tuple-element.25), channel_id=1, source_target_pairs={{0,16},{16,0},{1,17},{17,1},{2,18},{18,2},{3,19},{19,3},{4,20},{20... | collective-permute-start | bytes 2949128 | tf_op jit(solution)/shard_map/ppermute | solution.py:112
  268.6 63.0 %collective-permute-start.7 = (bf16[1280,384]{1,0:T(8,128)(2,1)}, bf16[1280,384]{1,0:T(8,128)(2,1)}, u32[]{:S(2)}, u32[]{:S(2)}) collective-permute-start(bf16[1280,384]{1,0:T(8,128)(2,1)} %get-tuple-element.26), channel_id=1, source_target_pairs={{0,16},{16,0},{1,17},{17,1},{2,18},{18,2},{3,19},{19,3},{4,20},{20... | collective-permute-start | bytes 2949128 | tf_op jit(solution)/shard_map/ppermute | solution.py:112
  275.8 67.3 %copy-start.3 = (f32[384,768]{1,0:T(8,128)}, f32[384,768]{1,0:T(8,128)S(1)}, u32[]{:S(2)}) copy-start(f32[384,768]{1,0:T(8,128)S(1)} %fusion.84) | copy-start | bytes 3538948
  317.8 32.6 %collective-permute-start.10 = (bf16[768,768]{1,0:T(8,128)(2,1)}, bf16[768,768]{1,0:T(8,128)(2,1)}, u32[]{:S(2)}, u32[]{:S(2)}) collective-permute-start(bf16[768,768]{1,0:T(8,128)(2,1)} %multiply_convert_fusion.1), channel_id=1, source_target_pairs={{4,0},{8,4},{12,8},{5,1},{9,5},{13,9},{6,2},{10,6},{14,10},{7,3},{... | collective-permute-start | bytes 3538952 | tf_op jit(solution)/shard_map/ppermute | solution.py:18
  319.1 31.3 %collective-permute-start.9 = (bf16[768,768]{1,0:T(8,128)(2,1)}, bf16[768,768]{1,0:T(8,128)(2,1)}, u32[]{:S(2)}, u32[]{:S(2)}) collective-permute-start(bf16[768,768]{1,0:T(8,128)(2,1)} %multiply_convert_fusion.1), channel_id=1, source_target_pairs={{0,4},{4,8},{8,12},{1,5},{5,9},{9,13},{2,6},{6,10},{10,14},{3,7},{... | collective-permute-start | bytes 3538952 | tf_op jit(solution)/shard_map/ppermute | solution.py:18
  327.6 45.3 %collective-permute-start.12 = (bf16[768,768]{1,0:T(8,128)(2,1)S(1)}, bf16[768,768]{1,0:T(8,128)(2,1)}, u32[]{:S(2)}, u32[]{:S(2)}) collective-permute-start(bf16[768,768]{1,0:T(8,128)(2,1)S(1)} %fusion.1), channel_id=1, source_target_pairs={{4,0},{8,4},{12,8},{5,1},{9,5},{13,9},{6,2},{10,6},{14,10},{7,3},{... | collective-permute-start | bytes 3538952 | tf_op jit(solution)/shard_map/ppermute | solution.py:18
  331.7 42.2 %collective-permute-start.11 = (bf16[768,768]{1,0:T(8,128)(2,1)S(1)}, bf16[768,768]{1,0:T(8,128)(2,1)}, u32[]{:S(2)}, u32[]{:S(2)}) collective-permute-start(bf16[768,768]{1,0:T(8,128)(2,1)S(1)} %fusion.1), channel_id=1, source_target_pairs={{0,4},{4,8},{8,12},{1,5},{5,9},{9,13},{2,6},{6,10},{10,14},{3,7},{... | collective-permute-start | bytes 3538952 | tf_op jit(solution)/shard_map/ppermute | solution.py:18
  345.3 2.3 copy-start.14
  414.2 24.8 %collective-permute-start.14 = (bf16[768,640]{1,0:T(8,128)(2,1)S(1)}, bf16[768,640]{1,0:T(8,128)(2,1)}, u32[]{:S(2)}, u32[]{:S(2)}) collective-permute-start(bf16[768,640]{1,0:T(8,128)(2,1)S(1)} %get-tuple-element.22), channel_id=1, source_target_pairs={{0,16},{16,0},{1,17},{17,1},{2,18},{18,2},{3,19},{19,3},{4,20},{20... | collective-permute-start | bytes 2949128 | tf_op jit(solution)/shard_map/ppermute | solution.py:112
  415.7 44.3 %collective-permute-start.13 = (bf16[768,640]{1,0:T(8,128)(2,1)S(1)}, bf16[768,640]{1,0:T(8,128)(2,1)}, u32[]{:S(2)}, u32[]{:S(2)}) collective-permute-start(bf16[768,640]{1,0:T(8,128)(2,1)S(1)} %get-tuple-element.23), channel_id=1, source_target_pairs={{0,16},{16,0},{1,17},{17,1},{2,18},{18,2},{3,19},{19,3},{4,20},{20... | collective-permute-start | bytes 2949128 | tf_op jit(solution)/shard_map/ppermute | solution.py:112
  416.3 62.4 %collective-permute-start.15 = (bf16[768,640]{1,0:T(8,128)(2,1)S(1)}, bf16[768,640]{1,0:T(8,128)(2,1)}, u32[]{:S(2)}, u32[]{:S(2)}) collective-permute-start(bf16[768,640]{1,0:T(8,128)(2,1)S(1)} %get-tuple-element.21), channel_id=1, source_target_pairs={{0,16},{16,0},{1,17},{17,1},{2,18},{18,2},{3,19},{19,3},{4,20},{20... | collective-permute-start | bytes 2949128 | tf_op jit(solution)/shard_map/ppermute | solution.py:112
  451.2 11.4 %copy-start.12 = (bf16[768,3072]{1,0:T(8,128)(2,1)S(1)}, bf16[768,3072]{1,0:T(8,128)(2,1)}, u32[]{:S(2)}) copy-start(bf16[768,3072]{1,0:T(8,128)(2,1)} %all-gather.14.cloned.1.call-done) | copy-start | bytes 14155780
  453.9 8.7 %copy-start.9 = (bf16[768,640]{1,0:T(8,128)(2,1)S(1)}, bf16[768,640]{1,0:T(8,128)(2,1)}, u32[]{:S(2)}) copy-start(bf16[768,640]{1,0:T(8,128)(2,1)} %get-tuple-element.20) | copy-start | bytes 2949124
  462.6 2.1 copy-start.4
  481.0 6.1 %copy-start.1 = (bf16[1280,768]{1,0:T(8,128)(2,1)S(1)}, bf16[1280,768]{1,0:T(8,128)(2,1)}, u32[]{:S(2)}) copy-start(bf16[1280,768]{1,0:T(8,128)(2,1)} %param.11) | copy-start | bytes 5898244
Sparse Core Ops, SparseCore 0:
  9.1 79.1 all-gather.7
  89.9 74.9 all-gather.5
  166.4 74.9 all-gather.9
  242.8 74.9 all-gather.11
  412.2 38.9 all-gather.13

commit v7 on v6

--- a/solution.py
+++ b/solution.py
@@ -30,8 +30,8 @@
     tiles = q_ref.shape[0] // TILE
     picks = kb_ref.shape[1]
     scale = 1.0 / math.sqrt(HEAD_DIM)
-    lanes = lax.broadcasted_iota(jnp.int32, (TILE, TILE), 1)
-    rows = lax.broadcasted_iota(jnp.int32, (TILE, TILE), 0)
+    lanes = lax.broadcasted_iota(jnp.int32, (1, TILE), 1)
+    rows = lax.broadcasted_iota(jnp.int32, (TILE, 1), 0)
 
     def one_tile(i, carry):
         start = pl.multiple_of(i * TILE, TILE)
@@ -55,11 +55,12 @@
         total = jnp.sum(expo[0], axis=1, keepdims=True)
         for e in expo[1:]:
             total = total + jnp.sum(e, axis=1, keepdims=True)
+        inverse = 1.0 / total
         acc = None
         for j in range(picks):
             b = kb_ref[i, j]
             v = v_ref[pl.ds(pl.multiple_of(b * TILE, TILE), TILE), :]
-            w = (expo[j] / total).astype(jnp.bfloat16)
+            w = (expo[j] * inverse).astype(jnp.bfloat16)
             part = jnp.dot(w, v, preferred_element_type=jnp.float32)
             acc = part if acc is None else acc + part
         live = start + rows < lim_ref[1]
@@ -69,24 +70,25 @@
     lax.fori_loop(0, tiles, one_tile, 0)
 
 
-def attend(query, keys, values, blocks, limits, interpret=False):
+def attend(query, keys, values, blocks, limits, first=0, heads=None, interpret=False):
     rows, cols = query.shape
     window = keys.shape[0]
-    heads = cols // HEAD_DIM
+    if heads is None:
+        heads = cols // HEAD_DIM - first
     spec = pltpu.PrefetchScalarGridSpec(
         num_scalar_prefetch=2,
         grid=(heads,),
         in_specs=[
-            pl.BlockSpec((rows, HEAD_DIM), lambda h, kb, lim: (0, h)),
-            pl.BlockSpec((window, HEAD_DIM), lambda h, kb, lim: (0, h)),
-            pl.BlockSpec((window, HEAD_DIM), lambda h, kb, lim: (0, h)),
+            pl.BlockSpec((rows, HEAD_DIM), lambda h, kb, lim: (0, h + first)),
+            pl.BlockSpec((window, HEAD_DIM), lambda h, kb, lim: (0, h + first)),
+            pl.BlockSpec((window, HEAD_DIM), lambda h, kb, lim: (0, h + first)),
         ],
         out_specs=pl.BlockSpec((rows, HEAD_DIM), lambda h, kb, lim: (0, h)),
     )
     return pl.pallas_call(
         attend_kernel,
         grid_spec=spec,
-        out_shape=jax.ShapeDtypeStruct((rows, cols), jnp.bfloat16),
+        out_shape=jax.ShapeDtypeStruct((rows, heads * HEAD_DIM), jnp.bfloat16),
         interpret=interpret,
     )(blocks.astype(jnp.int32), limits.astype(jnp.int32), query, keys, values)
 
@@ -148,8 +150,14 @@
     zero = jnp.zeros((1,), jnp.int32)
     count_pad = jnp.concatenate([zero, slab_counts, zero], axis=0)
     limits = lax.dynamic_slice_in_dim(count_pad, position, 3, 0)
-    attended = attend(query, key_window, value_window, key_blocks, limits)
-    whole = lax.all_gather(attended, "wshard", axis=1, tiled=True)
+    heads = query.shape[1] // HEAD_DIM
+    split = heads // 2
+    groups = []
+    for first, count in ((0, split), (split, heads - split)):
+        part = attend(query, key_window, value_window, key_blocks, limits, first, count)
+        groups.append(lax.all_gather(part, "wshard", axis=1, tiled=False))
+    rows = query.shape[0]
+    whole = jnp.concatenate(groups, axis=2).reshape(rows, -1)
     mixed = split_dot(whole, o_rows)
     return mixed.astype(jnp.bfloat16)
 

time: 495 us -> 518 us (1.046)
  local copies, waits for them, and re-layouts: 32.3 us -> 53.9 us
    ppermute x12, waiting for transfers between devices: 99 us -> 82.7 us  [trade(): recv.append(lax.ppermute(part, 'clips', [(0, 1), (1, 0)]))]
    all_gather x0 -> x2, local copies, waits for them, and re-layouts: none -> 9.52 us  [layer(): groups.append(lax.all_gather(part, 'wshard', axis=1, tiled=False))]
    all_gather x1 -> x2, waiting for transfers between devices: 12.2 us -> 21.2 us  [layer(): groups.append(lax.all_gather(part, 'wshard', axis=1, tiled=False))]
    unnamed x36 -> x39, local copies, waits for them, and re-layouts: 2.57 us -> 9.52 us
    ppermute x4, waiting for transfers between devices: 20.1 us -> 25.7 us  [shifted(): return lax.ppermute(value, axis, pairs)]
    pallas_call x1 -> x2, Pallas kernels: 34.9 us -> 37.7 us  [attend(): pl.pallas_call(attend_kernel, grid_spec=spec, out_shape=jax.ShapeDtypeStr...]
  transfers between devices with their start and end apart: 21 -> 22, of which waited for: 12 -> 9; matrix products, arithmetic and copies ran while one was open for 19% -> 22% of each run, Pallas kernels for 0% -> 4%
where the time goes in v7:
time: 518 us; the launch traced here: 513 us
  waiting for transfers between devices  307 us (59%)
  matrix products  59.2 us (11%)
  local copies, waits for them, and re-layouts  53.9 us (10%)
  Pallas kernels  37.7 us (7%)
  starting transfers between devices  28.1 us (5%)
  between operations  14.3 us (3%)
  other arithmetic  12.4 us (2%)
    all_gather x4, waiting for transfers between devices, fetch(): return (lax.all_gather(mine, 'frames', axis=0, tiled=True), other)  178 us
    ppermute x12, waiting for transfers between devices, trade(): recv.append(lax.ppermute(part, 'clips', [(0, 1), (1, 0)]))  82.7 us
    pallas_call x2, Pallas kernels, attend(): pl.pallas_call(attend_kernel, grid_spec=spec, out_shape=jax.ShapeDtypeStr...  37.7 us
    dot_general x12, matrix products, split_dot(): jnp.dot(lax.dynamic_slice_in_dim(x, at * rows, rows, 1), part, preferred_...  27.4 us
    ppermute x4, waiting for transfers between devices, shifted(): return lax.ppermute(value, axis, pairs)  25.7 us
    dot_general x4, matrix products, split_dot(): own = jnp.dot(x, got, preferred_element_type=jnp.float32)  21.5 us
    all_gather x2, waiting for transfers between devices, layer(): groups.append(lax.all_gather(part, 'wshard', axis=1, tiled=False))  21.2 us
    ppermute x12, starting transfers between devices, trade(): recv.append(lax.ppermute(part, 'clips', [(0, 1), (1, 0)]))  14.1 us
  transfers between devices with their start and end apart: 22, of which 9 were waited for; matrix products, arithmetic and copies ran while one was open for 22% of the time, Pallas kernels for 4%

profile of v7, /device:TPU:0, one launch (start us, length us, event | category | flops | bytes accessed | tf_op | source)
XLA Modules:
  0.0 512.9 jit_solution(12934127490449137376)
XLA Ops:
  6.5 2.4 constant_dynamic-slice_fusion.13
  9.1 1.1 constant_dynamic-slice_fusion.17
  10.2 3.0 constant_dynamic-slice_fusion.8
  13.2 2.9 constant_dynamic-slice_fusion.3
  16.3 3.7 fusion.24
  20.0 2.8 fusion.22
  23.6 64.7 %all-gather.11.cloned.1.call-done = bf16[5120,384]{1,0:T(8,128)(2,1)} async-done(((bf16[1280,384]{1,0:T(8,128)(2,1)}), bf16[5120,384]{1,0:T(8,128)(2,1)}) %all-gather.11.cloned.1.call-update) | async-done | bytes 3932176 | tf_op jit(solution)/shard_map/all_gather | solution.py:102
  88.3 3.5 constant_dynamic-slice_fusion.12
  91.8 1.5 collective-permute-start.3
  93.8 71.0 %all-gather.9.cloned.1.call-done = bf16[5120,384]{1,0:T(8,128)(2,1)} async-done(((bf16[1280,384]{1,0:T(8,128)(2,1)}), bf16[5120,384]{1,0:T(8,128)(2,1)}) %all-gather.9.cloned.1.call-update) | async-done | bytes 3932176 | tf_op jit(solution)/shard_map/all_gather | solution.py:102
  164.8 2.2 constant_dynamic-slice_fusion.16
  167.1 1.5 collective-permute-start
  169.2 1.5 collective-permute-start.1
  170.7 7.4 %fusion.83 = f32[384,768]{1,0:T(8,128)S(1)} fusion(bf16[5120,384]{1,0:T(8,128)(2,1)S(1)} %copy-done.7, bf16[768,5120]{1,0:T(8,128)(2,1)} %param.9), kind=kOutput, calls=%fused_computation.101 | convolution fusion | flops 3019898880 | bytes 12976128 | tf_op jit(solution)/shard_map/dot_general | solution.py:123
  178.1 5.0 convolution_bitcast_fusion
  183.1 29.7 %collective-permute-done.2 = bf16[1280,384]{1,0:T(8,128)(2,1)S(1)} collective-permute-done((bf16[1280,384]{1,0:T(8,128)(2,1)S(1)}, bf16[1280,384]{1,0:T(8,128)(2,1)S(1)}, u32[]{:S(2)}, u32[]{:S(2)}) %collective-permute-start.2) | collective-permute-done | bytes 983072 | tf_op jit(solution)/shard_map/ppermute | solution.py:114
  212.8 1.5 collective-permute-start.4
  215.4 18.5 %collective-permute-done.1 = bf16[1280,384]{1,0:T(8,128)(2,1)S(1)} collective-permute-done((bf16[1280,384]{1,0:T(8,128)(2,1)S(1)}, bf16[1280,384]{1,0:T(8,128)(2,1)S(1)}, u32[]{:S(2)}, u32[]{:S(2)}) %collective-permute-start.1) | collective-permute-done | bytes 983072 | tf_op jit(solution)/shard_map/ppermute | solution.py:114
  234.9 1.2 fusion.46
  236.6 2.0 copy.24
  238.7 3.0 fusion.4
  241.7 12.1 %collective-permute-done.4 = bf16[1280,384]{1,0:T(8,128)(2,1)} collective-permute-done((bf16[1280,384]{1,0:T(8,128)(2,1)}, bf16[1280,384]{1,0:T(8,128)(2,1)}, u32[]{:S(2)}, u32[]{:S(2)}) %collective-permute-start.4) | collective-permute-done | bytes 983072 | tf_op jit(solution)/shard_map/ppermute | solution.py:114
  253.8 3.0 fusion.10
  256.8 3.1 fusion.49
  260.0 1.3 fusion.1
  262.1 1.3 multiply_convert_fusion.1
  263.3 3.2 constant_dynamic-slice_fusion.7
  266.5 1.5 collective-permute-start.6
  268.5 1.5 collective-permute-start.7
  270.0 5.8 %fusion.84 = f32[384,768]{1,0:T(8,128)S(1)} fusion(bf16[5120,384]{1,0:T(8,128)(2,1)S(1)} %copy-done.5, bf16[768,5120]{1,0:T(8,128)(2,1)} %param.9), kind=kOutput, calls=%fused_computation.102 | convolution fusion | flops 3019898880 | bytes 12976128 | tf_op jit(solution)/shard_map/dot_general | solution.py:123
  275.8 42.0 %all-gather.15.cloned.1.call-done = bf16[3072,640]{1,0:T(8,128)(2,1)} async-done(((bf16[768,640]{1,0:T(8,128)(2,1)}), bf16[3072,640]{1,0:T(8,128)(2,1)}) %all-gather.15.cloned.1.call-update) | async-done | bytes 3932176 | tf_op jit(solution)/shard_map/all_gather | solution.py:102
  317.8 1.3 collective-permute-start.10
  319.1 5.6 %collective-permute-start.9 = (bf16[768,768]{1,0:T(8,128)(2,1)}, bf16[768,768]{1,0:T(8,128)(2,1)}, u32[]{:S(2)}, u32[]{:S(2)}) collective-permute-start(bf16[768,768]{1,0:T(8,128)(2,1)} %multiply_convert_fusion.1), channel_id=1, source_target_pairs={{0,4},{4,8},{8,12},{1,5},{5,9},{9,13},{2,6},{6,10},{10,14},{3,7},{... | collective-permute-start | bytes 3538952 | tf_op jit(solution)/shard_map/ppermute | solution.py:18
  324.7 2.8 fusion.20
  327.5 1.3 collective-permute-start.12
  328.8 2.8 fusion.2
  331.6 5.7 %collective-permute-start.11 = (bf16[768,768]{1,0:T(8,128)(2,1)}, bf16[768,768]{1,0:T(8,128)(2,1)}, u32[]{:S(2)}, u32[]{:S(2)}) collective-permute-start(bf16[768,768]{1,0:T(8,128)(2,1)} %fusion.1), channel_id=1, source_target_pairs={{0,4},{4,8},{8,12},{1,5},{5,9},{9,13},{2,6},{6,10},{10,14},{3,7},{... | collective-permute-start | bytes 3538952 | tf_op jit(solution)/shard_map/ppermute | solution.py:18
  337.3 2.8 fusion.8
  340.1 2.9 fusion.52
  343.5 2.0 copy.30
  345.5 2.9 multiply_convert_fusion.q_ref
  348.3 25.7 %collective-permute-done.11 = bf16[768,768]{1,0:T(8,128)(2,1)} collective-permute-done((bf16[768,768]{1,0:T(8,128)(2,1)}, bf16[768,768]{1,0:T(8,128)(2,1)}, u32[]{:S(2)}, u32[]{:S(2)}) %collective-permute-start.11) | collective-permute-done | bytes 1179680 | tf_op jit(solution)/shard_map/ppermute | solution.py:18
  374.0 1.3 constant_dynamic-update-slice_fusion.5
  375.4 1.3 constant_dynamic-update-slice_fusion.4
  376.7 2.5 constant_dynamic-update-slice_fusion.2
  379.2 2.4 constant_dynamic-update-slice_fusion.1
  381.5 1.3 constant_dynamic-update-slice_fusion.3.v_ref
  382.9 3.3 constant_dynamic-update-slice_fusion.k_ref
  386.2 18.8 %shard_map.91 = bf16[768,384]{1,0:T(8,128)(2,1)} custom-call(s32[6,8]{1,0:T(8,128)} %kb_ref.3, s32[3]{0:T(128)} %dynamic_slice.95.lim_ref, bf16[768,768]{1,0:T(8,128)(2,1)} %multiply_convert_fusion.q_ref, bf16[2304,768]{1,0:T(8,128)(2,1)} %constant_dynamic-update-slice_fusion.k_ref, bf16[2304,768]{1,0:T(8,128)(2,1)} %copy-done.2), custom_call_target="tpu_custom_call" | custom-call | tf_op jit(solution)/shard_map/pallas_call | solution.py:88
  405.1 18.8 %shard_map.92 = bf16[768,384]{1,0:T(8,128)(2,1)} custom-call(s32[6,8]{1,0:T(8,128)} %kb_ref.3, s32[3]{0:T(128)} %dynamic_slice.95.lim_ref, bf16[768,768]{1,0:T(8,128)(2,1)} %multiply_convert_fusion.q_ref, bf16[2304,768]{1,0:T(8,128)(2,1)} %constant_dynamic-update-slice_fusion.k_ref, bf16[2304,768]{1,0:T(8,128)(2,1)} %copy-done.2), custom_call_target="tpu_custom_call" | custom-call | tf_op jit(solution)/shard_map/pallas_call | solution.py:88
  424.0 3.3 constant_dynamic-slice_fusion
  427.3 1.5 collective-permute-start.14
  429.3 1.5 collective-permute-start.13
  430.8 4.1 reshape.46
  435.0 21.2 %all-gather.19.cloned.1.call-done = bf16[768,1536]{1,0:T(8,128)(2,1)} async-done(((bf16[768,384]{1,0:T(8,128)(2,1)}), bf16[768,1536]{1,0:T(8,128)(2,1)}) %all-gather.19.cloned.1.call-update) | async-done | bytes 2359312 | tf_op jit(solution)/shard_map/all_gather | solution.py:158
  456.2 5.4 %reshape.47 = bf16[768,4,384]{2,1,0:T(4,128)(2,1)} reshape(bf16[768,1536]{1,0:T(8,128)(2,1)} %all-gather.19.cloned.1.call-done) | data formatting | bytes 4718592 | tf_op jit(solution)/shard_map/all_gather | solution.py:158
  461.5 3.8 pad_maximum_fusion
  467.5 2.2 fusion.59
  469.8 22.2 %collective-permute-done.13 = bf16[768,640]{1,0:T(8,128)(2,1)} collective-permute-done((bf16[768,640]{1,0:T(8,128)(2,1)}, bf16[768,640]{1,0:T(8,128)(2,1)}, u32[]{:S(2)}, u32[]{:S(2)}) %collective-permute-start.13) | collective-permute-done | bytes 983072 | tf_op jit(solution)/shard_map/ppermute | solution.py:114
  492.0 2.2 fusion.61
  494.2 3.3 fusion.85
  497.5 2.3 add_add_fusion
  499.8 2.1 fusion
  501.9 4.0 copy.31
  (76 shorter events, 9.3 us)
Async XLA Ops:
  6.5 2.5 copy-start
  6.5 81.8 %all-gather.11.cloned.1.call-start = ((), (), s32[]{:S(2)}) async-start(), calls=%async_computation.1 | async-start | bytes 4915200 | tf_op jit(solution)/shard_map/all_gather | solution.py:102
  9.0 155.8 %all-gather.9.cloned.1.call-start = ((), (), s32[]{:S(2)}) async-start(), calls=%async_computation | async-start | bytes 4915200 | tf_op jit(solution)/shard_map/all_gather | solution.py:102
  10.1 253.2 %all-gather.13.cloned.1.call-start = ((), (), s32[]{:S(2)}) async-start(), calls=%async_computation.2 | async-start | bytes 4915200 | tf_op jit(solution)/shard_map/all_gather | solution.py:102
  13.2 304.6 %all-gather.15.cloned.1.call-start = ((), (), s32[]{:S(2)}) async-start(), calls=%async_computation.3 | async-start | bytes 4915200 | tf_op jit(solution)/shard_map/all_gather | solution.py:102
  16.2 414.6 %all-gather.17.cloned.1.call-start = ((), (), s32[]{:S(2)}) async-start(), calls=%async_computation.4 | async-start | bytes 2949120 | tf_op jit(solution)/shard_map/all_gather | solution.py:158
  16.3 3.7 copy-start.11
  20.0 2.9 copy-start.14
  91.8 165.0 %collective-permute-start.3 = (bf16[1280,384]{1,0:T(8,128)(2,1)}, bf16[1280,384]{1,0:T(8,128)(2,1)}, u32[]{:S(2)}, u32[]{:S(2)}) collective-permute-start(bf16[1280,384]{1,0:T(8,128)(2,1)} %get-tuple-element.27), channel_id=1, source_target_pairs={{0,16},{16,0},{1,17},{17,1},{2,18},{18,2},{3,19},{19,3},{4,20},{20... | collective-permute-start | bytes 2949128 | tf_op jit(solution)/shard_map/ppermute | solution.py:114
  93.3 145.4 %collective-permute-start.5 = (bf16[1280,384]{1,0:T(8,128)(2,1)}, bf16[1280,384]{1,0:T(8,128)(2,1)}, u32[]{:S(2)}, u32[]{:S(2)}) collective-permute-start(bf16[1280,384]{1,0:T(8,128)(2,1)} %get-tuple-element.28), channel_id=1, source_target_pairs={{0,16},{16,0},{1,17},{17,1},{2,18},{18,2},{3,19},{19,3},{4,20},{20... | collective-permute-start | bytes 2949128 | tf_op jit(solution)/shard_map/ppermute | solution.py:114
  164.8 5.8 %copy-start.7 = (bf16[5120,384]{1,0:T(8,128)(2,1)S(1)}, bf16[5120,384]{1,0:T(8,128)(2,1)}, u32[]{:S(2)}) copy-start(bf16[5120,384]{1,0:T(8,128)(2,1)} %all-gather.9.cloned.1.call-done) | copy-start | bytes 11796484
  167.1 67.8 %collective-permute-start = (bf16[1280,384]{1,0:T(8,128)(2,1)S(1)}, bf16[1280,384]{1,0:T(8,128)(2,1)S(1)}, u32[]{:S(2)}, u32[]{:S(2)}) collective-permute-start(bf16[1280,384]{1,0:T(8,128)(2,1)S(1)} %get-tuple-element.30), channel_id=1, source_target_pairs={{0,16},{16,0},{1,17},{17,1},{2,18},{18,2},{3,19},{19,3},{4,20},{20... | collective-permute-start | bytes 2949128 | tf_op jit(solution)/shard_map/ppermute | solution.py:114
  168.6 44.2 %collective-permute-start.2 = (bf16[1280,384]{1,0:T(8,128)(2,1)S(1)}, bf16[1280,384]{1,0:T(8,128)(2,1)S(1)}, u32[]{:S(2)}, u32[]{:S(2)}) collective-permute-start(bf16[1280,384]{1,0:T(8,128)(2,1)S(1)} %get-tuple-element.31), channel_id=1, source_target_pairs={{0,16},{16,0},{1,17},{17,1},{2,18},{18,2},{3,19},{19,3},{4,20},{20... | collective-permute-start | bytes 2949128 | tf_op jit(solution)/shard_map/ppermute | solution.py:114
  169.2 8.9 %slice-start = ((s8[7864320]{0:T(1024)(128)(4,1)}), s8[4194304]{0:T(1024)(128)(4,1)S(1)}, s32[]{:S(2)}) async-start(s8[7864320]{0:T(1024)(128)(4,1)} %bitcast.52), calls=%async_computation.6 | async-start | bytes 8388608
  169.2 8.9 %slice-start.1 = ((s8[7864320]{0:T(1024)(128)(4,1)}), s8[3670016]{0:T(1024)(128)(4,1)S(1)}, s32[]{:S(2)}) async-start(s8[7864320]{0:T(1024)(128)(4,1)} %bitcast.52), calls=%async_computation.7 | async-start | bytes 7340032
  169.2 8.9 %copy-start.6 = (bf16[5120,384]{1,0:T(8,128)(2,1)S(1)}, bf16[5120,384]{1,0:T(8,128)(2,1)}, u32[]{:S(2)}) copy-start(bf16[5120,384]{1,0:T(8,128)(2,1)} %all-gather.11.cloned.1.call-done) | copy-start | bytes 11796484
  169.2 64.7 %collective-permute-start.1 = (bf16[1280,384]{1,0:T(8,128)(2,1)S(1)}, bf16[1280,384]{1,0:T(8,128)(2,1)S(1)}, u32[]{:S(2)}, u32[]{:S(2)}) collective-permute-start(bf16[1280,384]{1,0:T(8,128)(2,1)S(1)} %get-tuple-element.32), channel_id=1, source_target_pairs={{0,16},{16,0},{1,17},{17,1},{2,18},{18,2},{3,19},{19,3},{4,20},{20... | collective-permute-start | bytes 2949128 | tf_op jit(solution)/shard_map/ppermute | solution.py:114
  212.8 41.0 %collective-permute-start.4 = (bf16[1280,384]{1,0:T(8,128)(2,1)}, bf16[1280,384]{1,0:T(8,128)(2,1)}, u32[]{:S(2)}, u32[]{:S(2)}) collective-permute-start(bf16[1280,384]{1,0:T(8,128)(2,1)} %get-tuple-element.29), channel_id=1, source_target_pairs={{0,16},{16,0},{1,17},{17,1},{2,18},{18,2},{3,19},{19,3},{4,20},{20... | collective-permute-start | bytes 2949128 | tf_op jit(solution)/shard_map/ppermute | solution.py:114
  215.3 19.6 %copy-start.8 = (f32[768,384]{0,1:T(8,128)S(1)}, f32[768,384]{0,1:T(8,128)}, u32[]{:S(2)}) copy-start(f32[768,384]{0,1:T(8,128)} %fusion.24) | copy-start | bytes 3538948
  256.8 3.2 copy-start.10
  256.8 4.5 copy-start.12
  260.0 2.1 copy-start.3
  263.3 6.7 %copy-start.5 = (bf16[5120,384]{1,0:T(8,128)(2,1)S(1)}, bf16[5120,384]{1,0:T(8,128)(2,1)}, u32[]{:S(2)}) copy-start(bf16[5120,384]{1,0:T(8,128)(2,1)} %all-gather.13.cloned.1.call-done) | copy-start | bytes 11796484
  266.5 73.6 %collective-permute-start.6 = (bf16[1280,384]{1,0:T(8,128)(2,1)S(1)}, bf16[1280,384]{1,0:T(8,128)(2,1)}, u32[]{:S(2)}, u32[]{:S(2)}) collective-permute-start(bf16[1280,384]{1,0:T(8,128)(2,1)S(1)} %get-tuple-element.24), channel_id=1, source_target_pairs={{0,16},{16,0},{1,17},{17,1},{2,18},{18,2},{3,19},{19,3},{4,20},{20... | collective-permute-start | bytes 2949128 | tf_op jit(solution)/shard_map/ppermute | solution.py:114
  268.0 59.5 %collective-permute-start.8 = (bf16[1280,384]{1,0:T(8,128)(2,1)}, bf16[1280,384]{1,0:T(8,128)(2,1)}, u32[]{:S(2)}, u32[]{:S(2)}) collective-permute-start(bf16[1280,384]{1,0:T(8,128)(2,1)} %get-tuple-element.25), channel_id=1, source_target_pairs={{0,16},{16,0},{1,17},{17,1},{2,18},{18,2},{3,19},{19,3},{4,20},{20... | collective-permute-start | bytes 2949128 | tf_op jit(solution)/shard_map/ppermute | solution.py:114
  268.5 63.1 %collective-permute-start.7 = (bf16[1280,384]{1,0:T(8,128)(2,1)S(1)}, bf16[1280,384]{1,0:T(8,128)(2,1)}, u32[]{:S(2)}, u32[]{:S(2)}) collective-permute-start(bf16[1280,384]{1,0:T(8,128)(2,1)S(1)} %get-tuple-element.26), channel_id=1, source_target_pairs={{0,16},{16,0},{1,17},{17,1},{2,18},{18,2},{3,19},{19,3},{4,20},{20... | collective-permute-start | bytes 2949128 | tf_op jit(solution)/shard_map/ppermute | solution.py:114
  317.8 65.1 %collective-permute-start.10 = (bf16[768,768]{1,0:T(8,128)(2,1)}, bf16[768,768]{1,0:T(8,128)(2,1)}, u32[]{:S(2)}, u32[]{:S(2)}) collective-permute-start(bf16[768,768]{1,0:T(8,128)(2,1)} %multiply_convert_fusion.1), channel_id=1, source_target_pairs={{4,0},{8,4},{12,8},{5,1},{9,5},{13,9},{6,2},{10,6},{14,10},{7,3},{... | collective-permute-start | bytes 3538952 | tf_op jit(solution)/shard_map/ppermute | solution.py:18
  319.1 57.6 %collective-permute-start.9 = (bf16[768,768]{1,0:T(8,128)(2,1)}, bf16[768,768]{1,0:T(8,128)(2,1)}, u32[]{:S(2)}, u32[]{:S(2)}) collective-permute-start(bf16[768,768]{1,0:T(8,128)(2,1)} %multiply_convert_fusion.1), channel_id=1, source_target_pairs={{0,4},{4,8},{8,12},{1,5},{5,9},{9,13},{2,6},{6,10},{10,14},{3,7},{... | collective-permute-start | bytes 3538952 | tf_op jit(solution)/shard_map/ppermute | solution.py:18
  327.5 54.0 %collective-permute-start.12 = (bf16[768,768]{1,0:T(8,128)(2,1)}, bf16[768,768]{1,0:T(8,128)(2,1)}, u32[]{:S(2)}, u32[]{:S(2)}) collective-permute-start(bf16[768,768]{1,0:T(8,128)(2,1)} %fusion.1), channel_id=1, source_target_pairs={{4,0},{8,4},{12,8},{5,1},{9,5},{13,9},{6,2},{10,6},{14,10},{7,3},{... | collective-permute-start | bytes 3538952 | tf_op jit(solution)/shard_map/ppermute | solution.py:18
  331.6 42.4 %collective-permute-start.11 = (bf16[768,768]{1,0:T(8,128)(2,1)}, bf16[768,768]{1,0:T(8,128)(2,1)}, u32[]{:S(2)}, u32[]{:S(2)}) collective-permute-start(bf16[768,768]{1,0:T(8,128)(2,1)} %fusion.1), channel_id=1, source_target_pairs={{0,4},{4,8},{8,12},{1,5},{5,9},{9,13},{2,6},{6,10},{10,14},{3,7},{... | collective-permute-start | bytes 3538952 | tf_op jit(solution)/shard_map/ppermute | solution.py:18
  343.5 2.0 copy-start.13
  382.9 3.3 copy-start.2
  405.0 51.1 %all-gather.19.cloned.1.call-start = ((), (), s32[]{:S(2)}) async-start(), calls=%async_computation.5 | async-start | bytes 2949120 | tf_op jit(solution)/shard_map/all_gather | solution.py:158
  427.3 40.2 %collective-permute-start.14 = (bf16[768,640]{1,0:T(8,128)(2,1)}, bf16[768,640]{1,0:T(8,128)(2,1)}, u32[]{:S(2)}, u32[]{:S(2)}) collective-permute-start(bf16[768,640]{1,0:T(8,128)(2,1)} %get-tuple-element.22), channel_id=1, source_target_pairs={{0,16},{16,0},{1,17},{17,1},{2,18},{18,2},{3,19},{19,3},{4,20},{20... | collective-permute-start | bytes 2949128 | tf_op jit(solution)/shard_map/ppermute | solution.py:114
  428.8 68.7 %collective-permute-start.15 = (bf16[768,640]{1,0:T(8,128)(2,1)S(1)}, bf16[768,640]{1,0:T(8,128)(2,1)}, u32[]{:S(2)}, u32[]{:S(2)}) collective-permute-start(bf16[768,640]{1,0:T(8,128)(2,1)S(1)} %get-tuple-element.21), channel_id=1, source_target_pairs={{0,16},{16,0},{1,17},{17,1},{2,18},{18,2},{3,19},{19,3},{4,20},{20... | collective-permute-start | bytes 2949128 | tf_op jit(solution)/shard_map/ppermute | solution.py:114
  429.3 62.7 %collective-permute-start.13 = (bf16[768,640]{1,0:T(8,128)(2,1)}, bf16[768,640]{1,0:T(8,128)(2,1)}, u32[]{:S(2)}, u32[]{:S(2)}) collective-permute-start(bf16[768,640]{1,0:T(8,128)(2,1)} %get-tuple-element.23), channel_id=1, source_target_pairs={{0,16},{16,0},{1,17},{17,1},{2,18},{18,2},{3,19},{19,3},{4,20},{20... | collective-permute-start | bytes 2949128 | tf_op jit(solution)/shard_map/ppermute | solution.py:114
  465.3 1.2 copy-start.9
  469.8 24.5 %copy-start.4 = (bf16[3072,640]{1,0:T(8,128)(2,1)S(1)}, bf16[3072,640]{1,0:T(8,128)(2,1)}, u32[]{:S(2)}) copy-start(bf16[3072,640]{1,0:T(8,128)(2,1)} %all-gather.15.cloned.1.call-done) | copy-start | bytes 11796484
  499.8 6.1 %copy-start.1 = (bf16[1280,768]{1,0:T(8,128)(2,1)S(1)}, bf16[1280,768]{1,0:T(8,128)(2,1)}, u32[]{:S(2)}) copy-start(bf16[1280,768]{1,0:T(8,128)(2,1)} %param.11) | copy-start | bytes 5898244
Sparse Core Ops, SparseCore 0:
  9.1 79.1 all-gather.10
  89.9 74.9 all-gather.8
  166.4 74.9 all-gather.12
  242.8 74.9 all-gather.14
  405.2 25.4 all-gather.16
  432.1 24.0 all-gather.18

commit v8 on v6

--- a/solution.py
+++ b/solution.py
@@ -134,22 +134,32 @@
     v_got = fetch(w_value)
     q_got = fetch(w_query)
     o_got = fetch(w_out)
-    keys = head_norm(split_dot(tokens, trade(k_got)), k_gain)
-    values = split_dot(tokens, trade(v_got)).astype(jnp.bfloat16)
-    keys, values, q_got = lax.optimization_barrier((keys, values, q_got))
-    query = head_norm(split_dot(tokens, trade(q_got)), q_gain)
+    k_rows = trade(k_got)
+    v_rows = trade(v_got)
+    q_rows = trade(q_got)
+    keys = head_norm(split_dot(tokens, k_rows), k_gain)
+    values = split_dot(tokens, v_rows).astype(jnp.bfloat16)
+    query = head_norm(split_dot(tokens, q_rows), q_gain)
     keys, values, o_got = lax.optimization_barrier((keys, values, o_got))
     o_rows = trade(o_got)
-    before = shifted((keys, values), "frames", 1)
-    after = shifted((keys, values), "frames", -1)
-    key_window = jnp.concatenate([before[0], keys, after[0]], axis=0)
-    value_window = jnp.concatenate([before[1], values, after[1]], axis=0)
     position = lax.axis_index("frames")
     zero = jnp.zeros((1,), jnp.int32)
     count_pad = jnp.concatenate([zero, slab_counts, zero], axis=0)
     limits = lax.dynamic_slice_in_dim(count_pad, position, 3, 0)
-    attended = attend(query, key_window, value_window, key_blocks, limits)
-    whole = lax.all_gather(attended, "wshard", axis=1, tiled=True)
+    heads = query.shape[1] // HEAD_DIM
+    split = heads // 2
+    groups = []
+    for lo, hi in ((0, split), (split, heads)):
+        cols = slice(lo * HEAD_DIM, hi * HEAD_DIM)
+        own = (keys[:, cols], values[:, cols])
+        before = shifted(own, "frames", 1)
+        after = shifted(own, "frames", -1)
+        key_window = jnp.concatenate([before[0], own[0], after[0]], axis=0)
+        value_window = jnp.concatenate([before[1], own[1], after[1]], axis=0)
+        part = attend(query[:, cols], key_window, value_window, key_blocks, limits)
+        groups.append(lax.all_gather(part, "wshard", axis=1, tiled=False))
+    rows = query.shape[0]
+    whole = jnp.concatenate(groups, axis=2).reshape(rows, -1)
     mixed = split_dot(whole, o_rows)
     return mixed.astype(jnp.bfloat16)
 

time: 495 us -> 527 us (1.065)
  local copies, waits for them, and re-layouts: 32.3 us -> 44.8 us
  matrix products: 59.6 us -> 67.5 us
  starting transfers between devices: 28.2 us -> 35.3 us
  waiting for transfers between devices: 309 us -> 303 us
    ppermute x12, waiting for transfers between devices: 99 us -> 49.6 us  [trade(): recv.append(lax.ppermute(part, 'clips', [(0, 1), (1, 0)]))]
    all_gather x4, waiting for transfers between devices: 178 us -> 222 us  [fetch(): return (lax.all_gather(mine, 'frames', axis=0, tiled=True), other)]
    all_gather x0 -> x2, local copies, waits for them, and re-layouts: none -> 9.6 us  [layer(): groups.append(lax.all_gather(part, 'wshard', axis=1, tiled=False))]
    ppermute x4 -> x8, starting transfers between devices: 13.9 us -> 21.8 us  [shifted(): return lax.ppermute(value, axis, pairs)]
    concatenate x2 -> x5, other arithmetic: 6.66 us -> 12.3 us  [the longest x2 4.34 us: layer(): value_window = jnp.concatenate([before[1], own[1], after[1]], axis=0)]
    ppermute x4 -> x8, waiting for transfers between devices: 20.1 us -> 16.6 us  [shifted(): return lax.ppermute(value, axis, pairs)]
    pallas_call x1 -> x2, Pallas kernels: 34.9 us -> 37.8 us  [attend(): pl.pallas_call(attend_kernel, grid_spec=spec, out_shape=jax.ShapeDtypeStr...]
    all_gather x1 -> x2, waiting for transfers between devices: 12.2 us -> 14.1 us  [layer(): groups.append(lax.all_gather(part, 'wshard', axis=1, tiled=False))]
  transfers between devices with their start and end apart: 21 -> 26, of which waited for: 12 -> 12; matrix products, arithmetic and copies ran while one was open for 19% -> 22% of each run, Pallas kernels for 0% -> 4%
where the time goes in v8:
time: 527 us; the launch traced here: 522 us
  waiting for transfers between devices  303 us (57%)
  matrix products  67.5 us (13%)
  local copies, waits for them, and re-layouts  44.8 us (9%)
  Pallas kernels  37.8 us (7%)
  starting transfers between devices  35.3 us (7%)
  other arithmetic  19.5 us (4%)
  between operations  14.3 us (3%)
    all_gather x4, waiting for transfers between devices, fetch(): return (lax.all_gather(mine, 'frames', axis=0, tiled=True), other)  222 us
    ppermute x12, waiting for transfers between devices, trade(): recv.append(lax.ppermute(part, 'clips', [(0, 1), (1, 0)]))  49.6 us
    pallas_call x2, Pallas kernels, attend(): pl.pallas_call(attend_kernel, grid_spec=spec, out_shape=jax.ShapeDtypeStr...  37.8 us
    dot_general x12, matrix products, split_dot(): jnp.dot(lax.dynamic_slice_in_dim(x, at * rows, rows, 1), part, preferred_...  31.1 us
    dot_general x4, matrix products, split_dot(): own = jnp.dot(x, got, preferred_element_type=jnp.float32)  25.3 us
    ppermute x8, starting transfers between devices, shifted(): return lax.ppermute(value, axis, pairs)  21.8 us
    ppermute x8, waiting for transfers between devices, shifted(): return lax.ppermute(value, axis, pairs)  16.6 us
    all_gather x2, waiting for transfers between devices, layer(): groups.append(lax.all_gather(part, 'wshard', axis=1, tiled=False))  14.1 us
  transfers between devices with their start and end apart: 26, of which 12 were waited for; matrix products, arithmetic and copies ran while one was open for 22% of the time, Pallas kernels for 4%

profile of v8, /device:TPU:0, one launch (start us, length us, event | category | flops | bytes accessed | tf_op | source)
XLA Modules:
  0.0 521.8 jit_solution(2347886280311724409)
XLA Ops:
  6.5 2.4 constant_dynamic-slice_fusion.8
  9.0 2.3 constant_dynamic-slice_fusion.12
  12.6 3.0 constant_dynamic-slice_fusion.3
  15.8 3.7 fusion.24
  19.5 2.8 fusion.22
  22.3 3.7 fusion.20
  26.7 61.5 %all-gather.13.cloned.1.call-done = bf16[5120,384]{1,0:T(8,128)(2,1)} async-done(((bf16[1280,384]{1,0:T(8,128)(2,1)}), bf16[5120,384]{1,0:T(8,128)(2,1)}) %all-gather.13.cloned.1.call-update) | async-done | bytes 3932176 | tf_op jit(solution)/shard_map/all_gather | solution.py:100
  88.3 3.5 constant_dynamic-slice_fusion.7
  91.8 1.5 collective-permute-start.6
  93.8 71.0 %all-gather.11.cloned.1.call-done = bf16[5120,384]{1,0:T(8,128)(2,1)} async-done(((bf16[1280,384]{1,0:T(8,128)(2,1)}), bf16[5120,384]{1,0:T(8,128)(2,1)}) %all-gather.11.cloned.1.call-update) | async-done | bytes 3932176 | tf_op jit(solution)/shard_map/all_gather | solution.py:100
  164.8 3.6 constant_dynamic-slice_fusion.11
  168.4 1.5 collective-permute-start.3
  170.4 1.5 collective-permute-start.4
  171.9 6.3 %fusion.88 = f32[384,768]{1,0:T(8,128)S(1)} fusion(bf16[5120,384]{1,0:T(8,128)(2,1)S(1)} %copy-done.8, bf16[768,5120]{1,0:T(8,128)(2,1)} %param.9), kind=kOutput, calls=%fused_computation.103 | convolution fusion | flops 3019898880 | bytes 12976128 | tf_op jit(solution)/shard_map/dot_general | solution.py:121
  178.3 63.1 %all-gather.9.cloned.1.call-done = bf16[5120,384]{1,0:T(8,128)(2,1)} async-done(((bf16[1280,384]{1,0:T(8,128)(2,1)}), bf16[5120,384]{1,0:T(8,128)(2,1)}) %all-gather.9.cloned.1.call-update) | async-done | bytes 3932176 | tf_op jit(solution)/shard_map/all_gather | solution.py:100
  241.4 7.8 %fusion.87 = f32[384,768]{1,0:T(8,128)S(1)} fusion(bf16[5120,384]{1,0:T(8,128)(2,1)} %all-gather.9.cloned.1.call-done, bf16[768,5120]{1,0:T(8,128)(2,1)} %param.9), kind=kOutput, calls=%fused_computation.102 | convolution fusion | flops 3019898880 | bytes 12976128 | tf_op jit(solution)/shard_map/dot_general | solution.py:121
  249.2 7.8 %convolution_bitcast_fusion = bf16[768,384]{1,0:T(8,128)(2,1)} fusion(bf16[768,5120]{1,0:T(8,128)(2,1)} %param.9, bf16[5120,384]{1,0:T(8,128)(2,1)S(1)} %copy-done.7), kind=kOutput, calls=%fused_computation.43 | convolution fusion | flops 3019898880 | bytes 12386304 | tf_op jit(solution)/shard_map/dot_general | solution.py:121
  257.1 1.7 constant_dynamic-slice_fusion.15
  258.7 1.5 collective-permute-start.7
  260.2 2.2 fusion.4
  263.1 2.2 fusion.10
  265.3 1.5 collective-permute-start.2
  266.8 2.3 fusion.49
  269.5 2.0 fusion.35
  271.5 2.1 copy.25
  274.2 3.0 fusion.2
  277.2 6.4 %collective-permute-done.7 = bf16[1280,384]{1,0:T(8,128)(2,1)} collective-permute-done((bf16[1280,384]{1,0:T(8,128)(2,1)}, bf16[1280,384]{1,0:T(8,128)(2,1)}, u32[]{:S(2)}, u32[]{:S(2)}) %collective-permute-start.7) | collective-permute-done | bytes 983072 | tf_op jit(solution)/shard_map/ppermute | solution.py:112
  283.7 3.0 fusion.8
  286.7 3.2 fusion.52
  291.3 26.5 %all-gather.15.cloned.1.call-done = bf16[3072,640]{1,0:T(8,128)(2,1)} async-done(((bf16[768,640]{1,0:T(8,128)(2,1)}), bf16[3072,640]{1,0:T(8,128)(2,1)}) %all-gather.15.cloned.1.call-update) | async-done | bytes 3932176 | tf_op jit(solution)/shard_map/all_gather | solution.py:100
  320.2 5.4 %collective-permute-start.9 = (bf16[768,384]{1,0:T(8,128)(2,1)}, bf16[768,384]{1,0:T(8,128)(2,1)}, u32[]{:S(2)}, u32[]{:S(2)}) collective-permute-start(bf16[768,384]{1,0:T(8,128)(2,1)} %get-tuple-element.29), channel_id=1, source_target_pairs={{0,4},{4,8},{8,12},{1,5},{5,9},{9,13},{2,6},{6,10},{10,14},{3,7},{... | collective-permute-start | bytes 1769480 | tf_op jit(solution)/shard_map/ppermute | solution.py:18
  328.0 2.8 fusion.6
  330.8 14.8 %collective-permute-done.1 = bf16[1280,384]{1,0:T(8,128)(2,1)} collective-permute-done((bf16[1280,384]{1,0:T(8,128)(2,1)}, bf16[1280,384]{1,0:T(8,128)(2,1)}, u32[]{:S(2)}, u32[]{:S(2)}) %collective-permute-start.1) | collective-permute-done | bytes 983072 | tf_op jit(solution)/shard_map/ppermute | solution.py:112
  345.6 2.1 collective-permute-start.11
  347.7 2.8 fusion.12
  350.5 2.9 fusion.46
  353.9 2.0 copy.24
  355.9 1.8 multiply_convert_fusion.1
  358.9 2.8 pad_maximum_fusion.1.k_ref
  361.7 2.9 pad_maximum_fusion.2.v_ref
  364.6 19.0 %shard_map.91 = bf16[768,384]{1,0:T(8,128)(2,1)} custom-call(s32[6,8]{1,0:T(8,128)} %kb_ref.3, s32[3]{0:T(128)} %dynamic_slice.95.lim_ref, bf16[768,384]{1,0:T(8,128)(2,1)} %get-tuple-element.31.q_ref, bf16[2304,384]{1,0:T(8,128)(2,1)} %pad_maximum_fusion.1.k_ref, bf16[2304,384]{1,0:T(8,128)(2,1)} %pad_maximum_fusion.2.v_ref), custom_call_target="tpu_custom_call" | custom-call | tf_op jit(solution)/shard_map/pallas_call | solution.py:86
  384.9 4.6 collective-permute-start.13
  389.5 1.3 collective-permute-start.16
  390.8 4.6 collective-permute-start.15
  395.4 6.3 %collective-permute-done.14 = bf16[768,384]{1,0:T(8,128)(2,1)S(1)} collective-permute-done((bf16[768,384]{1,0:T(8,128)(2,1)S(1)}, bf16[768,384]{1,0:T(8,128)(2,1)S(1)}, u32[]{:S(2)}, u32[]{:S(2)}) %collective-permute-start.14) | collective-permute-done | bytes 589856 | tf_op jit(solution)/shard_map/ppermute | solution.py:18
  401.7 1.5 collective-permute-done.13
  403.2 1.4 pad_maximum_fusion.3.k_ref
  404.6 7.7 %collective-permute-done.16 = bf16[768,384]{1,0:T(8,128)(2,1)S(1)} collective-permute-done((bf16[768,384]{1,0:T(8,128)(2,1)S(1)}, bf16[768,384]{1,0:T(8,128)(2,1)S(1)}, u32[]{:S(2)}, u32[]{:S(2)}) %collective-permute-start.16) | collective-permute-done | bytes 589856 | tf_op jit(solution)/shard_map/ppermute | solution.py:18
  413.4 1.5 pad_maximum_fusion.4.v_ref
  414.9 18.8 %shard_map.92 = bf16[768,384]{1,0:T(8,128)(2,1)} custom-call(s32[6,8]{1,0:T(8,128)} %kb_ref.3, s32[3]{0:T(128)} %dynamic_slice.95.lim_ref, bf16[768,384]{1,0:T(8,128)(2,1)} %get-tuple-element.32.q_ref, bf16[2304,384]{1,0:T(8,128)(2,1)} %pad_maximum_fusion.3.k_ref, bf16[2304,384]{1,0:T(8,128)(2,1)} %pad_maximum_fusion.4.v_ref), custom_call_target="tpu_custom_call" | custom-call | tf_op jit(solution)/shard_map/pallas_call | solution.py:86
  433.8 3.3 constant_dynamic-slice_fusion
  437.1 1.5 collective-permute-start.18
  439.1 1.5 collective-permute-start.17
  440.7 4.2 reshape.46
  444.9 14.1 %all-gather.19.cloned.1.call-done = bf16[768,1536]{1,0:T(8,128)(2,1)} async-done(((bf16[768,384]{1,0:T(8,128)(2,1)}), bf16[768,1536]{1,0:T(8,128)(2,1)}) %all-gather.19.cloned.1.call-update) | async-done | bytes 2359312 | tf_op jit(solution)/shard_map/all_gather | solution.py:160
  459.0 5.4 %reshape.47 = bf16[768,4,384]{2,1,0:T(4,128)(2,1)} reshape(bf16[768,1536]{1,0:T(8,128)(2,1)} %all-gather.19.cloned.1.call-done) | data formatting | bytes 4718592 | tf_op jit(solution)/shard_map/all_gather | solution.py:160
  464.4 3.8 pad_maximum_fusion
  470.4 2.2 fusion.59
  472.6 28.3 %collective-permute-done.17 = bf16[768,640]{1,0:T(8,128)(2,1)} collective-permute-done((bf16[768,640]{1,0:T(8,128)(2,1)}, bf16[768,640]{1,0:T(8,128)(2,1)}, u32[]{:S(2)}, u32[]{:S(2)}) %collective-permute-start.17) | collective-permute-done | bytes 983072 | tf_op jit(solution)/shard_map/ppermute | solution.py:112
  500.9 2.2 fusion.61
  503.1 3.3 fusion.89
  506.4 2.3 add_add_fusion
  508.7 2.1 fusion
  510.8 4.0 copy.31
  (93 shorter events, 17.9 us)
Async XLA Ops:
  6.5 4.9 copy-start
  6.5 81.7 %all-gather.13.cloned.1.call-start = ((), (), s32[]{:S(2)}) async-start(), calls=%async_computation.2 | async-start | bytes 4915200 | tf_op jit(solution)/shard_map/all_gather | solution.py:100
  9.0 155.8 %all-gather.11.cloned.1.call-start = ((), (), s32[]{:S(2)}) async-start(), calls=%async_computation.1 | async-start | bytes 4915200 | tf_op jit(solution)/shard_map/all_gather | solution.py:100
  11.3 230.0 %all-gather.9.cloned.1.call-start = ((), (), s32[]{:S(2)}) async-start(), calls=%async_computation | async-start | bytes 4915200 | tf_op jit(solution)/shard_map/all_gather | solution.py:100
  12.6 305.2 %all-gather.15.cloned.1.call-start = ((), (), s32[]{:S(2)}) async-start(), calls=%async_computation.3 | async-start | bytes 4915200 | tf_op jit(solution)/shard_map/all_gather | solution.py:100
  15.6 425.0 %all-gather.17.cloned.1.call-start = ((), (), s32[]{:S(2)}) async-start(), calls=%async_computation.4 | async-start | bytes 2949120 | tf_op jit(solution)/shard_map/all_gather | solution.py:160
  15.8 3.7 copy-start.14
  19.5 2.8 copy-start.15
  22.3 3.8 copy-start.18
  91.8 194.9 %collective-permute-start.6 = (bf16[1280,384]{1,0:T(8,128)(2,1)}, bf16[1280,384]{1,0:T(8,128)(2,1)}, u32[]{:S(2)}, u32[]{:S(2)}) collective-permute-start(bf16[1280,384]{1,0:T(8,128)(2,1)} %get-tuple-element.19), channel_id=1, source_target_pairs={{0,16},{16,0},{1,17},{17,1},{2,18},{18,2},{3,19},{19,3},{4,20},{20... | collective-permute-start | bytes 2949128 | tf_op jit(solution)/shard_map/ppermute | solution.py:112
  93.2 180.4 %collective-permute-start.8 = (bf16[1280,384]{1,0:T(8,128)(2,1)}, bf16[1280,384]{1,0:T(8,128)(2,1)}, u32[]{:S(2)}, u32[]{:S(2)}) collective-permute-start(bf16[1280,384]{1,0:T(8,128)(2,1)} %get-tuple-element.20), channel_id=1, source_target_pairs={{0,16},{16,0},{1,17},{17,1},{2,18},{18,2},{3,19},{19,3},{4,20},{20... | collective-permute-start | bytes 2949128 | tf_op jit(solution)/shard_map/ppermute | solution.py:112
  164.8 7.1 %copy-start.8 = (bf16[5120,384]{1,0:T(8,128)(2,1)S(1)}, bf16[5120,384]{1,0:T(8,128)(2,1)}, u32[]{:S(2)}) copy-start(bf16[5120,384]{1,0:T(8,128)(2,1)} %all-gather.11.cloned.1.call-done) | copy-start | bytes 11796484
  168.4 96.9 %collective-permute-start.3 = (bf16[1280,384]{1,0:T(8,128)(2,1)}, bf16[1280,384]{1,0:T(8,128)(2,1)}, u32[]{:S(2)}, u32[]{:S(2)}) collective-permute-start(bf16[1280,384]{1,0:T(8,128)(2,1)} %get-tuple-element.22), channel_id=1, source_target_pairs={{0,16},{16,0},{1,17},{17,1},{2,18},{18,2},{3,19},{19,3},{4,20},{20... | collective-permute-start | bytes 2949128 | tf_op jit(solution)/shard_map/ppermute | solution.py:112
  169.9 88.8 %collective-permute-start.5 = (bf16[1280,384]{1,0:T(8,128)(2,1)}, bf16[1280,384]{1,0:T(8,128)(2,1)}, u32[]{:S(2)}, u32[]{:S(2)}) collective-permute-start(bf16[1280,384]{1,0:T(8,128)(2,1)} %get-tuple-element.23), channel_id=1, source_target_pairs={{0,16},{16,0},{1,17},{17,1},{2,18},{18,2},{3,19},{19,3},{4,20},{20... | collective-permute-start | bytes 2949128 | tf_op jit(solution)/shard_map/ppermute | solution.py:112
  170.4 92.0 %collective-permute-start.4 = (bf16[1280,384]{1,0:T(8,128)(2,1)}, bf16[1280,384]{1,0:T(8,128)(2,1)}, u32[]{:S(2)}, u32[]{:S(2)}) collective-permute-start(bf16[1280,384]{1,0:T(8,128)(2,1)} %get-tuple-element.24), channel_id=1, source_target_pairs={{0,16},{16,0},{1,17},{17,1},{2,18},{18,2},{3,19},{19,3},{4,20},{20... | collective-permute-start | bytes 2949128 | tf_op jit(solution)/shard_map/ppermute | solution.py:112
  178.3 90.9 %copy-start.3 = (f32[384,768]{1,0:T(8,128)}, f32[384,768]{1,0:T(8,128)S(1)}, u32[]{:S(2)}) copy-start(f32[384,768]{1,0:T(8,128)S(1)} %fusion.88) | copy-start | bytes 3538948
  241.4 7.8 %copy-start.7 = (bf16[5120,384]{1,0:T(8,128)(2,1)S(1)}, bf16[5120,384]{1,0:T(8,128)(2,1)}, u32[]{:S(2)}) copy-start(bf16[5120,384]{1,0:T(8,128)(2,1)} %all-gather.13.cloned.1.call-done) | copy-start | bytes 11796484
  241.4 18.8 %slice-start = ((s8[7864320]{0:T(1024)(128)(4,1)}), s8[3670016]{0:T(1024)(128)(4,1)S(1)}, s32[]{:S(2)}) async-start(s8[7864320]{0:T(1024)(128)(4,1)} %bitcast.51), calls=%async_computation.6 | async-start | bytes 7340032
  249.2 7.9 %copy-start.9 = (bf16[5120,384]{1,0:T(8,128)(2,1)S(1)}, bf16[5120,384]{1,0:T(8,128)(2,1)}, u32[]{:S(2)}) copy-start(bf16[5120,384]{1,0:T(8,128)(2,1)} %all-gather.9.cloned.1.call-done) | copy-start | bytes 11796484
  249.2 11.0 %slice-start.1 = ((s8[7864320]{0:T(1024)(128)(4,1)}), s8[4194304]{0:T(1024)(128)(4,1)S(1)}, s32[]{:S(2)}) async-start(s8[7864320]{0:T(1024)(128)(4,1)} %bitcast.51), calls=%async_computation.7 | async-start | bytes 8388608
  258.7 24.9 %collective-permute-start.7 = (bf16[1280,384]{1,0:T(8,128)(2,1)}, bf16[1280,384]{1,0:T(8,128)(2,1)}, u32[]{:S(2)}, u32[]{:S(2)}) collective-permute-start(bf16[1280,384]{1,0:T(8,128)(2,1)} %get-tuple-element.21), channel_id=1, source_target_pairs={{0,16},{16,0},{1,17},{17,1},{2,18},{18,2},{3,19},{19,3},{4,20},{20... | collective-permute-start | bytes 2949128 | tf_op jit(solution)/shard_map/ppermute | solution.py:112
  262.4 88.0 %collective-permute-start = (bf16[1280,384]{1,0:T(8,128)(2,1)}, bf16[1280,384]{1,0:T(8,128)(2,1)}, u32[]{:S(2)}, u32[]{:S(2)}) collective-permute-start(bf16[1280,384]{1,0:T(8,128)(2,1)} %get-tuple-element.16), channel_id=1, source_target_pairs={{0,16},{16,0},{1,17},{17,1},{2,18},{18,2},{3,19},{19,3},{4,20},{20... | collective-permute-start | bytes 2949128 | tf_op jit(solution)/shard_map/ppermute | solution.py:112
  265.3 61.4 %collective-permute-start.2 = (bf16[1280,384]{1,0:T(8,128)(2,1)}, bf16[1280,384]{1,0:T(8,128)(2,1)}, u32[]{:S(2)}, u32[]{:S(2)}) collective-permute-start(bf16[1280,384]{1,0:T(8,128)(2,1)} %get-tuple-element.17), channel_id=1, source_target_pairs={{0,16},{16,0},{1,17},{17,1},{2,18},{18,2},{3,19},{19,3},{4,20},{20... | collective-permute-start | bytes 2949128 | tf_op jit(solution)/shard_map/ppermute | solution.py:112
  273.6 72.0 %collective-permute-start.1 = (bf16[1280,384]{1,0:T(8,128)(2,1)}, bf16[1280,384]{1,0:T(8,128)(2,1)}, u32[]{:S(2)}, u32[]{:S(2)}) collective-permute-start(bf16[1280,384]{1,0:T(8,128)(2,1)} %get-tuple-element.18), channel_id=1, source_target_pairs={{0,16},{16,0},{1,17},{17,1},{2,18},{18,2},{3,19},{19,3},{4,20},{20... | collective-permute-start | bytes 2949128 | tf_op jit(solution)/shard_map/ppermute | solution.py:112
  277.2 9.5 %copy-start.10 = (f32[768,384]{1,0:T(8,128)S(1)}, f32[768,384]{1,0:T(8,128)}, u32[]{:S(2)}) copy-start(f32[768,384]{1,0:T(8,128)} %fusion.20) | copy-start | bytes 3538948
  286.6 3.3 copy-start.2
  286.6 3.3 copy-start.16
  289.9 1.1 copy-start.13
  318.9 40.0 %collective-permute-start.10 = (bf16[768,384]{1,0:T(8,128)(2,1)}, bf16[768,384]{1,0:T(8,128)(2,1)}, u32[]{:S(2)}, u32[]{:S(2)}) collective-permute-start(bf16[768,384]{1,0:T(8,128)(2,1)} %get-tuple-element.29), channel_id=1, source_target_pairs={{4,0},{8,4},{12,8},{5,1},{9,5},{13,9},{6,2},{10,6},{14,10},{7,3},{... | collective-permute-start | bytes 1769480 | tf_op jit(solution)/shard_map/ppermute | solution.py:18
  320.2 38.7 %collective-permute-start.9 = (bf16[768,384]{1,0:T(8,128)(2,1)}, bf16[768,384]{1,0:T(8,128)(2,1)}, u32[]{:S(2)}, u32[]{:S(2)}) collective-permute-start(bf16[768,384]{1,0:T(8,128)(2,1)} %get-tuple-element.29), channel_id=1, source_target_pairs={{0,4},{4,8},{8,12},{1,5},{5,9},{9,13},{2,6},{6,10},{10,14},{3,7},{... | collective-permute-start | bytes 1769480 | tf_op jit(solution)/shard_map/ppermute | solution.py:18
  326.7 35.0 %collective-permute-start.12 = (bf16[768,384]{1,0:T(8,128)(2,1)}, bf16[768,384]{1,0:T(8,128)(2,1)}, u32[]{:S(2)}, u32[]{:S(2)}) collective-permute-start(bf16[768,384]{1,0:T(8,128)(2,1)} %get-tuple-element.27), channel_id=1, source_target_pairs={{4,0},{8,4},{12,8},{5,1},{9,5},{13,9},{6,2},{10,6},{14,10},{7,3},{... | collective-permute-start | bytes 1769480 | tf_op jit(solution)/shard_map/ppermute | solution.py:18
  330.8 19.7 %copy-start.11 = (f32[768,384]{0,1:T(8,128)S(1)}, f32[768,384]{0,1:T(8,128)}, u32[]{:S(2)}) copy-start(f32[768,384]{0,1:T(8,128)} %fusion.24) | copy-start | bytes 3538948
  345.6 16.2 %collective-permute-start.11 = (bf16[768,384]{1,0:T(8,128)(2,1)}, bf16[768,384]{1,0:T(8,128)(2,1)}, u32[]{:S(2)}, u32[]{:S(2)}) collective-permute-start(bf16[768,384]{1,0:T(8,128)(2,1)} %get-tuple-element.27), channel_id=1, source_target_pairs={{0,4},{4,8},{8,12},{1,5},{5,9},{9,13},{2,6},{6,10},{10,14},{3,7},{... | collective-permute-start | bytes 1769480 | tf_op jit(solution)/shard_map/ppermute | solution.py:18
  353.9 2.0 copy-start.17
  364.6 19.0 %copy-start.4 = (bf16[768,384]{1,0:T(8,128)(2,1)S(1)}, bf16[768,384]{1,0:T(8,128)(2,1)}, u32[]{:S(2)}) copy-start(bf16[768,384]{1,0:T(8,128)(2,1)} %get-tuple-element.30) | copy-start | bytes 1769476
  364.6 24.9 %copy-start.5 = (bf16[768,384]{1,0:T(8,128)(2,1)S(1)}, bf16[768,384]{1,0:T(8,128)(2,1)}, u32[]{:S(2)}) copy-start(bf16[768,384]{1,0:T(8,128)(2,1)} %get-tuple-element.28) | copy-start | bytes 1769476
  383.6 75.4 %all-gather.19.cloned.1.call-start = ((), (), s32[]{:S(2)}) async-start(), calls=%async_computation.5 | async-start | bytes 2949120 | tf_op jit(solution)/shard_map/all_gather | solution.py:160
  383.6 18.1 %collective-permute-start.14 = (bf16[768,384]{1,0:T(8,128)(2,1)S(1)}, bf16[768,384]{1,0:T(8,128)(2,1)S(1)}, u32[]{:S(2)}, u32[]{:S(2)}) collective-permute-start(bf16[768,384]{1,0:T(8,128)(2,1)S(1)} %copy-done.4), channel_id=1, source_target_pairs={{4,0},{8,4},{12,8},{5,1},{9,5},{13,9},{6,2},{10,6},{14,10},{7,3},{... | collective-permute-start | bytes 1769480 | tf_op jit(solution)/shard_map/ppermute | solution.py:18
  384.9 18.3 %collective-permute-start.13 = (bf16[768,384]{1,0:T(8,128)(2,1)S(1)}, bf16[768,384]{1,0:T(8,128)(2,1)S(1)}, u32[]{:S(2)}, u32[]{:S(2)}) collective-permute-start(bf16[768,384]{1,0:T(8,128)(2,1)S(1)} %copy-done.4), channel_id=1, source_target_pairs={{0,4},{4,8},{8,12},{1,5},{5,9},{9,13},{2,6},{6,10},{10,14},{3,7},{... | collective-permute-start | bytes 1769480 | tf_op jit(solution)/shard_map/ppermute | solution.py:18
  389.5 22.7 %collective-permute-start.16 = (bf16[768,384]{1,0:T(8,128)(2,1)S(1)}, bf16[768,384]{1,0:T(8,128)(2,1)S(1)}, u32[]{:S(2)}, u32[]{:S(2)}) collective-permute-start(bf16[768,384]{1,0:T(8,128)(2,1)S(1)} %copy-done.5), channel_id=1, source_target_pairs={{4,0},{8,4},{12,8},{5,1},{9,5},{13,9},{6,2},{10,6},{14,10},{7,3},{... | collective-permute-start | bytes 1769480 | tf_op jit(solution)/shard_map/ppermute | solution.py:18
  390.8 22.6 %collective-permute-start.15 = (bf16[768,384]{1,0:T(8,128)(2,1)S(1)}, bf16[768,384]{1,0:T(8,128)(2,1)S(1)}, u32[]{:S(2)}, u32[]{:S(2)}) collective-permute-start(bf16[768,384]{1,0:T(8,128)(2,1)S(1)} %copy-done.5), channel_id=1, source_target_pairs={{0,4},{4,8},{8,12},{1,5},{5,9},{9,13},{2,6},{6,10},{10,14},{3,7},{... | collective-permute-start | bytes 1769480 | tf_op jit(solution)/shard_map/ppermute | solution.py:18
  437.1 33.2 %collective-permute-start.18 = (bf16[768,640]{1,0:T(8,128)(2,1)}, bf16[768,640]{1,0:T(8,128)(2,1)}, u32[]{:S(2)}, u32[]{:S(2)}) collective-permute-start(bf16[768,640]{1,0:T(8,128)(2,1)} %get-tuple-element.14), channel_id=1, source_target_pairs={{0,16},{16,0},{1,17},{17,1},{2,18},{18,2},{3,19},{19,3},{4,20},{20... | collective-permute-start | bytes 2949128 | tf_op jit(solution)/shard_map/ppermute | solution.py:112
  438.6 67.8 %collective-permute-start.19 = (bf16[768,640]{1,0:T(8,128)(2,1)S(1)}, bf16[768,640]{1,0:T(8,128)(2,1)}, u32[]{:S(2)}, u32[]{:S(2)}) collective-permute-start(bf16[768,640]{1,0:T(8,128)(2,1)S(1)} %get-tuple-element.13), channel_id=1, source_target_pairs={{0,16},{16,0},{1,17},{17,1},{2,18},{18,2},{3,19},{19,3},{4,20},{20... | collective-permute-start | bytes 2949128 | tf_op jit(solution)/shard_map/ppermute | solution.py:112
  439.1 61.8 %collective-permute-start.17 = (bf16[768,640]{1,0:T(8,128)(2,1)}, bf16[768,640]{1,0:T(8,128)(2,1)}, u32[]{:S(2)}, u32[]{:S(2)}) collective-permute-start(bf16[768,640]{1,0:T(8,128)(2,1)} %get-tuple-element.15), channel_id=1, source_target_pairs={{0,16},{16,0},{1,17},{17,1},{2,18},{18,2},{3,19},{19,3},{4,20},{20... | collective-permute-start | bytes 2949128 | tf_op jit(solution)/shard_map/ppermute | solution.py:112
  468.2 1.2 copy-start.12
  472.6 30.5 %copy-start.6 = (bf16[3072,640]{1,0:T(8,128)(2,1)S(1)}, bf16[3072,640]{1,0:T(8,128)(2,1)}, u32[]{:S(2)}) copy-start(bf16[3072,640]{1,0:T(8,128)(2,1)} %all-gather.15.cloned.1.call-done) | copy-start | bytes 11796484
  508.7 6.1 %copy-start.1 = (bf16[1280,768]{1,0:T(8,128)(2,1)S(1)}, bf16[1280,768]{1,0:T(8,128)(2,1)}, u32[]{:S(2)}) copy-start(bf16[1280,768]{1,0:T(8,128)(2,1)} %param.10) | copy-start | bytes 5898244
Sparse Core Ops, SparseCore 0:
  9.1 79.1 all-gather.12
  89.8 74.9 all-gather.10
  166.4 74.9 all-gather.8
  242.8 74.9 all-gather.14
  383.7 23.1 all-gather.16
  433.9 25.0 all-gather.18

commit v9 on v6

--- a/solution.py
+++ b/solution.py
@@ -30,8 +30,8 @@
     tiles = q_ref.shape[0] // TILE
     picks = kb_ref.shape[1]
     scale = 1.0 / math.sqrt(HEAD_DIM)
-    lanes = lax.broadcasted_iota(jnp.int32, (TILE, TILE), 1)
-    rows = lax.broadcasted_iota(jnp.int32, (TILE, TILE), 0)
+    lanes = lax.broadcasted_iota(jnp.int32, (1, TILE), 1)
+    rows = lax.broadcasted_iota(jnp.int32, (TILE, 1), 0)
 
     def one_tile(i, carry):
         start = pl.multiple_of(i * TILE, TILE)
@@ -48,13 +48,15 @@
             limit = lim_ref[slab]
             pos = (b - slab * tiles) * TILE + lanes
             scores.append(jnp.where(pos < limit, s, -1e30))
-        top = jnp.max(scores[0], axis=1, keepdims=True)
+        top = scores[0]
         for s in scores[1:]:
-            top = jnp.maximum(top, jnp.max(s, axis=1, keepdims=True))
+            top = jnp.maximum(top, s)
+        top = jnp.max(top, axis=1, keepdims=True)
         expo = [jnp.exp(s - top) for s in scores]
-        total = jnp.sum(expo[0], axis=1, keepdims=True)
+        total = expo[0]
         for e in expo[1:]:
-            total = total + jnp.sum(e, axis=1, keepdims=True)
+            total = total + e
+        total = jnp.sum(total, axis=1, keepdims=True)
         acc = None
         for j in range(picks):
             b = kb_ref[i, j]

time: 495 us -> 492 us (level)
  no operation moved by 1% of the time
where the time goes in v9:
time: 492 us; the launch traced here: 491 us
  waiting for transfers between devices  309 us (63%)
  matrix products  59.5 us (12%)
  local copies, waits for them, and re-layouts  32.4 us (7%)
  Pallas kernels  32.1 us (7%)
  starting transfers between devices  28.2 us (6%)
  other arithmetic  16 us (3%)
  between operations  13.7 us (3%)
    all_gather x4, waiting for transfers between devices, fetch(): return (lax.all_gather(mine, 'frames', axis=0, tiled=True), other)  178 us
    ppermute x12, waiting for transfers between devices, trade(): recv.append(lax.ppermute(part, 'clips', [(0, 1), (1, 0)]))  99 us
    pallas_call x1, Pallas kernels, attend(): pl.pallas_call(attend_kernel, grid_spec=spec, out_shape=jax.ShapeDtypeStr...  32.1 us
    dot_general x12, matrix products, split_dot(): jnp.dot(lax.dynamic_slice_in_dim(x, at * rows, rows, 1), part, preferred_...  28.3 us
    dot_general x4, matrix products, split_dot(): own = jnp.dot(x, got, preferred_element_type=jnp.float32)  20.9 us
    ppermute x4, waiting for transfers between devices, shifted(): return lax.ppermute(value, axis, pairs)  20.1 us
    ppermute x12, starting transfers between devices, trade(): recv.append(lax.ppermute(part, 'clips', [(0, 1), (1, 0)]))  14.1 us
    ppermute x4, starting transfers between devices, shifted(): return lax.ppermute(value, axis, pairs)  13.9 us
  transfers between devices with their start and end apart: 21, of which 12 were waited for; matrix products, arithmetic and copies ran while one was open for 19% of the time, Pallas kernels for 0%

profile of v9, /device:TPU:0, one launch (start us, length us, event | category | flops | bytes accessed | tf_op | source)
XLA Modules:
  0.0 490.7 jit_solution(1598497693625996844)
XLA Ops:
  6.5 2.4 constant_dynamic-slice_fusion.13
  9.1 1.1 constant_dynamic-slice_fusion.17
  10.2 3.0 constant_dynamic-slice_fusion.8
  13.3 3.0 constant_dynamic-slice_fusion.3
  16.4 3.7 fusion.24
  20.1 2.8 fusion.22
  23.7 64.6 %all-gather.8.cloned.1.call-done = bf16[5120,384]{1,0:T(8,128)(2,1)} async-done(((bf16[1280,384]{1,0:T(8,128)(2,1)}), bf16[5120,384]{1,0:T(8,128)(2,1)}) %all-gather.8.cloned.1.call-update) | async-done | bytes 3932176 | tf_op jit(solution)/shard_map/all_gather | solution.py:102
  88.3 3.5 constant_dynamic-slice_fusion.12
  91.8 1.5 collective-permute-start.3
  93.9 71.0 %all-gather.6.cloned.1.call-done = bf16[5120,384]{1,0:T(8,128)(2,1)} async-done(((bf16[1280,384]{1,0:T(8,128)(2,1)}), bf16[5120,384]{1,0:T(8,128)(2,1)}) %all-gather.6.cloned.1.call-update) | async-done | bytes 3932176 | tf_op jit(solution)/shard_map/all_gather | solution.py:102
  164.8 2.2 constant_dynamic-slice_fusion.16
  167.1 1.5 collective-permute-start
  169.2 1.5 collective-permute-start.1
  170.7 6.9 %fusion.83 = f32[384,768]{1,0:T(8,128)S(1)} fusion(bf16[5120,384]{1,0:T(8,128)(2,1)S(1)} %copy-done.7, bf16[768,5120]{1,0:T(8,128)(2,1)} %param.9), kind=kOutput, calls=%fused_computation.96 | convolution fusion | flops 3019898880 | bytes 12976128 | tf_op jit(solution)/shard_map/dot_general | solution.py:123
  177.7 5.1 %convolution_bitcast_fusion = bf16[768,384]{1,0:T(8,128)(2,1)} fusion(bf16[768,5120]{1,0:T(8,128)(2,1)S(1)} %bitcast.45, bf16[5120,384]{1,0:T(8,128)(2,1)S(1)} %copy-done.6), kind=kOutput, calls=%fused_computation.40 | convolution fusion | flops 3019898880 | bytes 12386304 | tf_op jit(solution)/shard_map/dot_general | solution.py:123
  182.7 30.1 %collective-permute-done.2 = bf16[1280,384]{1,0:T(8,128)(2,1)S(1)} collective-permute-done((bf16[1280,384]{1,0:T(8,128)(2,1)S(1)}, bf16[1280,384]{1,0:T(8,128)(2,1)S(1)}, u32[]{:S(2)}, u32[]{:S(2)}) %collective-permute-start.2) | collective-permute-done | bytes 983072 | tf_op jit(solution)/shard_map/ppermute | solution.py:114
  212.8 1.5 collective-permute-start.4
  214.3 1.0 fusion.6
  215.4 18.5 %collective-permute-done.1 = bf16[1280,384]{1,0:T(8,128)(2,1)S(1)} collective-permute-done((bf16[1280,384]{1,0:T(8,128)(2,1)S(1)}, bf16[1280,384]{1,0:T(8,128)(2,1)S(1)}, u32[]{:S(2)}, u32[]{:S(2)}) %collective-permute-start.1) | collective-permute-done | bytes 983072 | tf_op jit(solution)/shard_map/ppermute | solution.py:114
  233.9 1.0 fusion.12
  235.0 1.2 fusion.46
  236.6 1.9 copy.24
  238.6 3.0 fusion.4
  241.6 12.2 %collective-permute-done.4 = bf16[1280,384]{1,0:T(8,128)(2,1)} collective-permute-done((bf16[1280,384]{1,0:T(8,128)(2,1)}, bf16[1280,384]{1,0:T(8,128)(2,1)}, u32[]{:S(2)}, u32[]{:S(2)}) %collective-permute-start.4) | collective-permute-done | bytes 983072 | tf_op jit(solution)/shard_map/ppermute | solution.py:114
  253.8 3.0 fusion.10
  256.8 3.1 fusion.49
  260.3 1.4 copy-done.2
  261.6 1.3 multiply_convert_fusion.1
  263.0 3.7 constant_dynamic-slice_fusion.7
  266.6 1.5 collective-permute-start.6
  268.6 1.5 collective-permute-start.7
  270.1 5.6 %fusion.84 = f32[384,768]{1,0:T(8,128)S(1)} fusion(bf16[5120,384]{1,0:T(8,128)(2,1)S(1)} %copy-done.5, bf16[768,5120]{1,0:T(8,128)(2,1)} %param.9), kind=kOutput, calls=%fused_computation.97 | convolution fusion | flops 3019898880 | bytes 12976128 | tf_op jit(solution)/shard_map/dot_general | solution.py:123
  275.8 42.0 %all-gather.12.cloned.1.call-done = bf16[3072,640]{1,0:T(8,128)(2,1)} async-done(((bf16[768,640]{1,0:T(8,128)(2,1)}), bf16[3072,640]{1,0:T(8,128)(2,1)}) %all-gather.12.cloned.1.call-update) | async-done | bytes 3932176 | tf_op jit(solution)/shard_map/all_gather | solution.py:102
  317.8 1.3 collective-permute-start.10
  319.1 5.7 %collective-permute-start.9 = (bf16[768,768]{1,0:T(8,128)(2,1)}, bf16[768,768]{1,0:T(8,128)(2,1)}, u32[]{:S(2)}, u32[]{:S(2)}) collective-permute-start(bf16[768,768]{1,0:T(8,128)(2,1)} %multiply_convert_fusion.1), channel_id=1, source_target_pairs={{0,4},{4,8},{8,12},{1,5},{5,9},{9,13},{2,6},{6,10},{10,14},{3,7},{... | collective-permute-start | bytes 3538952 | tf_op jit(solution)/shard_map/ppermute | solution.py:18
  324.8 2.8 fusion.20
  327.6 1.3 collective-permute-start.12
  328.9 2.8 fusion.2
  331.7 5.6 %collective-permute-start.11 = (bf16[768,768]{1,0:T(8,128)(2,1)S(1)}, bf16[768,768]{1,0:T(8,128)(2,1)}, u32[]{:S(2)}, u32[]{:S(2)}) collective-permute-start(bf16[768,768]{1,0:T(8,128)(2,1)S(1)} %fusion.1), channel_id=1, source_target_pairs={{0,4},{4,8},{8,12},{1,5},{5,9},{9,13},{2,6},{6,10},{10,14},{3,7},{... | collective-permute-start | bytes 3538952 | tf_op jit(solution)/shard_map/ppermute | solution.py:18
  337.3 2.8 fusion.8
  340.1 3.0 fusion.52
  343.4 1.9 fusion.35
  345.3 2.2 copy.30
  347.6 2.9 multiply_convert_fusion.q_ref
  350.4 3.4 pad_maximum_fusion.k_ref
  353.8 19.0 %collective-permute-done.12 = bf16[768,768]{1,0:T(8,128)(2,1)} collective-permute-done((bf16[768,768]{1,0:T(8,128)(2,1)S(1)}, bf16[768,768]{1,0:T(8,128)(2,1)}, u32[]{:S(2)}, u32[]{:S(2)}) %collective-permute-start.12) | collective-permute-done | bytes 1179680 | tf_op jit(solution)/shard_map/ppermute | solution.py:18
  372.8 1.1 collective-permute-done.11
  373.9 3.2 pad_maximum_fusion.1.v_ref
  377.1 32.1 %shard_map.91 = bf16[768,768]{1,0:T(8,128)(2,1)} custom-call(s32[6,8]{1,0:T(8,128)} %kb_ref.1, s32[3]{0:T(128)} %dynamic_slice.95.lim_ref, bf16[768,768]{1,0:T(8,128)(2,1)} %multiply_convert_fusion.q_ref, bf16[2304,768]{1,0:T(8,128)(2,1)} %pad_maximum_fusion.k_ref, bf16[2304,768]{1,0:T(8,128)(2,1)} %pad_maximum_fusion.1.v_ref), custom_call_target="tpu_custom_call" | custom-call | tf_op jit(solution)/shard_map/pallas_call | solution.py:88
  409.3 2.1 constant_dynamic-slice_fusion
  411.4 1.5 collective-permute-start.14
  413.4 1.5 collective-permute-start.15
  414.9 21.2 %collective-permute-done.14 = bf16[768,640]{1,0:T(8,128)(2,1)} collective-permute-done((bf16[768,640]{1,0:T(8,128)(2,1)S(1)}, bf16[768,640]{1,0:T(8,128)(2,1)}, u32[]{:S(2)}, u32[]{:S(2)}) %collective-permute-start.14) | collective-permute-done | bytes 983072 | tf_op jit(solution)/shard_map/ppermute | solution.py:114
  436.2 12.2 %all-gather.14.cloned.1.call-done = bf16[768,3072]{1,0:T(8,128)(2,1)} async-done(((bf16[768,768]{1,0:T(8,128)(2,1)}), bf16[768,3072]{1,0:T(8,128)(2,1)}) %all-gather.14.cloned.1.call-update) | async-done | bytes 4718608 | tf_op jit(solution)/shard_map/all_gather | solution.py:154
  448.4 2.7 fusion.59
  451.1 6.1 %collective-permute-done.13 = bf16[768,640]{1,0:T(8,128)(2,1)} collective-permute-done((bf16[768,640]{1,0:T(8,128)(2,1)S(1)}, bf16[768,640]{1,0:T(8,128)(2,1)}, u32[]{:S(2)}, u32[]{:S(2)}) %collective-permute-start.13) | collective-permute-done | bytes 983072 | tf_op jit(solution)/shard_map/ppermute | solution.py:114
  457.2 2.5 fusion.61
  459.8 1.0 fusion.63
  460.8 1.1 copy-done.4
  461.9 3.3 fusion.85
  465.2 10.7 %collective-permute-done.15 = bf16[768,640]{1,0:T(8,128)(2,1)} collective-permute-done((bf16[768,640]{1,0:T(8,128)(2,1)S(1)}, bf16[768,640]{1,0:T(8,128)(2,1)}, u32[]{:S(2)}, u32[]{:S(2)}) %collective-permute-start.15) | collective-permute-done | bytes 983072 | tf_op jit(solution)/shard_map/ppermute | solution.py:114
  475.9 2.3 add_add_fusion
  478.1 2.1 fusion
  480.2 4.0 copy.31
  (66 shorter events, 4.4 us)
Async XLA Ops:
  6.5 2.5 copy-start
  6.5 81.8 %all-gather.8.cloned.1.call-start = ((), (), s32[]{:S(2)}) async-start(), calls=%async_computation.1 | async-start | bytes 4915200 | tf_op jit(solution)/shard_map/all_gather | solution.py:102
  9.0 155.8 %all-gather.6.cloned.1.call-start = ((), (), s32[]{:S(2)}) async-start(), calls=%async_computation | async-start | bytes 4915200 | tf_op jit(solution)/shard_map/all_gather | solution.py:102
  10.1 252.8 %all-gather.10.cloned.1.call-start = ((), (), s32[]{:S(2)}) async-start(), calls=%async_computation.2 | async-start | bytes 4915200 | tf_op jit(solution)/shard_map/all_gather | solution.py:102
  13.2 304.6 %all-gather.12.cloned.1.call-start = ((), (), s32[]{:S(2)}) async-start(), calls=%async_computation.3 | async-start | bytes 4915200 | tf_op jit(solution)/shard_map/all_gather | solution.py:102
  16.3 432.1 %all-gather.14.cloned.1.call-start = ((), (), s32[]{:S(2)}) async-start(), calls=%async_computation.4 | async-start | bytes 5898240 | tf_op jit(solution)/shard_map/all_gather | solution.py:154
  16.4 3.7 copy-start.11
  20.1 2.9 copy-start.15
  91.8 164.9 %collective-permute-start.3 = (bf16[1280,384]{1,0:T(8,128)(2,1)}, bf16[1280,384]{1,0:T(8,128)(2,1)}, u32[]{:S(2)}, u32[]{:S(2)}) collective-permute-start(bf16[1280,384]{1,0:T(8,128)(2,1)} %get-tuple-element.27), channel_id=1, source_target_pairs={{0,16},{16,0},{1,17},{17,1},{2,18},{18,2},{3,19},{19,3},{4,20},{20... | collective-permute-start | bytes 2949128 | tf_op jit(solution)/shard_map/ppermute | solution.py:114
  93.3 145.3 %collective-permute-start.5 = (bf16[1280,384]{1,0:T(8,128)(2,1)}, bf16[1280,384]{1,0:T(8,128)(2,1)}, u32[]{:S(2)}, u32[]{:S(2)}) collective-permute-start(bf16[1280,384]{1,0:T(8,128)(2,1)} %get-tuple-element.28), channel_id=1, source_target_pairs={{0,16},{16,0},{1,17},{17,1},{2,18},{18,2},{3,19},{19,3},{4,20},{20... | collective-permute-start | bytes 2949128 | tf_op jit(solution)/shard_map/ppermute | solution.py:114
  164.8 5.8 %copy-start.7 = (bf16[5120,384]{1,0:T(8,128)(2,1)S(1)}, bf16[5120,384]{1,0:T(8,128)(2,1)}, u32[]{:S(2)}) copy-start(bf16[5120,384]{1,0:T(8,128)(2,1)} %all-gather.6.cloned.1.call-done) | copy-start | bytes 11796484
  167.1 67.8 %collective-permute-start = (bf16[1280,384]{1,0:T(8,128)(2,1)S(1)}, bf16[1280,384]{1,0:T(8,128)(2,1)S(1)}, u32[]{:S(2)}, u32[]{:S(2)}) collective-permute-start(bf16[1280,384]{1,0:T(8,128)(2,1)S(1)} %get-tuple-element.30), channel_id=1, source_target_pairs={{0,16},{16,0},{1,17},{17,1},{2,18},{18,2},{3,19},{19,3},{4,20},{20... | collective-permute-start | bytes 2949128 | tf_op jit(solution)/shard_map/ppermute | solution.py:114
  168.6 44.2 %collective-permute-start.2 = (bf16[1280,384]{1,0:T(8,128)(2,1)S(1)}, bf16[1280,384]{1,0:T(8,128)(2,1)S(1)}, u32[]{:S(2)}, u32[]{:S(2)}) collective-permute-start(bf16[1280,384]{1,0:T(8,128)(2,1)S(1)} %get-tuple-element.31), channel_id=1, source_target_pairs={{0,16},{16,0},{1,17},{17,1},{2,18},{18,2},{3,19},{19,3},{4,20},{20... | collective-permute-start | bytes 2949128 | tf_op jit(solution)/shard_map/ppermute | solution.py:114
  169.2 8.4 %slice-start = ((s8[7864320]{0:T(1024)(128)(4,1)}), s8[4194304]{0:T(1024)(128)(4,1)S(1)}, s32[]{:S(2)}) async-start(s8[7864320]{0:T(1024)(128)(4,1)} %bitcast.44), calls=%async_computation.5 | async-start | bytes 8388608
  169.2 8.5 %slice-start.1 = ((s8[7864320]{0:T(1024)(128)(4,1)}), s8[3670016]{0:T(1024)(128)(4,1)S(1)}, s32[]{:S(2)}) async-start(s8[7864320]{0:T(1024)(128)(4,1)} %bitcast.44), calls=%async_computation.6 | async-start | bytes 7340032
  169.2 8.5 %copy-start.6 = (bf16[5120,384]{1,0:T(8,128)(2,1)S(1)}, bf16[5120,384]{1,0:T(8,128)(2,1)}, u32[]{:S(2)}) copy-start(bf16[5120,384]{1,0:T(8,128)(2,1)} %all-gather.8.cloned.1.call-done) | copy-start | bytes 11796484
  169.2 64.7 %collective-permute-start.1 = (bf16[1280,384]{1,0:T(8,128)(2,1)S(1)}, bf16[1280,384]{1,0:T(8,128)(2,1)S(1)}, u32[]{:S(2)}, u32[]{:S(2)}) collective-permute-start(bf16[1280,384]{1,0:T(8,128)(2,1)S(1)} %get-tuple-element.32), channel_id=1, source_target_pairs={{0,16},{16,0},{1,17},{17,1},{2,18},{18,2},{3,19},{19,3},{4,20},{20... | collective-permute-start | bytes 2949128 | tf_op jit(solution)/shard_map/ppermute | solution.py:114
  212.8 41.0 %collective-permute-start.4 = (bf16[1280,384]{1,0:T(8,128)(2,1)}, bf16[1280,384]{1,0:T(8,128)(2,1)}, u32[]{:S(2)}, u32[]{:S(2)}) collective-permute-start(bf16[1280,384]{1,0:T(8,128)(2,1)} %get-tuple-element.29), channel_id=1, source_target_pairs={{0,16},{16,0},{1,17},{17,1},{2,18},{18,2},{3,19},{19,3},{4,20},{20... | collective-permute-start | bytes 2949128 | tf_op jit(solution)/shard_map/ppermute | solution.py:114
  215.3 19.6 %copy-start.8 = (f32[768,384]{0,1:T(8,128)S(1)}, f32[768,384]{0,1:T(8,128)}, u32[]{:S(2)}) copy-start(f32[768,384]{0,1:T(8,128)} %fusion.24) | copy-start | bytes 3538948
  256.8 3.2 copy-start.10
  256.8 3.5 copy-start.13
  260.0 1.7 copy-start.2
  263.0 7.2 %copy-start.5 = (bf16[5120,384]{1,0:T(8,128)(2,1)S(1)}, bf16[5120,384]{1,0:T(8,128)(2,1)}, u32[]{:S(2)}) copy-start(bf16[5120,384]{1,0:T(8,128)(2,1)} %all-gather.10.cloned.1.call-done) | copy-start | bytes 11796484
  266.6 73.5 %collective-permute-start.6 = (bf16[1280,384]{1,0:T(8,128)(2,1)}, bf16[1280,384]{1,0:T(8,128)(2,1)}, u32[]{:S(2)}, u32[]{:S(2)}) collective-permute-start(bf16[1280,384]{1,0:T(8,128)(2,1)} %get-tuple-element.24), channel_id=1, source_target_pairs={{0,16},{16,0},{1,17},{17,1},{2,18},{18,2},{3,19},{19,3},{4,20},{20... | collective-permute-start | bytes 2949128 | tf_op jit(solution)/shard_map/ppermute | solution.py:114
  268.1 59.5 %collective-permute-start.8 = (bf16[1280,384]{1,0:T(8,128)(2,1)}, bf16[1280,384]{1,0:T(8,128)(2,1)}, u32[]{:S(2)}, u32[]{:S(2)}) collective-permute-start(bf16[1280,384]{1,0:T(8,128)(2,1)} %get-tuple-element.25), channel_id=1, source_target_pairs={{0,16},{16,0},{1,17},{17,1},{2,18},{18,2},{3,19},{19,3},{4,20},{20... | collective-permute-start | bytes 2949128 | tf_op jit(solution)/shard_map/ppermute | solution.py:114
  268.6 63.0 %collective-permute-start.7 = (bf16[1280,384]{1,0:T(8,128)(2,1)}, bf16[1280,384]{1,0:T(8,128)(2,1)}, u32[]{:S(2)}, u32[]{:S(2)}) collective-permute-start(bf16[1280,384]{1,0:T(8,128)(2,1)} %get-tuple-element.26), channel_id=1, source_target_pairs={{0,16},{16,0},{1,17},{17,1},{2,18},{18,2},{3,19},{19,3},{4,20},{20... | collective-permute-start | bytes 2949128 | tf_op jit(solution)/shard_map/ppermute | solution.py:114
  275.8 67.3 %copy-start.3 = (f32[384,768]{1,0:T(8,128)}, f32[384,768]{1,0:T(8,128)S(1)}, u32[]{:S(2)}) copy-start(f32[384,768]{1,0:T(8,128)S(1)} %fusion.84) | copy-start | bytes 3538948
  317.8 32.6 %collective-permute-start.10 = (bf16[768,768]{1,0:T(8,128)(2,1)}, bf16[768,768]{1,0:T(8,128)(2,1)}, u32[]{:S(2)}, u32[]{:S(2)}) collective-permute-start(bf16[768,768]{1,0:T(8,128)(2,1)} %multiply_convert_fusion.1), channel_id=1, source_target_pairs={{4,0},{8,4},{12,8},{5,1},{9,5},{13,9},{6,2},{10,6},{14,10},{7,3},{... | collective-permute-start | bytes 3538952 | tf_op jit(solution)/shard_map/ppermute | solution.py:18
  319.1 31.3 %collective-permute-start.9 = (bf16[768,768]{1,0:T(8,128)(2,1)}, bf16[768,768]{1,0:T(8,128)(2,1)}, u32[]{:S(2)}, u32[]{:S(2)}) collective-permute-start(bf16[768,768]{1,0:T(8,128)(2,1)} %multiply_convert_fusion.1), channel_id=1, source_target_pairs={{0,4},{4,8},{8,12},{1,5},{5,9},{9,13},{2,6},{6,10},{10,14},{3,7},{... | collective-permute-start | bytes 3538952 | tf_op jit(solution)/shard_map/ppermute | solution.py:18
  327.6 45.3 %collective-permute-start.12 = (bf16[768,768]{1,0:T(8,128)(2,1)S(1)}, bf16[768,768]{1,0:T(8,128)(2,1)}, u32[]{:S(2)}, u32[]{:S(2)}) collective-permute-start(bf16[768,768]{1,0:T(8,128)(2,1)S(1)} %fusion.1), channel_id=1, source_target_pairs={{4,0},{8,4},{12,8},{5,1},{9,5},{13,9},{6,2},{10,6},{14,10},{7,3},{... | collective-permute-start | bytes 3538952 | tf_op jit(solution)/shard_map/ppermute | solution.py:18
  331.7 42.2 %collective-permute-start.11 = (bf16[768,768]{1,0:T(8,128)(2,1)S(1)}, bf16[768,768]{1,0:T(8,128)(2,1)}, u32[]{:S(2)}, u32[]{:S(2)}) collective-permute-start(bf16[768,768]{1,0:T(8,128)(2,1)S(1)} %fusion.1), channel_id=1, source_target_pairs={{0,4},{4,8},{8,12},{1,5},{5,9},{9,13},{2,6},{6,10},{10,14},{3,7},{... | collective-permute-start | bytes 3538952 | tf_op jit(solution)/shard_map/ppermute | solution.py:18
  345.3 2.3 copy-start.14
  411.4 24.8 %collective-permute-start.14 = (bf16[768,640]{1,0:T(8,128)(2,1)S(1)}, bf16[768,640]{1,0:T(8,128)(2,1)}, u32[]{:S(2)}, u32[]{:S(2)}) collective-permute-start(bf16[768,640]{1,0:T(8,128)(2,1)S(1)} %get-tuple-element.22), channel_id=1, source_target_pairs={{0,16},{16,0},{1,17},{17,1},{2,18},{18,2},{3,19},{19,3},{4,20},{20... | collective-permute-start | bytes 2949128 | tf_op jit(solution)/shard_map/ppermute | solution.py:114
  412.9 44.3 %collective-permute-start.13 = (bf16[768,640]{1,0:T(8,128)(2,1)S(1)}, bf16[768,640]{1,0:T(8,128)(2,1)}, u32[]{:S(2)}, u32[]{:S(2)}) collective-permute-start(bf16[768,640]{1,0:T(8,128)(2,1)S(1)} %get-tuple-element.23), channel_id=1, source_target_pairs={{0,16},{16,0},{1,17},{17,1},{2,18},{18,2},{3,19},{19,3},{4,20},{20... | collective-permute-start | bytes 2949128 | tf_op jit(solution)/shard_map/ppermute | solution.py:114
  413.4 62.4 %collective-permute-start.15 = (bf16[768,640]{1,0:T(8,128)(2,1)S(1)}, bf16[768,640]{1,0:T(8,128)(2,1)}, u32[]{:S(2)}, u32[]{:S(2)}) collective-permute-start(bf16[768,640]{1,0:T(8,128)(2,1)S(1)} %get-tuple-element.21), channel_id=1, source_target_pairs={{0,16},{16,0},{1,17},{17,1},{2,18},{18,2},{3,19},{19,3},{4,20},{20... | collective-permute-start | bytes 2949128 | tf_op jit(solution)/shard_map/ppermute | solution.py:114
  448.4 11.4 %copy-start.12 = (bf16[768,3072]{1,0:T(8,128)(2,1)S(1)}, bf16[768,3072]{1,0:T(8,128)(2,1)}, u32[]{:S(2)}) copy-start(bf16[768,3072]{1,0:T(8,128)(2,1)} %all-gather.14.cloned.1.call-done) | copy-start | bytes 14155780
  451.1 8.7 %copy-start.9 = (bf16[768,640]{1,0:T(8,128)(2,1)S(1)}, bf16[768,640]{1,0:T(8,128)(2,1)}, u32[]{:S(2)}) copy-start(bf16[768,640]{1,0:T(8,128)(2,1)} %get-tuple-element.20) | copy-start | bytes 2949124
  459.8 2.1 copy-start.4
  478.1 6.1 %copy-start.1 = (bf16[1280,768]{1,0:T(8,128)(2,1)S(1)}, bf16[1280,768]{1,0:T(8,128)(2,1)}, u32[]{:S(2)}) copy-start(bf16[1280,768]{1,0:T(8,128)(2,1)} %param.11) | copy-start | bytes 5898244
Sparse Core Ops, SparseCore 0:
  9.1 79.1 all-gather.7
  89.9 74.9 all-gather.5
  166.4 74.9 all-gather.9
  242.8 74.9 all-gather.11
  409.4 38.9 all-gather.13
